TPU v7x, 32 devices: a whole 2x2x4 slice. The times are simulated.
32 devices in a mesh: row: 2 (over x), col: 16 (over z, y, core).
Axes of the slice: x: 2, y: 2, z: 4, core: 2. Of those that a mesh axis runs over, the one named last changes fastest.
Arguments:
- source: float32 [48, 1536, 1536], P('row', 'col'), may hold values from -16 to 16
- lower_coef: float32 [48], replicated, may hold values from 0.004 to 18, as said below
- upper_coef: float32 [48], replicated, may hold values from 0.004 to 18, as said below
Outputs:
- pressure: float32 [48, 1536, 1536], P('row', 'col')
Inputs may be any that keep to these rules, and one draw needn't show every extreme that they name: lower_coef[z] = 2 / (h[z] (h[z] + h[z-1])) and upper_coef[z] = 2 / (h[z] (h[z] + h[z+1])) for positive level thicknesses h shared by both, with h[-1] = h[0]. `upper_coef`: the same thicknesses as for lower_coef, with h[48] = h[47].
All inputs are finite; a program needn't handle non-finite values.
Results may differ from a plain program's by a relative error of at most 0.0018.
Values sent between devices are 32-bit elements; how exact they have to be, the bound alone decides.
No kernel may reach another device: no remote copies, remote signals or barrier semaphores. Data moves between devices by JAX's collectives and lax.ppermute only.
A program may use at most 192 MiB of HBM per device.

v0:
```python
import math

import jax
import jax.numpy as jnp
from jax import lax
from jax.sharding import PartitionSpec as P


def cas_table(row_index, col_index, length):
    product = row_index[:, None] * col_index[None, :] % length
    angles = product.astype(jnp.float32) * (2.0 * math.pi / length)
    return jnp.cos(angles) + jnp.sin(angles)


def eigen_values(wave_index, length):
    return 2.0 * jnp.cos(wave_index.astype(jnp.float32) * (2.0 * math.pi / length)) - 2.0


def vertical_solve(spectra, lower_coef, upper_coef, eigen_sum, pinned):
    levels = spectra.shape[0]
    level_index = lax.iota(jnp.int32, levels)
    below = jnp.where(level_index > 0, lower_coef, 0.0)
    above = jnp.where(level_index < levels - 1, upper_coef, 0.0)
    head_diag = jnp.where(pinned, 1.0, eigen_sum - above[0])
    head_upper = jnp.where(pinned, 0.0, above[0])
    head_right = jnp.where(pinned, 0.0, spectra[0])
    start = (head_upper / head_diag, head_right / head_diag)

    def forward(carry, item):
        ratio_before, value_before = carry
        low_coef, high_coef, right_side = item
        pivot = eigen_sum - low_coef - high_coef - low_coef * ratio_before
        ratio_next = high_coef / pivot
        value_next = (right_side - low_coef * value_before) / pivot
        return ((ratio_next, value_next), (ratio_next, value_next))

    unused, (ratios, values) = lax.scan(forward, start, (below[1:], above[1:], spectra[1:]))
    ratios = jnp.concatenate([start[0][None], ratios], axis=0)
    values = jnp.concatenate([start[1][None], values], axis=0)

    def backward(later, item):
        ratio_here, value_here = item
        result = value_here - ratio_here * later
        return (result, result)

    unused, solved = lax.scan(backward, jnp.zeros_like(eigen_sum), (ratios, values), reverse=True)
    return solved


def body(source, lower_coef, upper_coef):
    highest = lax.Precision.HIGHEST
    slab_levels, slab_rows, full_x = source.shape
    col_count = lax.axis_size("col")
    full_y = slab_rows * col_count
    index_x = lax.iota(jnp.int32, full_x)
    index_y = lax.iota(jnp.int32, full_y)
    table_x = cas_table(index_x, index_x, full_x)
    table_y = cas_table(index_y, index_y, full_y)
    along_x = jnp.einsum("zyx,xk->zky", source, table_x, precision=highest)
    scale = 1.0 / (full_x * full_y)
    spectra = jnp.einsum(
        "zxy,yk->zxk",
        lax.all_to_all(along_x, "col", split_axis=1, concat_axis=2, tiled=True),
        table_y,
        precision=highest,
    )
    columns = lax.all_to_all(spectra, "row", split_axis=2, concat_axis=0, tiled=True)
    part_x = columns.shape[1]
    part_y = columns.shape[2]
    wave_x = lax.axis_index("col") * part_x + lax.iota(jnp.int32, part_x)
    wave_y = lax.axis_index("row") * part_y + lax.iota(jnp.int32, part_y)
    eigen_sum = eigen_values(wave_x, full_x)[:, None] + eigen_values(wave_y, full_y)[None, :]
    pinned = (wave_x == 0)[:, None] & (wave_y == 0)[None, :]
    solved = vertical_solve(columns, lower_coef, upper_coef, eigen_sum, pinned)
    returned = lax.all_to_all(solved, "row", split_axis=0, concat_axis=2, tiled=True)
    inverse_y = jnp.einsum("zxk,ky->zxy", returned, table_y, precision=highest)
    pressure = jnp.einsum(
        "zky,kn->zyn",
        lax.all_to_all(inverse_y, "col", split_axis=2, concat_axis=1, tiled=True),
        table_x,
        precision=highest,
    )
    return pressure * scale


def solution(mesh):
    placed = (P("row", "col", None), P(), P())
    return jax.shard_map(
        body, mesh=mesh, in_specs=placed, out_specs=P("row", "col", None), check_vma=False
    )
```

profile of v0, /device:TPU:15, one launch (start us, length us, event | category | flops | bytes accessed | tf_op | source)
XLA Modules:
  0.0 2082.6 jit_solution(8030665542638222199)
XLA Ops:
  0.0 38.2 %fusion.66 = f32[1536,1536,1]{1,0,2:T(8,128)S(1)} fusion(), kind=kLoop, calls=%fused_computation.27.clone.clone.clone.1 | loop fusion | flops 23592960 | bytes 9437184 | tf_op jit(solution)/shard_map/zyx,xk->zky/dot_general | solution.py:59
  38.2 73.1 %fusion.23 = f32[24,1536,96]{1,2,0:T(8,128)} fusion(f32[24,96,1536]{2,1,0:T(8,128)} %param.7, f32[1536,1536,1]{1,0,2:T(8,128)S(1)} %fusion.66), kind=kOutput, calls=%fused_computation.34 | convolution fusion | flops 65229815808 | bytes 37748736 | tf_op jit(solution)/shard_map/zyx,xk->zky/dot_general | solution.py:59
  111.3 16.9 copy.8
  128.3 6.6 all-to-all-start
  134.8 39.5 %fusion.62 = f32[1536,1536,1]{1,0,2:T(8,128)} fusion(), kind=kLoop, calls=%fused_computation.25.clone | loop fusion | flops 23592960 | bytes 9437184 | tf_op jit(solution)/shard_map/zxy,yk->zxk/dot_general | solution.py:61
  174.4 367.5 %all-to-all-done = f32[24,1536,96]{2,0,1:T(8,128)} async-done(((f32[24,1536,96]{2,0,1:T(8,128)}), f32[24,1536,96]{2,0,1:T(8,128)}, u32[]{:S(2)}, u32[]{:S(2)}) %all-to-all-start) | async-done | bytes 14155808 | tf_op jit(solution)/shard_map/all_to_all | solution.py:63
  541.9 19.7 copy.19
  561.6 20.5 all_to_all.55
  582.1 79.5 %fusion.13 = f32[24,96,1536]{2,1,0:T(8,128)} fusion(f32[24,96,1536]{2,1,0:T(8,128)} %all_to_all.55, f32[1536,1536,1]{1,0,2:T(8,128)} %fusion.62), kind=kOutput, calls=%fused_computation.24 | convolution fusion | flops 65229815808 | bytes 37748736 | tf_op jit(solution)/shard_map/zxy,yk->zxk/dot_general | solution.py:61
  661.6 16.9 copy.10
  678.5 11.3 all-to-all-start.1
  690.1 203.2 %all-to-all-done.1 = f32[24,96,1536]{1,0,2:T(8,128)} async-done(((f32[24,96,1536]{1,0,2:T(8,128)}), f32[24,96,1536]{1,0,2:T(8,128)}, u32[]{:S(2)}, u32[]{:S(2)}) %all-to-all-start.1) | async-done | bytes 14155808 | tf_op jit(solution)/shard_map/all_to_all | solution.py:67
  893.4 17.1 copy.11
  910.5 11.5 slice.22
  924.3 201.6 %while.34 = (s32[]{:T(128)}, f32[96,768]{1,0:T(8,128)S(1)}, f32[96,768]{1,0:T(8,128)S(1)}, f32[47,96,768]{2,1,0:T(8,128)}, f32[47,96,768]{2,1,0:T(8,128)}, /*ind...) while((s32[]{:T(128)}, f32[96,768]{1,0:T(8,128)S(1)}, ...), condition=%wide.region_1.2_spmd.clone, body=%wide.region_0.1_spmd.clone.sunk | while | flops 663554 | bytes 2069509 | solution.py:37
  1092.6 3.2 bitcast_dynamic-update-slice_fusion.5
  1125.9 18.3 pad_maximum_fusion
  1144.2 7.0 broadcast_in_dim.56
  1151.2 96.7 %while.35 = (s32[]{:T(128)}, f32[96,768]{1,0:T(8,128)S(1)}, f32[48,96,768]{2,1,0:T(8,128)}, f32[48,96,768]{2,1,0:T(8,128)}, f32[48,96,768]{2,1,0:T(8,128)}, /*index=5*/s32[]{:T(128)}, s32[]{:T(128)}, s32[]{:T(128)}) while((s32[]{:T(128)}, f32[96,768]{1,0:T(8,128)S(1)}, f32[48,96,768]{2,1,0:T(8,128)}, f32[48,96,768]{2,1,0:T(8,128)}, ...), condition=%wide.region_3.4_spmd.clone, body=%wide.region_2.3_spmd.clone.sunk | while | flops 221188 | bytes 1474671 | solution.py:46
  1247.9 10.0 all-to-all-start.2
  1257.9 39.5 %fusion.60 = f32[1536,1536,1]{1,0,2:T(8,128)} fusion(), kind=kLoop, calls=%fused_computation.23.clone.1 | loop fusion | flops 23592960 | bytes 9437184 | tf_op jit(solution)/shard_map/zxk,ky->zxy/dot_general | solution.py:76
  1297.4 112.5 %all-to-all-done.2 = f32[48,96,768]{2,1,0:T(8,128)} async-done(((f32[48,96,768]{2,1,0:T(8,128)}), f32[48,96,768]{2,1,0:T(8,128)}, u32[]{:S(2)}, u32[]{:S(2)}) %all-to-all-start.2) | async-done | bytes 14155808 | tf_op jit(solution)/shard_map/all_to_all | solution.py:75
  1409.9 24.5 %copy.20 = f32[2,24,96,768]{3,0,2,1:T(2,128)} copy(f32[2,24,96,768]{3,2,1,0:T(8,128)} %bitcast.9) | data formatting | bytes 28311552 | tf_op jit(solution)/shard_map/all_to_all | solution.py:75
  1434.4 18.4 all_to_all.63
  1452.8 79.4 %fusion.11 = f32[24,96,1536]{2,1,0:T(8,128)} fusion(f32[24,96,1536]{2,1,0:T(8,128)} %all_to_all.63, f32[1536,1536,1]{1,0,2:T(8,128)} %fusion.60), kind=kOutput, calls=%fused_computation.22 | convolution fusion | flops 65229815808 | bytes 37748736 | tf_op jit(solution)/shard_map/zxk,ky->zxy/dot_general | solution.py:76
  1532.3 16.9 copy.13
  1549.2 6.6 all-to-all-start.3
  1555.8 39.5 %fusion.64 = f32[1536,1536,1]{1,0,2:T(8,128)} fusion(), kind=kLoop, calls=%fused_computation.21.clone.clone.clone.1 | loop fusion | flops 23592960 | bytes 9437184 | tf_op jit(solution)/shard_map/zky,kn->zyn/dot_general | solution.py:77
  1595.4 367.4 %all-to-all-done.3 = f32[24,96,1536]{1,0,2:T(8,128)} async-done(((f32[24,96,1536]{1,0,2:T(8,128)}), f32[24,96,1536]{1,0,2:T(8,128)}, u32[]{:S(2)}, u32[]{:S(2)}) %all-to-all-start.3) | async-done | bytes 14155808 | tf_op jit(solution)/shard_map/all_to_all | solution.py:79
  1962.8 19.7 copy.18
  1982.4 20.5 all_to_all.67
  2003.0 79.5 %fusion.20 = f32[24,96,1536]{2,1,0:T(8,128)} fusion(f32[24,1536,96]{1,2,0:T(8,128)} %all_to_all.67, f32[1536,1536,1]{1,0,2:T(8,128)} %fusion.64), kind=kOutput, calls=%fused_computation.33 | convolution fusion | flops 65233354752 | bytes 37748736 | tf_op jit(solution)/shard_map/zky,kn->zyn/dot_general | solution.py:77
  (205 shorter events, 297.6 us)
Async XLA Ops:
  128.3 413.6 %all-to-all-start = ((f32[24,1536,96]{2,0,1:T(8,128)}), f32[24,1536,96]{2,0,1:T(8,128)}, u32[]{:S(2)}, u32[]{:S(2)}) async-start(f32[24,1536,96]{2,0,1:T(8,128)} %copy.8), calls=%async_computation | async-start | bytes 37748736 | tf_op jit(solution)/shard_map/all_to_all | solution.py:63
  678.5 11.3 copy-start
  678.5 11.4 copy-start.1
  678.5 214.8 %all-to-all-start.1 = ((f32[24,96,1536]{1,0,2:T(8,128)}), f32[24,96,1536]{1,0,2:T(8,128)}, u32[]{:S(2)}, u32[]{:S(2)}) async-start(f32[24,96,1536]{1,0,2:T(8,128)} %copy.10), calls=%async_computation.1 | async-start | bytes 37748736 | tf_op jit(solution)/shard_map/all_to_all | solution.py:67
  1247.9 162.0 %all-to-all-start.2 = ((f32[48,96,768]{2,1,0:T(8,128)}), f32[48,96,768]{2,1,0:T(8,128)}, u32[]{:S(2)}, u32[]{:S(2)}) async-start(f32[48,96,768]{2,1,0:T(8,128)} %get-tuple-element.158), calls=%async_computation.2 | async-start | bytes 28311552 | tf_op jit(solution)/shard_map/all_to_all | solution.py:75
  1549.2 413.6 %all-to-all-start.3 = ((f32[24,96,1536]{1,0,2:T(8,128)}), f32[24,96,1536]{1,0,2:T(8,128)}, u32[]{:S(2)}, u32[]{:S(2)}) async-start(f32[24,96,1536]{1,0,2:T(8,128)} %copy.13), calls=%async_computation.3 | async-start | bytes 37748736 | tf_op jit(solution)/shard_map/all_to_all | solution.py:79
where the time goes:
time: 2110 us; the launch traced here: 2080 us
  waiting for transfers between devices  1050 us (50%)
  other arithmetic  422 us (20%)
  matrix products  312 us (15%)
  local copies, waits for them, and re-layouts  263 us (12%)
  starting transfers between devices  34.5 us (2%)
    all_to_all x1, waiting for transfers between devices, body(): lax.all_to_all(along_x, 'col', split_axis=1, concat_axis=2, tiled=True)  368 us
    all_to_all x1, waiting for transfers between devices, body(): lax.all_to_all(inverse_y, 'col', split_axis=2, concat_axis=1, tiled=True)  367 us
    all_to_all x1, waiting for transfers between devices, body(): lax.all_to_all(spectra, 'row', split_axis=2, concat_axis=0, tiled=True)  203 us
    dynamic_update_slice x47, other arithmetic, vertical_solve(): lax.scan(forward, start, (below[1:], above[1:], spectra[1:]))  148 us
    all_to_all x1, waiting for transfers between devices, body(): lax.all_to_all(solved, 'row', split_axis=0, concat_axis=2, tiled=True)  113 us
    dynamic_update_slice x48, other arithmetic, vertical_solve(): lax.scan(backward, jnp.zeros_like(eigen_sum), (ratios, values), reverse=T...  96.6 us
    dot_general x1, matrix products, body(): jnp.einsum('zxy,yk->zxk', lax.all_to_all(along_x, 'col', split_axis=1, co...  79.5 us
    dot_general x1, matrix products, body(): jnp.einsum('zky,kn->zyn', lax.all_to_all(inverse_y, 'col', split_axis=2,...  79.5 us
  transfers between devices with their start and end apart: 4, of which 4 were waited for; matrix products, arithmetic and copies ran while one was open for 6% of the time, Pallas kernels for 0%

commit v1 on v0

--- a/solution.py
+++ b/solution.py
@@ -4,6 +4,8 @@
 import jax.numpy as jnp
 from jax import lax
 from jax.sharding import PartitionSpec as P
+from jax.experimental import pallas as pl
+from jax.experimental.pallas import tpu as pltpu
 
 
 def cas_table(row_index, col_index, length):
@@ -16,35 +18,53 @@
     return 2.0 * jnp.cos(wave_index.astype(jnp.float32) * (2.0 * math.pi / length)) - 2.0
 
 
-def vertical_solve(spectra, lower_coef, upper_coef, eigen_sum, pinned):
-    levels = spectra.shape[0]
-    level_index = lax.iota(jnp.int32, levels)
-    below = jnp.where(level_index > 0, lower_coef, 0.0)
-    above = jnp.where(level_index < levels - 1, upper_coef, 0.0)
-    head_diag = jnp.where(pinned, 1.0, eigen_sum - above[0])
-    head_upper = jnp.where(pinned, 0.0, above[0])
-    head_right = jnp.where(pinned, 0.0, spectra[0])
-    start = (head_upper / head_diag, head_right / head_diag)
+def solve_kernel(lower_ref, upper_ref, eigen_ref, pinned_ref, spectra_ref, solved_ref, ratio_ref):
+    levels = spectra_ref.shape[0]
+    eigen_sum = eigen_ref[...]
+    pinned = pinned_ref[...] > 0.5
+    above_first = upper_ref[0]
+    head_diag = jnp.where(pinned, 1.0, eigen_sum - above_first)
+    head_upper = jnp.where(pinned, 0.0, above_first)
+    head_right = jnp.where(pinned, 0.0, spectra_ref[0])
+    ratio_ref[0] = head_upper / head_diag
+    solved_ref[0] = head_right / head_diag
 
-    def forward(carry, item):
+    def forward(level, carry):
         ratio_before, value_before = carry
-        low_coef, high_coef, right_side = item
+        low_coef = lower_ref[level]
+        high_coef = jnp.where(level < levels - 1, upper_ref[level], 0.0)
         pivot = eigen_sum - low_coef - high_coef - low_coef * ratio_before
         ratio_next = high_coef / pivot
-        value_next = (right_side - low_coef * value_before) / pivot
-        return ((ratio_next, value_next), (ratio_next, value_next))
+        value_next = (spectra_ref[level] - low_coef * value_before) / pivot
+        ratio_ref[level] = ratio_next
+        solved_ref[level] = value_next
+        return ratio_next, value_next
 
-    unused, (ratios, values) = lax.scan(forward, start, (below[1:], above[1:], spectra[1:]))
-    ratios = jnp.concatenate([start[0][None], ratios], axis=0)
-    values = jnp.concatenate([start[1][None], values], axis=0)
+    unused, last = lax.fori_loop(1, levels, forward, (ratio_ref[0], solved_ref[0]))
 
-    def backward(later, item):
-        ratio_here, value_here = item
-        result = value_here - ratio_here * later
-        return (result, result)
+    def backward(step, later):
+        level = levels - 2 - step
+        result = solved_ref[level] - ratio_ref[level] * later
+        solved_ref[level] = result
+        return result
 
-    unused, solved = lax.scan(backward, jnp.zeros_like(eigen_sum), (ratios, values), reverse=True)
-    return solved
+    lax.fori_loop(0, levels - 1, backward, last)
+
+
+def vertical_solve(spectra, lower_coef, upper_coef, eigen_sum, pinned):
+    levels, part_x, part_y = spectra.shape
+    block = 8 if part_x % 8 == 0 else part_x
+    column_spec = pl.BlockSpec((levels, block, part_y), lambda i: (0, i, 0))
+    plane_spec = pl.BlockSpec((block, part_y), lambda i: (i, 0))
+    scalar_spec = pl.BlockSpec(memory_space=pltpu.SMEM)
+    return pl.pallas_call(
+        solve_kernel,
+        grid=(part_x // block,),
+        in_specs=[scalar_spec, scalar_spec, plane_spec, plane_spec, column_spec],
+        out_specs=column_spec,
+        out_shape=jax.ShapeDtypeStruct(spectra.shape, jnp.float32),
+        scratch_shapes=[pltpu.VMEM((levels, block, part_y), jnp.float32)],
+    )(lower_coef, upper_coef, eigen_sum, pinned.astype(jnp.float32), spectra)
 
 
 def body(source, lower_coef, upper_coef):

time: 2110 us -> 1750 us (0.83)
  other arithmetic: 422 us -> 159 us
  local copies, waits for them, and re-layouts: 263 us -> 161 us
    dynamic_update_slice x95 -> x0, other arithmetic: 245 us -> none  [the longest x47 148 us: vertical_solve(): lax.scan(forward, start, (below[1:], above[1:], spectra[1:]))]
    dynamic_slice x94 -> x0, local copies, waits for them, and re-layouts: 53.4 us -> none  [vertical_solve(): lax.scan(forward, start, (below[1:], above[1:], spectra[1:]))]
    all_to_all x2 -> x1, local copies, waits for them, and re-layouts: 42.9 us -> 12.2 us  [body(): lax.all_to_all(solved, 'row', split_axis=0, concat_axis=2, tiled=True)]
  transfers between devices with their start and end apart: 4 -> 4, of which waited for: 4 -> 4; matrix products, arithmetic and copies ran while one was open for 6% -> 7% of each run, Pallas kernels for 0% -> 0%
where the time goes in v1:
time: 1750 us; the launch traced here: 1730 us
  waiting for transfers between devices  1050 us (60%)
  matrix products  312 us (18%)
  local copies, waits for them, and re-layouts  161 us (9%)
  other arithmetic  159 us (9%)
  starting transfers between devices  34.2 us (2%)
  Pallas kernels  19.8 us (1%)
    all_to_all x1, waiting for transfers between devices, body(): lax.all_to_all(along_x, 'col', split_axis=1, concat_axis=2, tiled=True)  368 us
    all_to_all x1, waiting for transfers between devices, body(): lax.all_to_all(inverse_y, 'col', split_axis=2, concat_axis=1, tiled=True)  367 us
    all_to_all x1, waiting for transfers between devices, body(): lax.all_to_all(spectra, 'row', split_axis=2, concat_axis=0, tiled=True)  202 us
    all_to_all x1, waiting for transfers between devices, body(): lax.all_to_all(solved, 'row', split_axis=0, concat_axis=2, tiled=True)  112 us
    dot_general x1, matrix products, body(): inverse_y = jnp.einsum('zxk,ky->zxy', returned, table_y, precision=highest)  79.5 us
    dot_general x1, matrix products, body(): jnp.einsum('zxy,yk->zxk', lax.all_to_all(along_x, 'col', split_axis=1, co...  79.5 us
    dot_general x1, matrix products, body(): jnp.einsum('zky,kn->zyn', lax.all_to_all(inverse_y, 'col', split_axis=2,...  79.5 us
    dot_general x1, matrix products, body(): along_x = jnp.einsum('zyx,xk->zky', source, table_x, precision=highest)  73.1 us
  transfers between devices with their start and end apart: 4, of which 4 were waited for; matrix products, arithmetic and copies ran while one was open for 7% of the time, Pallas kernels for 0%

profile of v1, /device:TPU:15, one launch (start us, length us, event | category | flops | bytes accessed | tf_op | source)
XLA Modules:
  0.0 1734.3 jit_solution(6520808327392776310)
XLA Ops:
  0.0 38.2 %fusion.52 = f32[1536,1536,1]{1,0,2:T(8,128)S(1)} fusion(), kind=kLoop, calls=%fused_computation.12.clone.clone.clone.1 | loop fusion | flops 23592960 | bytes 9437184 | tf_op jit(solution)/shard_map/zyx,xk->zky/dot_general | solution.py:79
  38.2 73.1 %fusion.16 = f32[24,1536,96]{1,2,0:T(8,128)} fusion(f32[24,96,1536]{2,1,0:T(8,128)} %param.3, f32[1536,1536,1]{1,0,2:T(8,128)S(1)} %fusion.52), kind=kOutput, calls=%fused_computation.19 | convolution fusion | flops 65229815808 | bytes 37748736 | tf_op jit(solution)/shard_map/zyx,xk->zky/dot_general | solution.py:79
  111.3 17.0 copy.8
  128.3 6.6 all-to-all-start
  134.8 39.5 %fusion.48 = f32[1536,1536,1]{1,0,2:T(8,128)} fusion(), kind=kLoop, calls=%fused_computation.10.clone | loop fusion | flops 23592960 | bytes 9437184 | tf_op jit(solution)/shard_map/zxy,yk->zxk/dot_general | solution.py:81
  174.4 367.5 %all-to-all-done = f32[24,1536,96]{2,0,1:T(8,128)} async-done(((f32[24,1536,96]{2,0,1:T(8,128)}), f32[24,1536,96]{2,0,1:T(8,128)}, u32[]{:S(2)}, u32[]{:S(2)}) %all-to-all-start) | async-done | bytes 14155808 | tf_op jit(solution)/shard_map/all_to_all | solution.py:83
  541.9 19.7 %copy.19 = f32[24,16,96,96]{3,1,2,0:T(8,128)} copy(f32[24,16,96,96]{3,0,2,1:T(8,128)} %bitcast.2) | data formatting | bytes 28311552 | tf_op jit(solution)/shard_map/all_to_all | solution.py:83
  561.6 20.5 %all_to_all.55 = f32[24,96,1536]{2,1,0:T(8,128)} reshape(f32[24,96,16,96]{3,2,1,0:T(8,128)} %bitcast.60) | data formatting | bytes 28311552 | tf_op jit(solution)/shard_map/all_to_all | solution.py:83
  582.1 79.5 %fusion.6 = f32[24,96,1536]{2,1,0:T(8,128)} fusion(f32[24,96,1536]{2,1,0:T(8,128)} %all_to_all.55, f32[1536,1536,1]{1,0,2:T(8,128)} %fusion.48), kind=kOutput, calls=%fused_computation.9 | convolution fusion | flops 65229815808 | bytes 37748736 | tf_op jit(solution)/shard_map/zxy,yk->zxk/dot_general | solution.py:81
  661.6 17.0 copy.10
  678.5 11.0 all-to-all-start.1
  689.7 0.8 and_convert_fusion.pinned_ref
  690.4 0.8 broadcast_add_fusion.eigen_ref
  691.2 201.8 %all-to-all-done.1 = f32[24,96,1536]{1,0,2:T(8,128)} async-done(((f32[24,96,1536]{1,0,2:T(8,128)}), f32[24,96,1536]{1,0,2:T(8,128)}, u32[]{:S(2)}, u32[]{:S(2)}) %all-to-all-start.1) | async-done | bytes 14155808 | tf_op jit(solution)/shard_map/all_to_all | solution.py:87
  893.0 17.1 copy.11
  910.1 19.8 %shard_map.37 = f32[48,96,768]{2,1,0:T(8,128)} custom-call(f32[48]{0:T(128)} %lower_ref.1, f32[48]{0:T(128)} %upper_ref.1, f32[96,768]{1,0:T(8,128)} %broadcast_add_fusion.eigen_ref, f32[96,768]{1,0:T(8,128)} %and_convert_fusion.pinned_ref, f32[48,96,768]{2,1,0:T(8,128)} %bitcast.62), custom_call_target="tpu_custom_call" | custom-call | tf_op jit(solution)/shard_map/pallas_call | solution.py:60
  930.0 9.9 all-to-all-start.2
  939.9 39.5 %fusion.46 = f32[1536,1536,1]{1,0,2:T(8,128)} fusion(), kind=kLoop, calls=%fused_computation.8.clone.1 | loop fusion | flops 23592960 | bytes 9437184 | tf_op jit(solution)/shard_map/zxk,ky->zxy/dot_general | solution.py:96
  979.4 112.5 %all-to-all-done.2 = f32[48,96,768]{2,1,0:T(8,128)} async-done(((f32[48,96,768]{2,1,0:T(8,128)}), f32[48,96,768]{2,1,0:T(8,128)}, u32[]{:S(2)}, u32[]{:S(2)}) %all-to-all-start.2) | async-done | bytes 14155808 | tf_op jit(solution)/shard_map/all_to_all | solution.py:95
  1091.9 12.2 copy.15
  1104.1 79.5 %fusion.4 = f32[24,96,1536]{2,1,0:T(8,128)} fusion(f32[24,96,1536]{2,1,0:T(8,128)} %bitcast.63, f32[1536,1536,1]{1,0,2:T(8,128)} %fusion.46), kind=kOutput, calls=%fused_computation.7 | convolution fusion | flops 65229815808 | bytes 37748736 | tf_op jit(solution)/shard_map/zxk,ky->zxy/dot_general | solution.py:96
  1183.6 17.0 copy.13
  1200.6 6.7 all-to-all-start.3
  1207.3 39.5 %fusion.50 = f32[1536,1536,1]{1,0,2:T(8,128)} fusion(), kind=kLoop, calls=%fused_computation.6.clone.clone.clone.1 | loop fusion | flops 23592960 | bytes 9437184 | tf_op jit(solution)/shard_map/zky,kn->zyn/dot_general | solution.py:97
  1246.8 367.4 %all-to-all-done.3 = f32[24,96,1536]{1,0,2:T(8,128)} async-done(((f32[24,96,1536]{1,0,2:T(8,128)}), f32[24,96,1536]{1,0,2:T(8,128)}, u32[]{:S(2)}, u32[]{:S(2)}) %all-to-all-start.3) | async-done | bytes 14155808 | tf_op jit(solution)/shard_map/all_to_all | solution.py:99
  1614.2 19.7 %copy.18 = f32[24,96,16,96]{1,2,3,0:T(8,128)} copy(f32[24,96,16,96]{1,0,3,2:T(8,128)} %bitcast.9) | data formatting | bytes 28311552 | tf_op jit(solution)/shard_map/all_to_all | solution.py:99
  1633.8 20.5 %all_to_all.67 = f32[24,1536,96]{1,2,0:T(8,128)} reshape(f32[24,16,96,96]{2,1,3,0:T(8,128)} %bitcast.61) | data formatting | bytes 28311552 | tf_op jit(solution)/shard_map/all_to_all | solution.py:99
  1654.4 79.5 %fusion.13 = f32[24,96,1536]{2,1,0:T(8,128)} fusion(f32[24,1536,96]{1,2,0:T(8,128)} %all_to_all.67, f32[1536,1536,1]{1,0,2:T(8,128)} %fusion.50), kind=kOutput, calls=%fused_computation.18 | convolution fusion | flops 65233354752 | bytes 37748736 | tf_op jit(solution)/shard_map/zky,kn->zyn/dot_general | solution.py:97
  (4 shorter events, 0.1 us)
Async XLA Ops:
  128.3 413.6 %all-to-all-start = ((f32[24,1536,96]{2,0,1:T(8,128)}), f32[24,1536,96]{2,0,1:T(8,128)}, u32[]{:S(2)}, u32[]{:S(2)}) async-start(f32[24,1536,96]{2,0,1:T(8,128)} %copy.8), calls=%async_computation | async-start | bytes 37748736 | tf_op jit(solution)/shard_map/all_to_all | solution.py:83
  678.5 214.5 %all-to-all-start.1 = ((f32[24,96,1536]{1,0,2:T(8,128)}), f32[24,96,1536]{1,0,2:T(8,128)}, u32[]{:S(2)}, u32[]{:S(2)}) async-start(f32[24,96,1536]{1,0,2:T(8,128)} %copy.10), calls=%async_computation.1 | async-start | bytes 37748736 | tf_op jit(solution)/shard_map/all_to_all | solution.py:87
  930.0 161.9 %all-to-all-start.2 = ((f32[48,96,768]{2,1,0:T(8,128)}), f32[48,96,768]{2,1,0:T(8,128)}, u32[]{:S(2)}, u32[]{:S(2)}) async-start(f32[48,96,768]{2,1,0:T(8,128)} %shard_map.37), calls=%async_computation.2 | async-start | bytes 28311552 | tf_op jit(solution)/shard_map/all_to_all | solution.py:95
  1200.6 413.6 %all-to-all-start.3 = ((f32[24,96,1536]{1,0,2:T(8,128)}), f32[24,96,1536]{1,0,2:T(8,128)}, u32[]{:S(2)}, u32[]{:S(2)}) async-start(f32[24,96,1536]{1,0,2:T(8,128)} %copy.13), calls=%async_computation.3 | async-start | bytes 37748736 | tf_op jit(solution)/shard_map/all_to_all | solution.py:99

commit v2 on v1

--- a/solution.py
+++ b/solution.py
@@ -1,4 +1,6 @@
 import math
+
+import numpy as np
 
 import jax
 import jax.numpy as jnp
@@ -12,6 +14,12 @@
     product = row_index[:, None] * col_index[None, :] % length
     angles = product.astype(jnp.float32) * (2.0 * math.pi / length)
     return jnp.cos(angles) + jnp.sin(angles)
+
+
+def cas_constant(row_index, col_index, length):
+    product = np.outer(row_index, col_index) % length
+    angles = product.astype(np.float64) * (2.0 * math.pi / length)
+    return jnp.asarray((np.cos(angles) + np.sin(angles)).astype(np.float32))
 
 
 def eigen_values(wave_index, length):
@@ -67,39 +75,45 @@
     )(lower_coef, upper_coef, eigen_sum, pinned.astype(jnp.float32), spectra)
 
 
-def body(source, lower_coef, upper_coef):
+def body(source, lower_coef, upper_coef, chunks=4):
     highest = lax.Precision.HIGHEST
     slab_levels, slab_rows, full_x = source.shape
     col_count = lax.axis_size("col")
     full_y = slab_rows * col_count
-    index_x = lax.iota(jnp.int32, full_x)
-    index_y = lax.iota(jnp.int32, full_y)
-    table_x = cas_table(index_x, index_x, full_x)
-    table_y = cas_table(index_y, index_y, full_y)
-    along_x = jnp.einsum("zyx,xk->zky", source, table_x, precision=highest)
+    part_x = full_x // col_count
+    chunk_x = part_x // chunks
+    index_x = np.arange(full_x)
+    table_y = cas_constant(np.arange(full_y), np.arange(full_y), full_y)
     scale = 1.0 / (full_x * full_y)
-    spectra = jnp.einsum(
-        "zxy,yk->zxk",
-        lax.all_to_all(along_x, "col", split_axis=1, concat_axis=2, tiled=True),
-        table_y,
-        precision=highest,
-    )
-    columns = lax.all_to_all(spectra, "row", split_axis=2, concat_axis=0, tiled=True)
-    part_x = columns.shape[1]
-    part_y = columns.shape[2]
-    wave_x = lax.axis_index("col") * part_x + lax.iota(jnp.int32, part_x)
-    wave_y = lax.axis_index("row") * part_y + lax.iota(jnp.int32, part_y)
-    eigen_sum = eigen_values(wave_x, full_x)[:, None] + eigen_values(wave_y, full_y)[None, :]
-    pinned = (wave_x == 0)[:, None] & (wave_y == 0)[None, :]
-    solved = vertical_solve(columns, lower_coef, upper_coef, eigen_sum, pinned)
-    returned = lax.all_to_all(solved, "row", split_axis=0, concat_axis=2, tiled=True)
-    inverse_y = jnp.einsum("zxk,ky->zxy", returned, table_y, precision=highest)
-    pressure = jnp.einsum(
-        "zky,kn->zyn",
-        lax.all_to_all(inverse_y, "col", split_axis=2, concat_axis=1, tiled=True),
-        table_x,
-        precision=highest,
-    )
+    pressure = None
+    for chunk in range(chunks):
+        waves = (np.arange(col_count)[:, None] * part_x + chunk * chunk_x
+                 + np.arange(chunk_x)[None, :]).reshape(-1)
+        table_chunk = cas_constant(index_x, waves, full_x)
+        table_back = cas_constant(waves, index_x, full_x)
+        along_x = jnp.einsum("zyx,xk->zky", source, table_chunk, precision=highest)
+        spectra = jnp.einsum(
+            "zxy,yk->zxk",
+            lax.all_to_all(along_x, "col", split_axis=1, concat_axis=2, tiled=True),
+            table_y,
+            precision=highest,
+        )
+        columns = lax.all_to_all(spectra, "row", split_axis=2, concat_axis=0, tiled=True)
+        part_y = columns.shape[2]
+        wave_x = lax.axis_index("col") * part_x + chunk * chunk_x + lax.iota(jnp.int32, chunk_x)
+        wave_y = lax.axis_index("row") * part_y + lax.iota(jnp.int32, part_y)
+        eigen_sum = eigen_values(wave_x, full_x)[:, None] + eigen_values(wave_y, full_y)[None, :]
+        pinned = (wave_x == 0)[:, None] & (wave_y == 0)[None, :]
+        solved = vertical_solve(columns, lower_coef, upper_coef, eigen_sum, pinned)
+        returned = lax.all_to_all(solved, "row", split_axis=0, concat_axis=2, tiled=True)
+        inverse_y = jnp.einsum("zxk,ky->zxy", returned, table_y, precision=highest)
+        part = jnp.einsum(
+            "zky,kn->zyn",
+            lax.all_to_all(inverse_y, "col", split_axis=2, concat_axis=1, tiled=True),
+            table_back,
+            precision=highest,
+        )
+        pressure = part if pressure is None else pressure + part
     return pressure * scale
 
 

time: 1750 us -> 1680 us (0.960)
  waiting for transfers between devices: 1050 us -> 330 us
  local copies, waits for them, and re-layouts: 161 us -> 634 us
  matrix products: 312 us -> 377 us
  other arithmetic: 159 us -> 218 us
  starting transfers between devices: 34.2 us -> 85.1 us
    unnamed x0 -> x36, local copies, waits for them, and re-layouts: none -> 354 us
    all_to_all x1 -> x4, waiting for transfers between devices: 367 us -> 71.1 us  [body(): lax.all_to_all(inverse_y, 'col', split_axis=2, concat_axis=1, tiled=True)]
    all_to_all x0 -> x8, other arithmetic: none -> 216 us  [the longest x4 124 us: body(): lax.all_to_all(spectra, 'row', split_axis=2, concat_axis=0, tiled=True)]
    all_to_all x1 -> x4, waiting for transfers between devices: 202 us -> 0.01 us  [body(): lax.all_to_all(spectra, 'row', split_axis=2, concat_axis=0, tiled=True)]
    dot_general x4 -> x0, other arithmetic: 157 us -> none  [the longest x1 39.5 us: body(): inverse_y = jnp.einsum('zxk,ky->zxy', returned, table_y, precision=highest)]
    all_to_all x1 -> x4, waiting for transfers between devices: 112 us -> 0.01 us  [body(): lax.all_to_all(solved, 'row', split_axis=0, concat_axis=2, tiled=True)]
    all_to_all x1 -> x4, waiting for transfers between devices: 368 us -> 259 us  [body(): lax.all_to_all(along_x, 'col', split_axis=1, concat_axis=2, tiled=True)]
    all_to_all x1 -> x5, local copies, waits for them, and re-layouts: 17.1 us -> 51.6 us  [body(): lax.all_to_all(spectra, 'row', split_axis=2, concat_axis=0, tiled=True)]
  transfers between devices with their start and end apart: 4 -> 16, of which waited for: 4 -> 7; matrix products, arithmetic and copies ran while one was open for 7% -> 60% of each run, Pallas kernels for 0% -> 2%
where the time goes in v2:
time: 1680 us; the launch traced here: 1670 us
  local copies, waits for them, and re-layouts  634 us (38%)
  matrix products  377 us (22%)
  waiting for transfers between devices  330 us (20%)
  other arithmetic  218 us (13%)
  starting transfers between devices  85.1 us (5%)
  Pallas kernels  26 us (2%)
    unnamed x36, local copies, waits for them, and re-layouts  354 us
    all_to_all x4, waiting for transfers between devices, body(): lax.all_to_all(along_x, 'col', split_axis=1, concat_axis=2, tiled=True)  259 us
    all_to_all x4, other arithmetic, body(): lax.all_to_all(spectra, 'row', split_axis=2, concat_axis=0, tiled=True)  124 us
    dot_general x4, matrix products, body(): jnp.einsum('zky,kn->zyn', lax.all_to_all(inverse_y, 'col', split_axis=2,...  109 us
    dot_general x4, matrix products, body(): along_x = jnp.einsum('zyx,xk->zky', source, table_chunk, precision=highest)  103 us
    all_to_all x4, other arithmetic, body(): lax.all_to_all(inverse_y, 'col', split_axis=2, concat_axis=1, tiled=True)  92.3 us
    dot_general x4, matrix products, body(): jnp.einsum('zxy,yk->zxk', lax.all_to_all(along_x, 'col', split_axis=1, co...  84.2 us
    dot_general x4, matrix products, body(): inverse_y = jnp.einsum('zxk,ky->zxy', returned, table_y, precision=highest)  81.8 us
  transfers between devices with their start and end apart: 16, of which 7 were waited for; matrix products, arithmetic and copies ran while one was open for 60% of the time, Pallas kernels for 2%

profile of v2, /device:TPU:15, one launch (start us, length us, event | category | flops | bytes accessed | tf_op | source)
XLA Modules:
  0.0 1671.3 jit_solution(12720615239209386746)
XLA Ops:
  0.0 25.7 %convolution_bitcast_fusion.3 = f32[24,384,96]{1,2,0:T(8,128)S(1)} fusion(f32[1536,384,1]{1,0,2:T(8,128)} %constant.75, f32[24,96,1536]{2,1,0:T(8,128)} %param.12), kind=kOutput, calls=%fused_computation.4 | convolution fusion | flops 16307453952 | bytes 20054016 | tf_op jit(solution)/shard_map/zyx,xk->zky/dot_general | solution.py:94
  36.1 25.7 %convolution_bitcast_fusion.2 = f32[24,384,96]{1,2,0:T(8,128)S(1)} fusion(f32[1536,384,1]{1,0,2:T(8,128)} %constant.78, f32[24,96,1536]{2,1,0:T(8,128)} %param.12), kind=kOutput, calls=%fused_computation.3 | convolution fusion | flops 16307453952 | bytes 20054016 | tf_op jit(solution)/shard_map/zyx,xk->zky/dot_general | solution.py:94
  65.4 74.3 %all-to-all-done = f32[24,384,96]{2,0,1:T(8,128)} async-done(((f32[24,384,96]{2,0,1:T(8,128)}), f32[24,384,96]{2,0,1:T(8,128)}, u32[]{:S(2)}, u32[]{:S(2)}) %all-to-all-start) | async-done | bytes 3538976 | tf_op jit(solution)/shard_map/all_to_all | solution.py:97
  145.3 25.7 %convolution_bitcast_fusion = f32[24,384,96]{1,2,0:T(8,128)S(1)} fusion(f32[1536,384,1]{1,0,2:T(8,128)} %constant.82, f32[24,96,1536]{2,1,0:T(8,128)} %param.12), kind=kOutput, calls=%fused_computation.1 | convolution fusion | flops 16307453952 | bytes 20054016 | tf_op jit(solution)/shard_map/zyx,xk->zky/dot_general | solution.py:94
  174.5 74.4 %all-to-all-done.4 = f32[24,384,96]{2,0,1:T(8,128)} async-done(((f32[24,384,96]{2,0,1:T(8,128)}), f32[24,384,96]{2,0,1:T(8,128)}, u32[]{:S(2)}, u32[]{:S(2)}) %all-to-all-start.4) | async-done | bytes 3538976 | tf_op jit(solution)/shard_map/all_to_all | solution.py:97
  254.1 25.7 %convolution_bitcast_fusion.1 = f32[24,384,96]{1,2,0:T(8,128)S(1)} fusion(f32[1536,384,1]{1,0,2:T(8,128)} %constant.80, f32[24,96,1536]{2,1,0:T(8,128)} %param.12), kind=kOutput, calls=%fused_computation.2 | convolution fusion | flops 16307453952 | bytes 20054016 | tf_op jit(solution)/shard_map/zyx,xk->zky/dot_general | solution.py:94
  283.2 74.5 %all-to-all-done.12 = f32[24,384,96]{2,0,1:T(8,128)} async-done(((f32[24,384,96]{2,0,1:T(8,128)}), f32[24,384,96]{2,0,1:T(8,128)}, u32[]{:S(2)}, u32[]{:S(2)}) %all-to-all-start.12) | async-done | bytes 3538976 | tf_op jit(solution)/shard_map/all_to_all | solution.py:97
  406.4 24.2 %reshape.97 = f32[2,1,442368]{2,1,0:T(1,128)} reshape(f32[1536,24,24]{2,1,0:T(8,128)} %bitcast.121) | data formatting | bytes 7077888
  430.6 35.9 %all-to-all-done.8 = f32[24,384,96]{2,0,1:T(8,128)} async-done(((f32[24,384,96]{2,0,1:T(8,128)}), f32[24,384,96]{2,0,1:T(8,128)}, u32[]{:S(2)}, u32[]{:S(2)}) %all-to-all-start.8) | async-done | bytes 3538976 | tf_op jit(solution)/shard_map/all_to_all | solution.py:97
  484.1 21.3 %fusion.11 = f32[24,24,1536]{2,1,0:T(8,128)} fusion(f32[24,24,1536]{2,1,0:T(8,128)} %all_to_all.243, f32[1536,1536,1]{1,0,2:T(8,128)} %constant.76), kind=kOutput, calls=%fused_computation.34 | convolution fusion | flops 16307453952 | bytes 16515072 | tf_op jit(solution)/shard_map/zxy,yk->zxk/dot_general | solution.py:95
  517.3 24.1 %reshape.85 = f32[2,1,442368]{2,1,0:T(1,128)} reshape(f32[1536,24,24]{2,1,0:T(8,128)} %bitcast.122) | data formatting | bytes 7077888
  559.9 21.3 %fusion.8 = f32[24,24,1536]{2,1,0:T(8,128)} fusion(f32[24,24,1536]{2,1,0:T(8,128)} %all_to_all.227, f32[1536,1536,1]{1,0,2:T(8,128)} %constant.76), kind=kOutput, calls=%fused_computation.31 | convolution fusion | flops 16307453952 | bytes 16515072 | tf_op jit(solution)/shard_map/zxy,yk->zxk/dot_general | solution.py:95
  592.9 24.2 %reshape.93 = f32[2,1,442368]{2,1,0:T(1,128)} reshape(f32[1536,24,24]{2,1,0:T(8,128)} %bitcast.123) | data formatting | bytes 7077888
  635.9 21.3 %fusion.5 = f32[24,24,1536]{2,1,0:T(8,128)} fusion(f32[24,24,1536]{2,1,0:T(8,128)} %all_to_all.211, f32[1536,1536,1]{1,0,2:T(8,128)} %constant.76), kind=kOutput, calls=%fused_computation.28 | convolution fusion | flops 16307453952 | bytes 16515072 | tf_op jit(solution)/shard_map/zxy,yk->zxk/dot_general | solution.py:95
  669.0 24.1 %reshape.89 = f32[2,1,442368]{2,1,0:T(1,128)} reshape(f32[1536,24,24]{2,1,0:T(8,128)} %bitcast.124) | data formatting | bytes 7077888
  700.8 30.4 %reduce.6 = f32[2,442368]{1,0:T(2,128)} reduce(f32[2,1,442368]{2,1,0:T(1,128)S(1)} %all-to-all-done.13, f32[]{:T(128)} %broadcast.170), dimensions={1}, to_apply=%all_to_all.260.reduce_sub_computation | reduce | bytes 7077892 | tf_op jit(solution)/shard_map/all_to_all | solution.py:101
  731.2 22.9 %reshape.98 = f32[1536,24,24]{2,1,0:T(8,128)} reshape(f32[2,442368]{1,0:T(2,128)} %reduce.6) | data formatting | bytes 7077888
  777.4 31.1 %reduce = f32[2,442368]{1,0:T(2,128)} reduce(f32[2,1,442368]{2,1,0:T(1,128)} %all-to-all-done.9, f32[]{:T(128)} %broadcast.170), dimensions={1}, to_apply=%all_to_all.244.reduce_sub_computation | reduce | bytes 7077892 | tf_op jit(solution)/shard_map/all_to_all | solution.py:101
  808.5 22.8 %reshape.86 = f32[1536,24,24]{2,1,0:T(8,128)} reshape(f32[2,442368]{1,0:T(2,128)} %reduce) | data formatting | bytes 7077888
  856.1 31.4 %reduce.4 = f32[2,442368]{1,0:T(2,128)} reduce(f32[2,1,442368]{2,1,0:T(1,128)} %all-to-all-done.5, f32[]{:T(128)} %broadcast.170), dimensions={1}, to_apply=%all_to_all.228.reduce_sub_computation | reduce | bytes 7077892 | tf_op jit(solution)/shard_map/all_to_all | solution.py:101
  887.4 22.7 %reshape.94 = f32[1536,24,24]{2,1,0:T(8,128)} reshape(f32[2,442368]{1,0:T(2,128)} %reduce.4) | data formatting | bytes 7077888
  934.8 31.2 %reduce.2 = f32[2,442368]{1,0:T(2,128)} reduce(f32[2,1,442368]{2,1,0:T(1,128)} %all-to-all-done.1, f32[]{:T(128)} %broadcast.170), dimensions={1}, to_apply=%all_to_all.212.reduce_sub_computation | reduce | bytes 7077892 | tf_op jit(solution)/shard_map/all_to_all | solution.py:101
  966.0 22.9 %reshape.90 = f32[1536,24,24]{2,1,0:T(8,128)} reshape(f32[2,442368]{1,0:T(2,128)} %reduce.2) | data formatting | bytes 7077888
  1125.7 23.7 %all-to-all-done.15 = f32[16,1,55296]{2,1,0:T(1,128)S(1)} async-done(((f32[16,1,55296]{2,1,0:T(1,128)}), f32[16,1,55296]{2,1,0:T(1,128)S(1)}, u32[]{:S(2)}, u32[]{:S(2)}) %all-to-all-start.15) | async-done | bytes 3538976 | tf_op jit(solution)/shard_map/all_to_all | solution.py:112
  1209.3 23.6 %all-to-all-done.11 = f32[16,1,55296]{2,1,0:T(1,128)} async-done(((f32[16,1,55296]{2,1,0:T(1,128)}), f32[16,1,55296]{2,1,0:T(1,128)}, u32[]{:S(2)}, u32[]{:S(2)}) %all-to-all-start.11) | async-done | bytes 3538976 | tf_op jit(solution)/shard_map/all_to_all | solution.py:112
  1292.6 23.8 %all-to-all-done.7 = f32[16,1,55296]{2,1,0:T(1,128)} async-done(((f32[16,1,55296]{2,1,0:T(1,128)}), f32[16,1,55296]{2,1,0:T(1,128)}, u32[]{:S(2)}, u32[]{:S(2)}) %all-to-all-start.7) | async-done | bytes 3538976 | tf_op jit(solution)/shard_map/all_to_all | solution.py:112
  1321.7 30.1 %reduce.7 = f32[16,55296]{1,0:T(8,128)} reduce(f32[16,1,55296]{2,1,0:T(1,128)S(1)} %all-to-all-done.15, f32[]{:T(128)} %broadcast.170), dimensions={1}, to_apply=%all_to_all.268.reduce_sub_computation | reduce | bytes 7077892 | tf_op jit(solution)/shard_map/all_to_all | solution.py:112
  1351.8 23.9 %reshape.100 = f32[1536,24,24]{2,1,0:T(8,128)} reshape(f32[16,55296]{1,0:T(8,128)} %reduce.7) | data formatting | bytes 7077888
  1562.2 27.0 %fusion.13 = f32[24,96,1536]{2,1,0:T(8,128)} fusion(f32[24,384,96]{2,1,0:T(8,128)} %reshape.66, f32[384,1536,1]{1,0,2:T(8,128)S(1)} %copy-done.3), kind=kOutput, calls=%fused_computation.36 | convolution fusion | flops 16307453952 | bytes 20054016 | tf_op jit(solution)/shard_map/zky,kn->zyn/dot_general | solution.py:110
  1589.2 25.6 %fusion.10 = f32[24,96,1536]{2,1,0:T(8,128)} fusion(f32[24,384,96]{2,1,0:T(8,128)S(1)} %bitcast.138, f32[384,1536,1]{1,0,2:T(8,128)S(1)} %copy-done.2), kind=kOutput, calls=%fused_computation.33 | convolution fusion | flops 16307453952 | bytes 20054016 | tf_op jit(solution)/shard_map/zky,kn->zyn/dot_general | solution.py:110
  1614.8 25.3 %fusion.7 = f32[24,96,1536]{2,1,0:T(8,128)} fusion(f32[24,384,96]{2,1,0:T(8,128)S(1)} %bitcast.140, f32[384,1536,1]{1,0,2:T(8,128)S(1)} %copy-done.1), kind=kOutput, calls=%fused_computation.30 | convolution fusion | flops 16307453952 | bytes 20054016 | tf_op jit(solution)/shard_map/zky,kn->zyn/dot_general | solution.py:110
  1640.1 30.9 %add_multiply_fusion = f32[24,96,1536]{2,1,0:T(8,128)} fusion(f32[24,96,1536]{2,1,0:T(8,128)} %fusion.13, f32[24,96,1536]{2,1,0:T(8,128)} %fusion.7, f32[24,96,1536]{2,1,0:T(8,128)} %fusion.10, f32[24,384,96]{2,1,0:T(8,128)S(1)} %bitcast.142, f32[384,1536,1]{1,0,2:T(8,128)S(1)} %copy-done), kind=kOutput, calls=%fused_computation | convolution fusion | flops 16321609728 | bytes 62521344 | tf_op jit(solution)/shard_map/zky,kn->zyn/dot_general | solution.py:110
  (112 shorter events, 699.4 us)
Async XLA Ops:
  29.1 110.6 %all-to-all-start = ((f32[24,384,96]{2,0,1:T(8,128)}), f32[24,384,96]{2,0,1:T(8,128)}, u32[]{:S(2)}, u32[]{:S(2)}) async-start(f32[24,384,96]{2,0,1:T(8,128)} %copy.49), calls=%async_computation | async-start | bytes 9437184 | tf_op jit(solution)/shard_map/all_to_all | solution.py:97
  139.7 109.2 %all-to-all-start.4 = ((f32[24,384,96]{2,0,1:T(8,128)}), f32[24,384,96]{2,0,1:T(8,128)}, u32[]{:S(2)}, u32[]{:S(2)}) async-start(f32[24,384,96]{2,0,1:T(8,128)} %copy.58), calls=%async_computation.4 | async-start | bytes 9437184 | tf_op jit(solution)/shard_map/all_to_all | solution.py:97
  248.9 108.8 %all-to-all-start.12 = ((f32[24,384,96]{2,0,1:T(8,128)}), f32[24,384,96]{2,0,1:T(8,128)}, u32[]{:S(2)}, u32[]{:S(2)}) async-start(f32[24,384,96]{2,0,1:T(8,128)} %copy.76), calls=%async_computation.12 | async-start | bytes 9437184 | tf_op jit(solution)/shard_map/all_to_all | solution.py:97
  357.6 108.8 %all-to-all-start.8 = ((f32[24,384,96]{2,0,1:T(8,128)}), f32[24,384,96]{2,0,1:T(8,128)}, u32[]{:S(2)}, u32[]{:S(2)}) async-start(f32[24,384,96]{2,0,1:T(8,128)} %copy.67), calls=%async_computation.8 | async-start | bytes 9437184 | tf_op jit(solution)/shard_map/all_to_all | solution.py:97
  466.4 74.9 %all-to-all-start.13 = ((f32[2,1,442368]{2,1,0:T(1,128)}), f32[2,1,442368]{2,1,0:T(1,128)S(1)}, u32[]{:S(2)}, u32[]{:S(2)}) async-start(f32[2,1,442368]{2,1,0:T(1,128)} %reshape.97), calls=%async_computation.13 | async-start | bytes 7077888 | tf_op jit(solution)/shard_map/all_to_all | solution.py:101
  541.3 75.8 %all-to-all-start.9 = ((f32[2,1,442368]{2,1,0:T(1,128)}), f32[2,1,442368]{2,1,0:T(1,128)}, u32[]{:S(2)}, u32[]{:S(2)}) async-start(f32[2,1,442368]{2,1,0:T(1,128)} %reshape.85), calls=%async_computation.9 | async-start | bytes 7077888 | tf_op jit(solution)/shard_map/all_to_all | solution.py:101
  617.1 76.0 %all-to-all-start.5 = ((f32[2,1,442368]{2,1,0:T(1,128)}), f32[2,1,442368]{2,1,0:T(1,128)}, u32[]{:S(2)}, u32[]{:S(2)}) async-start(f32[2,1,442368]{2,1,0:T(1,128)} %reshape.93), calls=%async_computation.5 | async-start | bytes 7077888 | tf_op jit(solution)/shard_map/all_to_all | solution.py:101
  693.1 80.2 %all-to-all-start.1 = ((f32[2,1,442368]{2,1,0:T(1,128)}), f32[2,1,442368]{2,1,0:T(1,128)}, u32[]{:S(2)}, u32[]{:S(2)}) async-start(f32[2,1,442368]{2,1,0:T(1,128)} %reshape.89), calls=%async_computation.1 | async-start | bytes 7077888 | tf_op jit(solution)/shard_map/all_to_all | solution.py:101
  773.3 77.3 %all-to-all-start.14 = ((f32[48,24,768]{2,1,0:T(8,128)}), f32[48,24,768]{2,1,0:T(8,128)S(1)}, u32[]{:S(2)}, u32[]{:S(2)}) async-start(f32[48,24,768]{2,1,0:T(8,128)} %shard_map.121), calls=%async_computation.14 | async-start | bytes 7077888 | tf_op jit(solution)/shard_map/all_to_all | solution.py:108
  850.6 78.8 %all-to-all-start.10 = ((f32[48,24,768]{2,1,0:T(8,128)}), f32[48,24,768]{2,1,0:T(8,128)}, u32[]{:S(2)}, u32[]{:S(2)}) async-start(f32[48,24,768]{2,1,0:T(8,128)} %shard_map.120), calls=%async_computation.10 | async-start | bytes 7077888 | tf_op jit(solution)/shard_map/all_to_all | solution.py:108
  929.4 78.7 %all-to-all-start.6 = ((f32[48,24,768]{2,1,0:T(8,128)}), f32[48,24,768]{2,1,0:T(8,128)}, u32[]{:S(2)}, u32[]{:S(2)}) async-start(f32[48,24,768]{2,1,0:T(8,128)} %shard_map.119), calls=%async_computation.6 | async-start | bytes 7077888 | tf_op jit(solution)/shard_map/all_to_all | solution.py:108
  1008.1 57.4 %all-to-all-start.2 = ((f32[48,24,768]{2,1,0:T(8,128)}), f32[48,24,768]{2,1,0:T(8,128)}, u32[]{:S(2)}, u32[]{:S(2)}) async-start(f32[48,24,768]{2,1,0:T(8,128)} %shard_map.118), calls=%async_computation.2 | async-start | bytes 7077888 | tf_op jit(solution)/shard_map/all_to_all | solution.py:108
  1065.5 84.0 %all-to-all-start.15 = ((f32[16,1,55296]{2,1,0:T(1,128)}), f32[16,1,55296]{2,1,0:T(1,128)S(1)}, u32[]{:S(2)}, u32[]{:S(2)}) async-start(f32[16,1,55296]{2,1,0:T(1,128)} %reshape.99), calls=%async_computation.15 | async-start | bytes 7077888 | tf_op jit(solution)/shard_map/all_to_all | solution.py:112
  1149.4 83.5 %all-to-all-start.11 = ((f32[16,1,55296]{2,1,0:T(1,128)}), f32[16,1,55296]{2,1,0:T(1,128)}, u32[]{:S(2)}, u32[]{:S(2)}) async-start(f32[16,1,55296]{2,1,0:T(1,128)} %reshape.87), calls=%async_computation.11 | async-start | bytes 7077888 | tf_op jit(solution)/shard_map/all_to_all | solution.py:112
  1232.9 83.5 %all-to-all-start.7 = ((f32[16,1,55296]{2,1,0:T(1,128)}), f32[16,1,55296]{2,1,0:T(1,128)}, u32[]{:S(2)}, u32[]{:S(2)}) async-start(f32[16,1,55296]{2,1,0:T(1,128)} %reshape.95), calls=%async_computation.7 | async-start | bytes 7077888 | tf_op jit(solution)/shard_map/all_to_all | solution.py:112
  1316.4 186.1 %all-to-all-start.3 = ((f32[16,1,55296]{2,1,0:T(1,128)}), f32[16,1,55296]{2,1,0:T(1,128)}, u32[]{:S(2)}, u32[]{:S(2)}) async-start(f32[16,1,55296]{2,1,0:T(1,128)} %reshape.91), calls=%async_computation.3 | async-start | bytes 7077888 | tf_op jit(solution)/shard_map/all_to_all | solution.py:112
  1556.7 5.5 copy-start.3
  1556.7 32.5 %slice-start = ((s8[4718592]{0:T(1024)(128)(4,1)}), s8[524288]{0:T(1024)(128)(4,1)S(1)}, s32[]{:S(2)}) async-start(s8[4718592]{0:T(1024)(128)(4,1)} %bitcast.137), calls=%async_computation.16 | async-start | bytes 1048576
  1562.2 27.0 %slice-start.1 = ((s8[4718592]{0:T(1024)(128)(4,1)}), s8[4194304]{0:T(1024)(128)(4,1)S(1)}, s32[]{:S(2)}) async-start(s8[4718592]{0:T(1024)(128)(4,1)} %bitcast.137), calls=%async_computation.17 | async-start | bytes 8388608
  1562.2 27.0 %copy-start.2 = (f32[384,1536,1]{1,0,2:T(8,128)S(1)}, f32[384,1536,1]{1,0,2:T(8,128)}, u32[]{:S(2)}) copy-start(f32[384,1536,1]{1,0,2:T(8,128)} %constant.79) | copy-start | bytes 7077892
  1562.2 52.6 %slice-start.2 = ((s8[4718592]{0:T(1024)(128)(4,1)}), s8[4194304]{0:T(1024)(128)(4,1)S(1)}, s32[]{:S(2)}) async-start(s8[4718592]{0:T(1024)(128)(4,1)} %bitcast.139), calls=%async_computation.18 | async-start | bytes 8388608
  1589.2 25.6 %slice-start.3 = ((s8[4718592]{0:T(1024)(128)(4,1)}), s8[524288]{0:T(1024)(128)(4,1)S(1)}, s32[]{:S(2)}) async-start(s8[4718592]{0:T(1024)(128)(4,1)} %bitcast.139), calls=%async_computation.19 | async-start | bytes 1048576
  1589.2 25.6 %copy-start.1 = (f32[384,1536,1]{1,0,2:T(8,128)S(1)}, f32[384,1536,1]{1,0,2:T(8,128)}, u32[]{:S(2)}) copy-start(f32[384,1536,1]{1,0,2:T(8,128)} %constant.77) | copy-start | bytes 7077892
  1589.2 50.9 %slice-start.4 = ((s8[4718592]{0:T(1024)(128)(4,1)}), s8[524288]{0:T(1024)(128)(4,1)S(1)}, s32[]{:S(2)}) async-start(s8[4718592]{0:T(1024)(128)(4,1)} %bitcast.141), calls=%async_computation.20 | async-start | bytes 1048576
  1614.8 25.3 %slice-start.5 = ((s8[4718592]{0:T(1024)(128)(4,1)}), s8[4194304]{0:T(1024)(128)(4,1)S(1)}, s32[]{:S(2)}) async-start(s8[4718592]{0:T(1024)(128)(4,1)} %bitcast.141), calls=%async_computation.21 | async-start | bytes 8388608
  1614.8 25.3 %copy-start = (f32[384,1536,1]{1,0,2:T(8,128)S(1)}, f32[384,1536,1]{1,0,2:T(8,128)}, u32[]{:S(2)}) copy-start(f32[384,1536,1]{1,0,2:T(8,128)} %constant.83) | copy-start | bytes 7077892

commit v3 on v2

--- a/solution.py
+++ b/solution.py
@@ -79,40 +79,37 @@
     highest = lax.Precision.HIGHEST
     slab_levels, slab_rows, full_x = source.shape
     col_count = lax.axis_size("col")
+    row_count = lax.axis_size("row")
     full_y = slab_rows * col_count
     part_x = full_x // col_count
+    part_y = full_y // row_count
     chunk_x = part_x // chunks
     index_x = np.arange(full_x)
     table_y = cas_constant(np.arange(full_y), np.arange(full_y), full_y)
+    forward_y = table_y.reshape(col_count, slab_rows, row_count, part_y)
+    inverse_y = table_y.reshape(row_count, part_y, col_count, slab_rows)
     scale = 1.0 / (full_x * full_y)
+    wave_y = lax.axis_index("row") * part_y + lax.iota(jnp.int32, part_y)
     pressure = None
     for chunk in range(chunks):
         waves = (np.arange(col_count)[:, None] * part_x + chunk * chunk_x
                  + np.arange(chunk_x)[None, :]).reshape(-1)
-        table_chunk = cas_constant(index_x, waves, full_x)
-        table_back = cas_constant(waves, index_x, full_x)
-        along_x = jnp.einsum("zyx,xk->zky", source, table_chunk, precision=highest)
-        spectra = jnp.einsum(
-            "zxy,yk->zxk",
-            lax.all_to_all(along_x, "col", split_axis=1, concat_axis=2, tiled=True),
-            table_y,
-            precision=highest,
-        )
-        columns = lax.all_to_all(spectra, "row", split_axis=2, concat_axis=0, tiled=True)
-        part_y = columns.shape[2]
+        table_chunk = cas_constant(index_x, waves, full_x).reshape(full_x, col_count, chunk_x)
+        table_back = cas_constant(waves, index_x, full_x).reshape(col_count, chunk_x, full_x)
+        along_x = jnp.einsum("zyx,xdi->dziy", source, table_chunk, precision=highest)
+        gathered = lax.all_to_all(along_x, "col", 0, 0, tiled=True)
+        spectra = jnp.einsum("sziy,syhj->hzij", gathered, forward_y, precision=highest)
+        columns = lax.all_to_all(spectra, "row", 0, 0, tiled=True)
+        columns = columns.reshape(row_count * slab_levels, chunk_x, part_y)
         wave_x = lax.axis_index("col") * part_x + chunk * chunk_x + lax.iota(jnp.int32, chunk_x)
-        wave_y = lax.axis_index("row") * part_y + lax.iota(jnp.int32, part_y)
         eigen_sum = eigen_values(wave_x, full_x)[:, None] + eigen_values(wave_y, full_y)[None, :]
         pinned = (wave_x == 0)[:, None] & (wave_y == 0)[None, :]
         solved = vertical_solve(columns, lower_coef, upper_coef, eigen_sum, pinned)
-        returned = lax.all_to_all(solved, "row", split_axis=0, concat_axis=2, tiled=True)
-        inverse_y = jnp.einsum("zxk,ky->zxy", returned, table_y, precision=highest)
-        part = jnp.einsum(
-            "zky,kn->zyn",
-            lax.all_to_all(inverse_y, "col", split_axis=2, concat_axis=1, tiled=True),
-            table_back,
-            precision=highest,
-        )
+        solved = solved.reshape(row_count, slab_levels, chunk_x, part_y)
+        returned = lax.all_to_all(solved, "row", 0, 0, tiled=True)
+        back_y = jnp.einsum("hzij,hjsy->sziy", returned, inverse_y, precision=highest)
+        scattered = lax.all_to_all(back_y, "col", 0, 0, tiled=True)
+        part = jnp.einsum("dziy,din->zyn", scattered, table_back, precision=highest)
         pressure = part if pressure is None else pressure + part
     return pressure * scale
 

time: 1680 us -> 1310 us (0.78)
  local copies, waits for them, and re-layouts: 634 us -> 9.85 us
  waiting for transfers between devices: 330 us -> 668 us
  other arithmetic: 218 us -> 1.76 us
  matrix products: 377 us -> 502 us
    unnamed x36 -> x20, local copies, waits for them, and re-layouts: 354 us -> 1.83 us
    all_to_all x16, waiting for transfers between devices: 330 us -> 668 us  [the longest x4 293 us: body(): gathered = lax.all_to_all(along_x, 'col', 0, 0, tiled=True)]
    all_to_all x8 -> x0, other arithmetic: 216 us -> none  [the longest x4 124 us: body(): lax.all_to_all(spectra, 'row', split_axis=2, concat_axis=0, tiled=True)]
    all_to_all x21 -> x0, local copies, waits for them, and re-layouts: 157 us -> none  [the longest x5 51.6 us: body(): lax.all_to_all(spectra, 'row', split_axis=2, concat_axis=0, tiled=True)]
    dot_general x16, matrix products: 377 us -> 502 us  [the longest x4 150 us: body(): jnp.einsum('sziy,syhj->hzij', gathered, forward_y, precision=highest)]
    dot_general x12 -> x0, local copies, waits for them, and re-layouts: 109 us -> none  [the longest x4 47.5 us: body(): jnp.einsum('zxy,yk->zxk', lax.all_to_all(along_x, 'col', split_axis=1, co...]
  transfers between devices with their start and end apart: 16 -> 16, of which waited for: 7 -> 13; matrix products, arithmetic and copies ran while one was open for 60% -> 33% of each run, Pallas kernels for 2% -> 2%
where the time goes in v3:
time: 1310 us; the launch traced here: 1300 us
  waiting for transfers between devices  668 us (51%)
  matrix products  502 us (38%)
  starting transfers between devices  93.3 us (7%)
  Pallas kernels  26.1 us (2%)
    all_to_all x4, waiting for transfers between devices, body(): gathered = lax.all_to_all(along_x, 'col', 0, 0, tiled=True)  293 us
    all_to_all x4, waiting for transfers between devices, body(): scattered = lax.all_to_all(back_y, 'col', 0, 0, tiled=True)  253 us
    dot_general x4, matrix products, body(): jnp.einsum('sziy,syhj->hzij', gathered, forward_y, precision=highest)  150 us
    dot_general x4, matrix products, body(): part = jnp.einsum('dziy,din->zyn', scattered, table_back, precision=highest)  134 us
    dot_general x4, matrix products, body(): jnp.einsum('hzij,hjsy->sziy', returned, inverse_y, precision=highest)  109 us
    dot_general x4, matrix products, body(): jnp.einsum('zyx,xdi->dziy', source, table_chunk, precision=highest)  109 us
    all_to_all x4, waiting for transfers between devices, body(): returned = lax.all_to_all(solved, 'row', 0, 0, tiled=True)  93.5 us
    all_to_all x4, waiting for transfers between devices, body(): columns = lax.all_to_all(spectra, 'row', 0, 0, tiled=True)  29.1 us
  transfers between devices with their start and end apart: 16, of which 13 were waited for; matrix products, arithmetic and copies ran while one was open for 33% of the time, Pallas kernels for 2%

profile of v3, /device:TPU:15, one launch (start us, length us, event | category | flops | bytes accessed | tf_op | source)
XLA Modules:
  0.0 1302.1 jit_solution(3144063873547155797)
XLA Ops:
  0.0 27.8 %fusion.41 = f32[16,24,24,96]{3,2,1,0:T(8,128)} fusion(f32[1536,16,24,1]{0,2,3,1:T(8,128)} %constant.73, f32[24,96,1536]{2,1,0:T(8,128)} %param.12), kind=kOutput, calls=%fused_computation.36 | convolution fusion | flops 16307453952 | bytes 20054016 | tf_op jit(solution)/shard_map/zyx,xdi->dziy/dot_general | solution.py:99
  27.8 7.0 all-to-all-start
  34.8 27.1 %fusion.44 = f32[16,24,24,96]{3,2,1,0:T(8,128)} fusion(f32[1536,16,24,1]{0,2,3,1:T(8,128)S(1)} %copy-done.9, f32[24,96,1536]{2,1,0:T(8,128)} %param.12), kind=kOutput, calls=%fused_computation.37 | convolution fusion | flops 16307453952 | bytes 20054016 | tf_op jit(solution)/shard_map/zyx,xdi->dziy/dot_general | solution.py:99
  62.0 76.4 %all-to-all-done = f32[16,24,24,96]{3,2,1,0:T(8,128)} async-done(((f32[16,24,24,96]{3,2,1,0:T(8,128)}), f32[16,24,24,96]{3,2,1,0:T(8,128)}, u32[]{:S(2)}, u32[]{:S(2)}) %all-to-all-start) | async-done | bytes 3538976 | tf_op jit(solution)/shard_map/all_to_all | solution.py:100
  143.7 27.1 %fusion.47 = f32[16,24,24,96]{3,2,1,0:T(8,128)} fusion(f32[1536,16,24,1]{0,2,3,1:T(8,128)S(1)} %copy-done.8, f32[24,96,1536]{2,1,0:T(8,128)} %param.12), kind=kOutput, calls=%fused_computation.38 | convolution fusion | flops 16307453952 | bytes 20054016 | tf_op jit(solution)/shard_map/zyx,xdi->dziy/dot_general | solution.py:99
  170.8 76.5 %all-to-all-done.4 = f32[16,24,24,96]{3,2,1,0:T(8,128)} async-done(((f32[16,24,24,96]{3,2,1,0:T(8,128)}), f32[16,24,24,96]{3,2,1,0:T(8,128)}, u32[]{:S(2)}, u32[]{:S(2)}) %all-to-all-start.4) | async-done | bytes 3538976 | tf_op jit(solution)/shard_map/all_to_all | solution.py:100
  252.7 27.1 %fusion.50 = f32[16,24,24,96]{3,2,1,0:T(8,128)} fusion(f32[1536,16,24,1]{0,2,3,1:T(8,128)S(1)} %copy-done.7, f32[24,96,1536]{2,1,0:T(8,128)} %param.12), kind=kOutput, calls=%fused_computation.39 | convolution fusion | flops 16307453952 | bytes 20054016 | tf_op jit(solution)/shard_map/zyx,xdi->dziy/dot_general | solution.py:99
  279.8 76.5 %all-to-all-done.8 = f32[16,24,24,96]{3,2,1,0:T(8,128)} async-done(((f32[16,24,24,96]{3,2,1,0:T(8,128)}), f32[16,24,24,96]{3,2,1,0:T(8,128)}, u32[]{:S(2)}, u32[]{:S(2)}) %all-to-all-start.8) | async-done | bytes 3538976 | tf_op jit(solution)/shard_map/all_to_all | solution.py:100
  361.4 37.5 %fusion.53 = f32[2,24,24,768]{3,2,0,1:T(8,128)S(1)} fusion(f32[16,96,2,768,1]{3,1,0,2,4:T(8,128)} %constant.74, f32[16,24,24,96]{3,2,1,0:T(8,128)} %all-to-all-done), kind=kOutput, calls=%fused_computation.40 | convolution fusion | flops 16307453952 | bytes 16515072 | tf_op jit(solution)/shard_map/sziy,syhj->hzij/dot_general | solution.py:101
  401.0 64.0 %all-to-all-done.12 = f32[16,24,24,96]{3,2,1,0:T(8,128)} async-done(((f32[16,24,24,96]{3,2,1,0:T(8,128)}), f32[16,24,24,96]{3,2,1,0:T(8,128)}, u32[]{:S(2)}, u32[]{:S(2)}) %all-to-all-start.12) | async-done | bytes 3538976 | tf_op jit(solution)/shard_map/all_to_all | solution.py:100
  469.2 37.5 %fusion.56 = f32[2,24,24,768]{3,2,0,1:T(8,128)S(1)} fusion(f32[16,96,2,768,1]{3,1,0,2,4:T(8,128)} %constant.74, f32[16,24,24,96]{3,2,1,0:T(8,128)} %all-to-all-done.4), kind=kOutput, calls=%fused_computation.41 | convolution fusion | flops 16307453952 | bytes 16515072 | tf_op jit(solution)/shard_map/sziy,syhj->hzij/dot_general | solution.py:101
  515.2 37.5 %fusion.59 = f32[2,24,24,768]{3,2,0,1:T(8,128)S(1)} fusion(f32[16,96,2,768,1]{3,1,0,2,4:T(8,128)} %constant.74, f32[16,24,24,96]{3,2,1,0:T(8,128)} %all-to-all-done.8), kind=kOutput, calls=%fused_computation.42 | convolution fusion | flops 16307453952 | bytes 16515072 | tf_op jit(solution)/shard_map/sziy,syhj->hzij/dot_general | solution.py:101
  558.8 37.5 %fusion.62 = f32[2,24,24,768]{3,2,0,1:T(8,128)S(1)} fusion(f32[16,96,2,768,1]{3,1,0,2,4:T(8,128)} %constant.74, f32[16,24,24,96]{3,2,1,0:T(8,128)} %all-to-all-done.12), kind=kOutput, calls=%fused_computation.43 | convolution fusion | flops 16307453952 | bytes 16515072 | tf_op jit(solution)/shard_map/sziy,syhj->hzij/dot_general | solution.py:101
  612.4 29.1 %all-to-all-done.13 = f32[2,24,24,768]{3,2,1,0:T(8,128)S(1)} async-done(((f32[2,24,24,768]{3,2,1,0:T(8,128)}), f32[2,24,24,768]{3,2,1,0:T(8,128)S(1)}, u32[]{:S(2)}, u32[]{:S(2)}) %all-to-all-start.13) | async-done | bytes 3538976 | tf_op jit(solution)/shard_map/all_to_all | solution.py:102
  654.5 30.1 %all-to-all-done.2 = f32[2,24,24,768]{3,2,1,0:T(8,128)} async-done(((f32[2,24,24,768]{3,2,1,0:T(8,128)}), f32[2,24,24,768]{3,2,1,0:T(8,128)}, u32[]{:S(2)}, u32[]{:S(2)}) %all-to-all-start.2) | async-done | bytes 3538976 | tf_op jit(solution)/shard_map/all_to_all | solution.py:109
  696.3 29.0 %all-to-all-done.6 = f32[2,24,24,768]{3,2,1,0:T(8,128)S(1)} async-done(((f32[2,24,24,768]{3,2,1,0:T(8,128)}), f32[2,24,24,768]{3,2,1,0:T(8,128)S(1)}, u32[]{:S(2)}, u32[]{:S(2)}) %all-to-all-start.6) | async-done | bytes 3538976 | tf_op jit(solution)/shard_map/all_to_all | solution.py:109
  725.3 6.6 all-to-all-start.10
  738.4 28.2 %all-to-all-done.10 = f32[2,24,24,768]{3,2,1,0:T(8,128)} async-done(((f32[2,24,24,768]{3,2,1,0:T(8,128)}), f32[2,24,24,768]{3,2,1,0:T(8,128)}, u32[]{:S(2)}, u32[]{:S(2)}) %all-to-all-start.10) | async-done | bytes 3538976 | tf_op jit(solution)/shard_map/all_to_all | solution.py:109
  766.6 6.7 all-to-all-start.14
  773.3 27.6 %fusion.29 = f32[16,24,24,96]{3,2,1,0:T(8,128)} fusion(f32[2,768,16,96,1]{1,3,0,4,2:T(8,128)} %constant.75, f32[2,24,24,768]{3,2,1,0:T(8,128)} %all-to-all-done.2), kind=kOutput, calls=%fused_computation.32 | convolution fusion | flops 16307453952 | bytes 16515072 | tf_op jit(solution)/shard_map/hzij,hjsy->sziy/dot_general | solution.py:110
  807.1 11.2 all-to-all-start.3
  818.3 26.5 %fusion.32 = f32[16,24,24,96]{3,2,1,0:T(8,128)} fusion(f32[2,768,16,96,1]{1,3,0,4,2:T(8,128)} %constant.75, f32[2,24,24,768]{3,2,1,0:T(8,128)S(1)} %all-to-all-done.6), kind=kOutput, calls=%fused_computation.33 | convolution fusion | flops 16307453952 | bytes 16515072 | tf_op jit(solution)/shard_map/hzij,hjsy->sziy/dot_general | solution.py:110
  844.8 77.2 %all-to-all-done.3 = f32[16,24,24,96]{3,2,1,0:T(8,128)} async-done(((f32[16,24,24,96]{3,2,1,0:T(8,128)}), f32[16,24,24,96]{3,2,1,0:T(8,128)}, u32[]{:S(2)}, u32[]{:S(2)}) %all-to-all-start.3) | async-done | bytes 3538976 | tf_op jit(solution)/shard_map/all_to_all | solution.py:111
  927.1 27.6 %fusion.35 = f32[16,24,24,96]{3,2,1,0:T(8,128)} fusion(f32[2,768,16,96,1]{1,3,0,4,2:T(8,128)} %constant.75, f32[2,24,24,768]{3,2,1,0:T(8,128)} %all-to-all-done.10), kind=kOutput, calls=%fused_computation.34 | convolution fusion | flops 16307453952 | bytes 16515072 | tf_op jit(solution)/shard_map/hzij,hjsy->sziy/dot_general | solution.py:110
  954.7 76.1 %all-to-all-done.7 = f32[16,24,24,96]{3,2,1,0:T(8,128)} async-done(((f32[16,24,24,96]{3,2,1,0:T(8,128)}), f32[16,24,24,96]{3,2,1,0:T(8,128)}, u32[]{:S(2)}, u32[]{:S(2)}) %all-to-all-start.7) | async-done | bytes 3538976 | tf_op jit(solution)/shard_map/all_to_all | solution.py:111
  1035.9 27.6 %fusion.38 = f32[16,24,24,96]{3,2,1,0:T(8,128)} fusion(f32[2,768,16,96,1]{1,3,0,4,2:T(8,128)} %constant.75, f32[2,24,24,768]{3,2,1,0:T(8,128)} %all-to-all-done.14), kind=kOutput, calls=%fused_computation.35 | convolution fusion | flops 16307453952 | bytes 16515072 | tf_op jit(solution)/shard_map/hzij,hjsy->sziy/dot_general | solution.py:110
  1063.5 76.1 %all-to-all-done.11 = f32[16,24,24,96]{3,2,1,0:T(8,128)} async-done(((f32[16,24,24,96]{3,2,1,0:T(8,128)}), f32[16,24,24,96]{3,2,1,0:T(8,128)}, u32[]{:S(2)}, u32[]{:S(2)}) %all-to-all-start.11) | async-done | bytes 3538976 | tf_op jit(solution)/shard_map/all_to_all | solution.py:111
  1144.9 26.7 %fusion.72 = f32[24,96,1536,1]{2,1,0,3:T(8,128)} fusion(f32[16,24,24,96]{3,2,1,0:T(8,128)} %all-to-all-done.11, f32[16,24,1536,1]{2,1,3,0:T(8,128)S(1)} %copy-done.6), kind=kOutput, calls=%fused_computation.69 | convolution fusion | flops 16307453952 | bytes 20054016 | tf_op jit(solution)/shard_map/dziy,din->zyn/dot_general | solution.py:112
  1171.7 26.9 %fusion.71 = f32[24,96,1536,1]{2,1,0,3:T(8,128)} fusion(f32[16,24,24,96]{3,2,1,0:T(8,128)} %all-to-all-done.7, f32[16,24,1536,1]{2,1,3,0:T(8,128)S(1)} %copy-done.5), kind=kOutput, calls=%fused_computation.68 | convolution fusion | flops 16307453952 | bytes 20054016 | tf_op jit(solution)/shard_map/dziy,din->zyn/dot_general | solution.py:112
  1198.6 26.9 %fusion.70 = f32[24,96,1536,1]{2,1,0,3:T(8,128)} fusion(f32[16,24,24,96]{3,2,1,0:T(8,128)} %all-to-all-done.3, f32[16,24,1536,1]{2,1,3,0:T(8,128)S(1)} %copy-done.4), kind=kOutput, calls=%fused_computation.67 | convolution fusion | flops 16307453952 | bytes 20054016 | tf_op jit(solution)/shard_map/dziy,din->zyn/dot_general | solution.py:112
  1225.5 23.1 %all-to-all-done.15 = f32[16,24,24,96]{3,2,1,0:T(8,128)} async-done(((f32[16,24,24,96]{3,2,1,0:T(8,128)}), f32[16,24,24,96]{3,2,1,0:T(8,128)}, u32[]{:S(2)}, u32[]{:S(2)}) %all-to-all-start.15) | async-done | bytes 3538976 | tf_op jit(solution)/shard_map/all_to_all | solution.py:111
  1248.6 53.2 %fusion = f32[24,96,1536]{2,1,0:T(8,128)} fusion(f32[24,96,1536,1]{2,1,0,3:T(8,128)} %fusion.72, f32[24,96,1536,1]{2,1,0,3:T(8,128)} %fusion.71, f32[24,96,1536,1]{2,1,0,3:T(8,128)} %fusion.70, f32[16,24,24,96]{3,2,1,0:T(8,128)} %all-to-all-done.15, f32[16,24,1536,1]{2,1,3,0:T(8,128)S(1)} %copy-done.3), kind=kOutput, calls=%fused_computation.1 | convolution fusion | flops 16321609728 | bytes 62521344 | tf_op jit(solution)/shard_map/dziy,din->zyn/dot_general | solution.py:112
  (52 shorter events, 105.8 us)
Async XLA Ops:
  27.8 7.0 copy-start.9
  27.8 110.6 %all-to-all-start = ((f32[16,24,24,96]{3,2,1,0:T(8,128)}), f32[16,24,24,96]{3,2,1,0:T(8,128)}, u32[]{:S(2)}, u32[]{:S(2)}) async-start(f32[16,24,24,96]{3,2,1,0:T(8,128)} %fusion.41), calls=%async_computation | async-start | bytes 9437184 | tf_op jit(solution)/shard_map/all_to_all | solution.py:100
  62.0 81.7 %copy-start.8 = (f32[1536,16,24,1]{0,2,3,1:T(8,128)S(1)}, f32[1536,16,24,1]{0,2,3,1:T(8,128)}, u32[]{:S(2)}) copy-start(f32[1536,16,24,1]{0,2,3,1:T(8,128)} %constant.79) | copy-start | bytes 7077892
  138.4 108.8 %all-to-all-start.4 = ((f32[16,24,24,96]{3,2,1,0:T(8,128)}), f32[16,24,24,96]{3,2,1,0:T(8,128)}, u32[]{:S(2)}, u32[]{:S(2)}) async-start(f32[16,24,24,96]{3,2,1,0:T(8,128)} %fusion.44), calls=%async_computation.4 | async-start | bytes 9437184 | tf_op jit(solution)/shard_map/all_to_all | solution.py:100
  170.7 81.9 %copy-start.7 = (f32[1536,16,24,1]{0,2,3,1:T(8,128)S(1)}, f32[1536,16,24,1]{0,2,3,1:T(8,128)}, u32[]{:S(2)}) copy-start(f32[1536,16,24,1]{0,2,3,1:T(8,128)} %constant.81) | copy-start | bytes 7077892
  247.2 109.0 %all-to-all-start.8 = ((f32[16,24,24,96]{3,2,1,0:T(8,128)}), f32[16,24,24,96]{3,2,1,0:T(8,128)}, u32[]{:S(2)}, u32[]{:S(2)}) async-start(f32[16,24,24,96]{3,2,1,0:T(8,128)} %fusion.47), calls=%async_computation.8 | async-start | bytes 9437184 | tf_op jit(solution)/shard_map/all_to_all | solution.py:100
  356.2 108.8 %all-to-all-start.12 = ((f32[16,24,24,96]{3,2,1,0:T(8,128)}), f32[16,24,24,96]{3,2,1,0:T(8,128)}, u32[]{:S(2)}, u32[]{:S(2)}) async-start(f32[16,24,24,96]{3,2,1,0:T(8,128)} %fusion.50), calls=%async_computation.12 | async-start | bytes 9437184 | tf_op jit(solution)/shard_map/all_to_all | solution.py:100
  465.0 43.7 %all-to-all-start.1 = ((f32[2,24,24,768]{3,2,1,0:T(8,128)}), f32[2,24,24,768]{3,2,1,0:T(8,128)S(1)}, u32[]{:S(2)}, u32[]{:S(2)}) async-start(f32[2,24,24,768]{3,2,1,0:T(8,128)} %copy.42), calls=%async_computation.1 | async-start | bytes 7077888 | tf_op jit(solution)/shard_map/all_to_all | solution.py:102
  508.7 44.0 %copy-start.1 = (f32[2,24,24,768]{3,2,1,0:T(8,128)}, f32[2,24,24,768]{3,2,1,0:T(8,128)S(1)}, u32[]{:S(2)}) copy-start(f32[2,24,24,768]{3,2,1,0:T(8,128)S(1)} %all-to-all-done.1) | copy-start | bytes 10616836
  508.7 46.0 %all-to-all-start.5 = ((f32[2,24,24,768]{3,2,1,0:T(8,128)}), f32[2,24,24,768]{3,2,1,0:T(8,128)}, u32[]{:S(2)}, u32[]{:S(2)}) async-start(f32[2,24,24,768]{3,2,1,0:T(8,128)} %copy.45), calls=%async_computation.5 | async-start | bytes 7077888 | tf_op jit(solution)/shard_map/all_to_all | solution.py:102
  554.7 43.5 %all-to-all-start.9 = ((f32[2,24,24,768]{3,2,1,0:T(8,128)}), f32[2,24,24,768]{3,2,1,0:T(8,128)S(1)}, u32[]{:S(2)}, u32[]{:S(2)}) async-start(f32[2,24,24,768]{3,2,1,0:T(8,128)} %copy.48), calls=%async_computation.9 | async-start | bytes 7077888 | tf_op jit(solution)/shard_map/all_to_all | solution.py:102
  598.2 1.8 copy-start.2
  600.0 41.4 %all-to-all-start.13 = ((f32[2,24,24,768]{3,2,1,0:T(8,128)}), f32[2,24,24,768]{3,2,1,0:T(8,128)S(1)}, u32[]{:S(2)}, u32[]{:S(2)}) async-start(f32[2,24,24,768]{3,2,1,0:T(8,128)} %copy.51), calls=%async_computation.13 | async-start | bytes 7077888 | tf_op jit(solution)/shard_map/all_to_all | solution.py:102
  641.5 13.0 %copy-start = (f32[2,24,24,768]{3,2,1,0:T(8,128)}, f32[2,24,24,768]{3,2,1,0:T(8,128)S(1)}, u32[]{:S(2)}) copy-start(f32[2,24,24,768]{3,2,1,0:T(8,128)S(1)} %all-to-all-done.13) | copy-start | bytes 10616836
  641.5 43.1 %all-to-all-start.2 = ((f32[2,24,24,768]{3,2,1,0:T(8,128)}), f32[2,24,24,768]{3,2,1,0:T(8,128)}, u32[]{:S(2)}, u32[]{:S(2)}) async-start(f32[2,24,24,768]{3,2,1,0:T(8,128)} %bitcast.175), calls=%async_computation.2 | async-start | bytes 7077888 | tf_op jit(solution)/shard_map/all_to_all | solution.py:109
  684.6 40.7 %all-to-all-start.6 = ((f32[2,24,24,768]{3,2,1,0:T(8,128)}), f32[2,24,24,768]{3,2,1,0:T(8,128)S(1)}, u32[]{:S(2)}, u32[]{:S(2)}) async-start(f32[2,24,24,768]{3,2,1,0:T(8,128)} %bitcast.176), calls=%async_computation.6 | async-start | bytes 7077888 | tf_op jit(solution)/shard_map/all_to_all | solution.py:109
  725.3 41.3 %all-to-all-start.10 = ((f32[2,24,24,768]{3,2,1,0:T(8,128)}), f32[2,24,24,768]{3,2,1,0:T(8,128)}, u32[]{:S(2)}, u32[]{:S(2)}) async-start(f32[2,24,24,768]{3,2,1,0:T(8,128)} %bitcast.174), calls=%async_computation.10 | async-start | bytes 7077888 | tf_op jit(solution)/shard_map/all_to_all | solution.py:109
  766.6 40.5 %all-to-all-start.14 = ((f32[2,24,24,768]{3,2,1,0:T(8,128)}), f32[2,24,24,768]{3,2,1,0:T(8,128)}, u32[]{:S(2)}, u32[]{:S(2)}) async-start(f32[2,24,24,768]{3,2,1,0:T(8,128)} %bitcast.177), calls=%async_computation.14 | async-start | bytes 7077888 | tf_op jit(solution)/shard_map/all_to_all | solution.py:109
  807.1 114.9 %all-to-all-start.3 = ((f32[16,24,24,96]{3,2,1,0:T(8,128)}), f32[16,24,24,96]{3,2,1,0:T(8,128)}, u32[]{:S(2)}, u32[]{:S(2)}) async-start(f32[16,24,24,96]{3,2,1,0:T(8,128)} %fusion.29), calls=%async_computation.3 | async-start | bytes 9437184 | tf_op jit(solution)/shard_map/all_to_all | solution.py:111
  922.0 108.8 %all-to-all-start.7 = ((f32[16,24,24,96]{3,2,1,0:T(8,128)}), f32[16,24,24,96]{3,2,1,0:T(8,128)}, u32[]{:S(2)}, u32[]{:S(2)}) async-start(f32[16,24,24,96]{3,2,1,0:T(8,128)} %fusion.32), calls=%async_computation.7 | async-start | bytes 9437184 | tf_op jit(solution)/shard_map/all_to_all | solution.py:111
  1030.8 108.8 %all-to-all-start.11 = ((f32[16,24,24,96]{3,2,1,0:T(8,128)}), f32[16,24,24,96]{3,2,1,0:T(8,128)}, u32[]{:S(2)}, u32[]{:S(2)}) async-start(f32[16,24,24,96]{3,2,1,0:T(8,128)} %fusion.35), calls=%async_computation.11 | async-start | bytes 9437184 | tf_op jit(solution)/shard_map/all_to_all | solution.py:111
  1063.5 81.4 %copy-start.6 = (f32[16,24,1536,1]{2,1,3,0:T(8,128)S(1)}, f32[16,24,1536,1]{2,1,3,0:T(8,128)}, u32[]{:S(2)}) copy-start(f32[16,24,1536,1]{2,1,3,0:T(8,128)} %constant.80) | copy-start | bytes 7077892
  1139.6 109.0 %all-to-all-start.15 = ((f32[16,24,24,96]{3,2,1,0:T(8,128)}), f32[16,24,24,96]{3,2,1,0:T(8,128)}, u32[]{:S(2)}, u32[]{:S(2)}) async-start(f32[16,24,24,96]{3,2,1,0:T(8,128)} %fusion.38), calls=%async_computation.15 | async-start | bytes 9437184 | tf_op jit(solution)/shard_map/all_to_all | solution.py:111
  1144.9 26.8 %copy-start.5 = (f32[16,24,1536,1]{2,1,3,0:T(8,128)S(1)}, f32[16,24,1536,1]{2,1,3,0:T(8,128)}, u32[]{:S(2)}) copy-start(f32[16,24,1536,1]{2,1,3,0:T(8,128)} %constant.78) | copy-start | bytes 7077892
  1171.7 26.9 %copy-start.4 = (f32[16,24,1536,1]{2,1,3,0:T(8,128)S(1)}, f32[16,24,1536,1]{2,1,3,0:T(8,128)}, u32[]{:S(2)}) copy-start(f32[16,24,1536,1]{2,1,3,0:T(8,128)} %constant.76) | copy-start | bytes 7077892
  1198.6 50.0 %copy-start.3 = (f32[16,24,1536,1]{2,1,3,0:T(8,128)S(1)}, f32[16,24,1536,1]{2,1,3,0:T(8,128)}, u32[]{:S(2)}) copy-start(f32[16,24,1536,1]{2,1,3,0:T(8,128)} %constant.82) | copy-start | bytes 7077892

commit v4 on v3

--- a/solution.py
+++ b/solution.py
@@ -90,14 +90,17 @@
     inverse_y = table_y.reshape(row_count, part_y, col_count, slab_rows)
     scale = 1.0 / (full_x * full_y)
     wave_y = lax.axis_index("row") * part_y + lax.iota(jnp.int32, part_y)
-    pressure = None
-    for chunk in range(chunks):
-        waves = (np.arange(col_count)[:, None] * part_x + chunk * chunk_x
-                 + np.arange(chunk_x)[None, :]).reshape(-1)
-        table_chunk = cas_constant(index_x, waves, full_x).reshape(full_x, col_count, chunk_x)
-        table_back = cas_constant(waves, index_x, full_x).reshape(col_count, chunk_x, full_x)
-        along_x = jnp.einsum("zyx,xdi->dziy", source, table_chunk, precision=highest)
-        gathered = lax.all_to_all(along_x, "col", 0, 0, tiled=True)
+
+    def chunk_waves(chunk):
+        return (np.arange(col_count)[:, None] * part_x + chunk * chunk_x
+                + np.arange(chunk_x)[None, :]).reshape(-1)
+
+    def along_x(chunk, slab):
+        table_chunk = cas_constant(index_x, chunk_waves(chunk), full_x).reshape(full_x, col_count, chunk_x)
+        spread = jnp.einsum("zyx,xdi->dziy", slab, table_chunk, precision=highest)
+        return lax.all_to_all(spread, "col", 0, 0, tiled=True)
+
+    def middle(chunk, gathered):
         spectra = jnp.einsum("sziy,syhj->hzij", gathered, forward_y, precision=highest)
         columns = lax.all_to_all(spectra, "row", 0, 0, tiled=True)
         columns = columns.reshape(row_count * slab_levels, chunk_x, part_y)
@@ -107,10 +110,27 @@
         solved = vertical_solve(columns, lower_coef, upper_coef, eigen_sum, pinned)
         solved = solved.reshape(row_count, slab_levels, chunk_x, part_y)
         returned = lax.all_to_all(solved, "row", 0, 0, tiled=True)
-        back_y = jnp.einsum("hzij,hjsy->sziy", returned, inverse_y, precision=highest)
+        return jnp.einsum("hzij,hjsy->sziy", returned, inverse_y, precision=highest)
+
+    def back_x(chunk, back_y):
+        table_back = cas_constant(chunk_waves(chunk), index_x, full_x).reshape(col_count, chunk_x, full_x)
         scattered = lax.all_to_all(back_y, "col", 0, 0, tiled=True)
-        part = jnp.einsum("dziy,din->zyn", scattered, table_back, precision=highest)
-        pressure = part if pressure is None else pressure + part
+        return jnp.einsum("dziy,din->zyn", scattered, table_back, precision=highest)
+
+    gathered = along_x(0, source)
+    gathered, source = lax.optimization_barrier((gathered, source))
+    pressure = None
+    back_y = None
+    for chunk in range(chunks):
+        gathered_next = along_x(chunk + 1, source) if chunk + 1 < chunks else None
+        if back_y is not None:
+            part = back_x(chunk - 1, back_y)
+            pressure = part if pressure is None else pressure + part
+        back_y = middle(chunk, gathered)
+        gathered = gathered_next
+        gathered, back_y, pressure, source = lax.optimization_barrier((gathered, back_y, pressure, source))
+    part = back_x(chunks - 1, back_y)
+    pressure = part if pressure is None else pressure + part
     return pressure * scale
 
 

time: 1310 us -> 1500 us (1.15)
  blocking collectives: 0 us -> 351 us
  waiting for transfers between devices: 668 us -> 549 us
  matrix products: 502 us -> 468 us
  starting transfers between devices: 93.3 us -> 63.3 us
  local copies, waits for them, and re-layouts: 9.85 us -> 29.9 us
    all_to_all x0 -> x5, blocking collectives: none -> 351 us  [the longest x3 133 us: middle(): columns = lax.all_to_all(spectra, 'row', 0, 0, tiled=True)]
    all_to_all x16 -> x11, waiting for transfers between devices: 668 us -> 549 us  [the longest x3 227 us: back_x(): scattered = lax.all_to_all(back_y, 'col', 0, 0, tiled=True)]
    dot_general x16, matrix products: 502 us -> 468 us  [the longest x4 148 us: middle(): jnp.einsum('sziy,syhj->hzij', gathered, forward_y, precision=highest)]
    all_to_all x16 -> x11, starting transfers between devices: 93.3 us -> 63.3 us  [the longest x4 20.8 us: middle(): returned = lax.all_to_all(solved, 'row', 0, 0, tiled=True)]
    optimization_barrier x0 -> x4, local copies, waits for them, and re-layouts: none -> 15.4 us  [body(): lax.optimization_barrier((gathered, back_y, pressure, source))]
  transfers between devices with their start and end apart: 16 -> 11, of which waited for: 13 -> 11; matrix products, arithmetic and copies ran while one was open for 33% -> 18% of each run, Pallas kernels for 2% -> 0%
where the time goes in v4:
time: 1500 us; the launch traced here: 1490 us
  waiting for transfers between devices  549 us (37%)
  matrix products  468 us (31%)
  blocking collectives  351 us (23%)
  starting transfers between devices  63.3 us (4%)
  local copies, waits for them, and re-layouts  29.9 us (2%)
  Pallas kernels  26 us (2%)
    all_to_all x3, waiting for transfers between devices, back_x(): scattered = lax.all_to_all(back_y, 'col', 0, 0, tiled=True)  227 us
    all_to_all x3, waiting for transfers between devices, along_x(): return lax.all_to_all(spread, 'col', 0, 0, tiled=True)  176 us
    dot_general x4, matrix products, middle(): jnp.einsum('sziy,syhj->hzij', gathered, forward_y, precision=highest)  148 us
    all_to_all x3, blocking collectives, middle(): columns = lax.all_to_all(spectra, 'row', 0, 0, tiled=True)  133 us
    all_to_all x1, blocking collectives, along_x(): return lax.all_to_all(spread, 'col', 0, 0, tiled=True)  110 us
    all_to_all x4, waiting for transfers between devices, middle(): returned = lax.all_to_all(solved, 'row', 0, 0, tiled=True)  109 us
    all_to_all x1, blocking collectives, back_x(): scattered = lax.all_to_all(back_y, 'col', 0, 0, tiled=True)  108 us
    dot_general x4, matrix products, back_x(): return jnp.einsum('dziy,din->zyn', scattered, table_back, precision=highest)  108 us
  transfers between devices with their start and end apart: 11, of which 11 were waited for; matrix products, arithmetic and copies ran while one was open for 18% of the time, Pallas kernels for 0%

profile of v4, /device:TPU:15, one launch (start us, length us, event | category | flops | bytes accessed | tf_op | source)
XLA Modules:
  0.0 1490.6 jit_solution(2661147493726819412)
XLA Ops:
  0.0 26.4 %fusion.37 = f32[16,24,24,96]{3,2,1,0:T(8,128)S(1)} fusion(f32[1536,16,24,1]{0,2,3,1:T(8,128)} %constant.73, f32[24,96,1536]{2,1,0:T(8,128)} %param.12), kind=kOutput, calls=%fused_computation.33 | convolution fusion | flops 16307453952 | bytes 20054016 | tf_op jit(solution)/shard_map/zyx,xdi->dziy/dot_general | solution.py:100
  26.5 110.3 %all_to_all.80 = f32[16,24,24,96]{3,2,1,0:T(8,128)S(1)} all-to-all(f32[16,24,24,96]{3,2,1,0:T(8,128)S(1)} %fusion.37), channel_id=1, replica_groups=mesh['row'=2,'col'=16] {'col'}, dimensions={0} | all-to-all | bytes 7077888 | tf_op jit(solution)/shard_map/all_to_all | solution.py:101
  136.8 35.6 %fusion.49 = f32[2,24,24,768]{3,2,0,1:T(8,128)S(1)} fusion(f32[16,96,2,768,1]{3,1,0,2,4:T(8,128)S(1)} %copy-done.6, f32[16,24,24,96]{3,2,1,0:T(8,128)S(1)} %all_to_all.80), kind=kOutput, calls=%fused_computation.37 | convolution fusion | flops 16307453952 | bytes 16515072 | tf_op jit(solution)/shard_map/sziy,syhj->hzij/dot_general | solution.py:104
  180.6 37.3 %all-to-all-done.2 = f32[2,24,24,768]{3,2,1,0:T(8,128)S(1)} async-done(((f32[2,24,24,768]{3,2,1,0:T(8,128)}), f32[2,24,24,768]{3,2,1,0:T(8,128)S(1)}, u32[]{:S(2)}, u32[]{:S(2)}) %all-to-all-start.2) | async-done | bytes 3538976 | tf_op jit(solution)/shard_map/all_to_all | solution.py:105
  231.5 25.8 %fusion.40 = f32[16,24,24,96]{3,2,0,1:T(8,128)S(1)} fusion(f32[1536,16,24,1]{0,2,1,3:T(8,128)} %constant.74, f32[24,96,1536]{2,1,0:T(8,128)} %param.12), kind=kOutput, calls=%fused_computation.34 | convolution fusion | flops 16307453952 | bytes 20054016 | tf_op jit(solution)/shard_map/zyx,xdi->dziy/dot_general | solution.py:100
  260.0 9.7 all-to-all-done.3
  277.0 26.6 %fusion.25 = f32[16,24,24,96]{3,2,0,1:T(8,128)} fusion(f32[2,768,16,96,1]{1,3,0,2,4:T(8,128)} %constant.76, f32[2,24,24,768]{3,2,1,0:T(8,128)S(1)} %all-to-all-done.3), kind=kOutput, calls=%fused_computation.29 | convolution fusion | flops 16307453952 | bytes 16515072 | tf_op jit(solution)/shard_map/hzij,hjsy->sziy/dot_general | solution.py:113
  303.6 77.0 %all-to-all-done.1 = f32[16,24,24,96]{3,2,1,0:T(8,128)} async-done(((f32[16,24,24,96]{3,2,1,0:T(8,128)}), f32[16,24,24,96]{3,2,1,0:T(8,128)}, u32[]{:S(2)}, u32[]{:S(2)}) %all-to-all-start.1) | async-done | bytes 3538976 | tf_op jit(solution)/shard_map/all_to_all | solution.py:101
  380.6 37.6 %fusion.52 = f32[2,24,24,768]{3,2,0,1:T(8,128)S(1)} fusion(f32[16,96,2,768,1]{3,1,0,2,4:T(8,128)} %constant.75, f32[16,24,24,96]{3,2,1,0:T(8,128)} %all-to-all-done.1), kind=kOutput, calls=%fused_computation.38 | convolution fusion | flops 16307453952 | bytes 16515072 | tf_op jit(solution)/shard_map/sziy,syhj->hzij/dot_general | solution.py:104
  418.5 44.2 %all_to_all.81 = f32[2,24,24,768]{3,2,1,0:T(8,128)} all-to-all(f32[2,24,24,768]{3,2,1,0:T(8,128)S(1)} %copy.28), channel_id=1, replica_groups=mesh['row'=2,'col'=16] {'row'}, dimensions={0} | all-to-all | bytes 7077888 | tf_op jit(solution)/shard_map/all_to_all | solution.py:105
  479.3 33.2 %all-to-all-done.6 = f32[2,24,24,768]{3,2,1,0:T(8,128)S(1)} async-done(((f32[2,24,24,768]{3,2,1,0:T(8,128)}), f32[2,24,24,768]{3,2,1,0:T(8,128)S(1)}, u32[]{:S(2)}, u32[]{:S(2)}) %all-to-all-start.6) | async-done | bytes 3538976 | tf_op jit(solution)/shard_map/all_to_all | solution.py:112
  519.1 25.8 %fusion.43 = f32[16,24,24,96]{3,2,0,1:T(8,128)S(1)} fusion(f32[1536,16,24,1]{0,2,1,3:T(8,128)} %constant.77, f32[24,96,1536]{2,1,0:T(8,128)} %param.12), kind=kOutput, calls=%fused_computation.35 | convolution fusion | flops 16307453952 | bytes 20054016 | tf_op jit(solution)/shard_map/zyx,xdi->dziy/dot_general | solution.py:100
  547.7 75.0 %all-to-all-done.7 = f32[16,24,24,96]{3,2,1,0:T(8,128)} async-done(((f32[16,24,24,96]{3,2,1,0:T(8,128)}), f32[16,24,24,96]{3,2,1,0:T(8,128)}, u32[]{:S(2)}, u32[]{:S(2)}) %all-to-all-start.7) | async-done | bytes 3538976 | tf_op jit(solution)/shard_map/all_to_all | solution.py:117
  628.1 26.7 %fusion.28 = f32[16,24,24,96]{3,2,0,1:T(8,128)} fusion(f32[2,768,16,96,1]{1,3,0,2,4:T(8,128)} %constant.76, f32[2,24,24,768]{3,2,1,0:T(8,128)S(1)} %all-to-all-done.6), kind=kOutput, calls=%fused_computation.30 | convolution fusion | flops 16307453952 | bytes 16515072 | tf_op jit(solution)/shard_map/hzij,hjsy->sziy/dot_general | solution.py:113
  654.9 26.8 %convolution_bitcast_fusion = f32[24,96,1536]{2,1,0:T(8,128)} fusion(f32[16,24,24,96]{3,2,1,0:T(8,128)} %all-to-all-done.7, f32[16,24,1536,1]{2,1,3,0:T(8,128)S(1)} %copy-done.5), kind=kOutput, calls=%fused_computation.12 | convolution fusion | flops 16307453952 | bytes 20054016 | tf_op jit(solution)/shard_map/dziy,din->zyn/dot_general | solution.py:118
  681.6 50.0 %all-to-all-done.4 = f32[16,24,24,96]{3,2,1,0:T(8,128)} async-done(((f32[16,24,24,96]{3,2,1,0:T(8,128)}), f32[16,24,24,96]{3,2,1,0:T(8,128)}, u32[]{:S(2)}, u32[]{:S(2)}) %all-to-all-start.4) | async-done | bytes 3538976 | tf_op jit(solution)/shard_map/all_to_all | solution.py:101
  731.7 37.5 %fusion.55 = f32[2,24,24,768]{3,2,0,1:T(8,128)S(1)} fusion(f32[16,96,2,768,1]{3,1,0,2,4:T(8,128)} %constant.75, f32[16,24,24,96]{3,2,1,0:T(8,128)} %all-to-all-done.4), kind=kOutput, calls=%fused_computation.39 | convolution fusion | flops 16307453952 | bytes 16515072 | tf_op jit(solution)/shard_map/sziy,syhj->hzij/dot_general | solution.py:104
  769.5 44.2 %all_to_all.82 = f32[2,24,24,768]{3,2,1,0:T(8,128)} all-to-all(f32[2,24,24,768]{3,2,1,0:T(8,128)S(1)} %copy.34), channel_id=1, replica_groups=mesh['row'=2,'col'=16] {'row'}, dimensions={0} | all-to-all | bytes 7077888 | tf_op jit(solution)/shard_map/all_to_all | solution.py:105
  830.3 33.1 %all-to-all-done.10 = f32[2,24,24,768]{3,2,1,0:T(8,128)S(1)} async-done(((f32[2,24,24,768]{3,2,1,0:T(8,128)}), f32[2,24,24,768]{3,2,1,0:T(8,128)S(1)}, u32[]{:S(2)}, u32[]{:S(2)}) %all-to-all-start.10) | async-done | bytes 3538976 | tf_op jit(solution)/shard_map/all_to_all | solution.py:112
  871.9 25.8 %fusion.46 = f32[16,24,24,96]{3,2,0,1:T(8,128)S(1)} fusion(f32[1536,16,24,1]{0,2,1,3:T(8,128)} %constant.79, f32[24,96,1536]{2,1,0:T(8,128)} %param.12), kind=kOutput, calls=%fused_computation.36 | convolution fusion | flops 16307453952 | bytes 20054016 | tf_op jit(solution)/shard_map/zyx,xdi->dziy/dot_general | solution.py:100
  900.4 75.1 %all-to-all-done.11 = f32[16,24,24,96]{3,2,1,0:T(8,128)} async-done(((f32[16,24,24,96]{3,2,1,0:T(8,128)}), f32[16,24,24,96]{3,2,1,0:T(8,128)}, u32[]{:S(2)}, u32[]{:S(2)}) %all-to-all-start.11) | async-done | bytes 3538976 | tf_op jit(solution)/shard_map/all_to_all | solution.py:117
  981.1 27.8 %fusion.31 = f32[16,24,24,96]{3,2,0,1:T(8,128)} fusion(f32[2,768,16,96,1]{1,3,0,2,4:T(8,128)} %constant.76, f32[2,24,24,768]{3,2,1,0:T(8,128)} %copy-done.2), kind=kOutput, calls=%fused_computation.31 | convolution fusion | flops 16307453952 | bytes 16515072 | tf_op jit(solution)/shard_map/hzij,hjsy->sziy/dot_general | solution.py:113
  1009.0 26.8 %bitcast_add_fusion.2 = f32[24,96,1536]{2,1,0:T(8,128)} fusion(f32[24,96,1536]{2,1,0:T(8,128)S(1)} %bitcast.165, f32[16,24,24,96]{3,2,1,0:T(8,128)} %all-to-all-done.11, f32[16,24,1536,1]{2,1,3,0:T(8,128)S(1)} %copy-done.4), kind=kOutput, calls=%fused_computation.9 | convolution fusion | flops 16310992896 | bytes 34209792 | tf_op jit(solution)/shard_map/dziy,din->zyn/dot_general | solution.py:118
  1035.8 48.8 %all-to-all-done.8 = f32[16,24,24,96]{3,2,1,0:T(8,128)} async-done(((f32[16,24,24,96]{3,2,1,0:T(8,128)}), f32[16,24,24,96]{3,2,1,0:T(8,128)}, u32[]{:S(2)}, u32[]{:S(2)}) %all-to-all-start.8) | async-done | bytes 3538976 | tf_op jit(solution)/shard_map/all_to_all | solution.py:101
  1084.6 37.5 %fusion.58 = f32[2,24,24,768]{3,2,0,1:T(8,128)S(1)} fusion(f32[16,96,2,768,1]{3,1,0,2,4:T(8,128)} %constant.75, f32[16,24,24,96]{3,2,1,0:T(8,128)} %all-to-all-done.8), kind=kOutput, calls=%fused_computation.40 | convolution fusion | flops 16307453952 | bytes 16515072 | tf_op jit(solution)/shard_map/sziy,syhj->hzij/dot_general | solution.py:104
  1122.4 44.2 %all_to_all.83 = f32[2,24,24,768]{3,2,1,0:T(8,128)} all-to-all(f32[2,24,24,768]{3,2,1,0:T(8,128)S(1)} %copy.39), channel_id=1, replica_groups=mesh['row'=2,'col'=16] {'row'}, dimensions={0} | all-to-all | bytes 7077888 | tf_op jit(solution)/shard_map/all_to_all | solution.py:105
  1183.2 33.2 %all-to-all-done.13 = f32[2,24,24,768]{3,2,1,0:T(8,128)S(1)} async-done(((f32[2,24,24,768]{3,2,1,0:T(8,128)}), f32[2,24,24,768]{3,2,1,0:T(8,128)S(1)}, u32[]{:S(2)}, u32[]{:S(2)}) %all-to-all-start.13) | async-done | bytes 3538976 | tf_op jit(solution)/shard_map/all_to_all | solution.py:112
  1223.1 26.7 %fusion.34 = f32[16,24,24,96]{3,2,0,1:T(8,128)} fusion(f32[2,768,16,96,1]{1,3,0,2,4:T(8,128)} %constant.76, f32[2,24,24,768]{3,2,1,0:T(8,128)S(1)} %all-to-all-done.13), kind=kOutput, calls=%fused_computation.32 | convolution fusion | flops 16307453952 | bytes 16515072 | tf_op jit(solution)/shard_map/hzij,hjsy->sziy/dot_general | solution.py:113
  1249.8 76.9 %all-to-all-done.14 = f32[16,24,24,96]{3,2,1,0:T(8,128)} async-done(((f32[16,24,24,96]{3,2,1,0:T(8,128)}), f32[16,24,24,96]{3,2,1,0:T(8,128)}, u32[]{:S(2)}, u32[]{:S(2)}) %all-to-all-start.14) | async-done | bytes 3538976 | tf_op jit(solution)/shard_map/all_to_all | solution.py:117
  1326.6 28.7 %bitcast_add_fusion.1 = f32[24,96,1536]{2,1,0:T(8,128)S(1)} fusion(f32[24,96,1536]{2,1,0:T(8,128)} %bitcast_add_fusion.2, f32[16,24,24,96]{3,2,1,0:T(8,128)} %all-to-all-done.14, f32[16,24,1536,1]{2,1,3,0:T(8,128)} %constant.81), kind=kOutput, calls=%fused_computation.8 | convolution fusion | flops 16310992896 | bytes 34209792 | tf_op jit(solution)/shard_map/dziy,din->zyn/dot_general | solution.py:118
  1355.9 108.5 %all_to_all.84 = f32[16,24,24,96]{3,2,1,0:T(8,128)S(1)} all-to-all(f32[16,24,24,96]{3,2,1,0:T(8,128)S(1)} %copy.43), channel_id=1, replica_groups=mesh['row'=2,'col'=16] {'col'}, dimensions={0} | all-to-all | bytes 7077888 | tf_op jit(solution)/shard_map/all_to_all | solution.py:117
  1464.4 26.0 %fusion.6 = f32[24,96,1536]{2,1,0:T(8,128)} fusion(f32[24,96,1536]{2,1,0:T(8,128)S(1)} %bitcast_add_fusion.1, f32[16,24,24,96]{3,2,1,0:T(8,128)S(1)} %all_to_all.84, f32[16,24,1536,1]{2,1,3,0:T(8,128)S(1)} %copy-done.3), kind=kOutput, calls=%fused_computation.7 | convolution fusion | flops 16314531840 | bytes 34209792 | tf_op jit(solution)/shard_map/dziy,din->zyn/dot_general | solution.py:118
  (57 shorter events, 121.0 us)
Async XLA Ops:
  26.4 110.3 %copy-start.6 = (f32[16,96,2,768,1]{3,1,0,2,4:T(8,128)S(1)}, f32[16,96,2,768,1]{3,1,0,2,4:T(8,128)}, u32[]{:S(2)}) copy-start(f32[16,96,2,768,1]{3,1,0,2,4:T(8,128)} %constant.75) | copy-start | bytes 28311556
  174.5 43.3 %all-to-all-start.2 = ((f32[2,24,24,768]{3,2,1,0:T(8,128)}), f32[2,24,24,768]{3,2,1,0:T(8,128)S(1)}, u32[]{:S(2)}, u32[]{:S(2)}) async-start(f32[2,24,24,768]{3,2,1,0:T(8,128)} %copy.24), calls=%async_computation.2 | async-start | bytes 7077888 | tf_op jit(solution)/shard_map/all_to_all | solution.py:105
  217.8 1.8 copy-start
  226.1 43.5 %all-to-all-start.3 = ((f32[2,24,24,768]{3,2,1,0:T(8,128)}), f32[2,24,24,768]{3,2,1,0:T(8,128)S(1)}, u32[]{:S(2)}, u32[]{:S(2)}) async-start(f32[2,24,24,768]{3,2,1,0:T(8,128)} %bitcast.167), calls=%async_computation.3 | async-start | bytes 7077888 | tf_op jit(solution)/shard_map/all_to_all | solution.py:112
  269.7 110.9 %all-to-all-start.1 = ((f32[16,24,24,96]{3,2,1,0:T(8,128)}), f32[16,24,24,96]{3,2,1,0:T(8,128)}, u32[]{:S(2)}, u32[]{:S(2)}) async-start(f32[16,24,24,96]{3,2,1,0:T(8,128)} %copy.22), calls=%async_computation.1 | async-start | bytes 9437184 | tf_op jit(solution)/shard_map/all_to_all | solution.py:101
  469.2 43.3 %all-to-all-start.6 = ((f32[2,24,24,768]{3,2,1,0:T(8,128)}), f32[2,24,24,768]{3,2,1,0:T(8,128)S(1)}, u32[]{:S(2)}, u32[]{:S(2)}) async-start(f32[2,24,24,768]{3,2,1,0:T(8,128)} %bitcast.168), calls=%async_computation.6 | async-start | bytes 7077888 | tf_op jit(solution)/shard_map/all_to_all | solution.py:112
  512.5 110.2 %all-to-all-start.7 = ((f32[16,24,24,96]{3,2,1,0:T(8,128)}), f32[16,24,24,96]{3,2,1,0:T(8,128)}, u32[]{:S(2)}, u32[]{:S(2)}) async-start(f32[16,24,24,96]{3,2,1,0:T(8,128)} %copy.30), calls=%async_computation.7 | async-start | bytes 9437184 | tf_op jit(solution)/shard_map/all_to_all | solution.py:117
  622.7 109.0 %all-to-all-start.4 = ((f32[16,24,24,96]{3,2,1,0:T(8,128)}), f32[16,24,24,96]{3,2,1,0:T(8,128)}, u32[]{:S(2)}, u32[]{:S(2)}) async-start(f32[16,24,24,96]{3,2,1,0:T(8,128)} %copy.26), calls=%async_computation.4 | async-start | bytes 9437184 | tf_op jit(solution)/shard_map/all_to_all | solution.py:101
  628.1 26.8 %copy-start.5 = (f32[16,24,1536,1]{2,1,3,0:T(8,128)S(1)}, f32[16,24,1536,1]{2,1,3,0:T(8,128)}, u32[]{:S(2)}) copy-start(f32[16,24,1536,1]{2,1,3,0:T(8,128)} %constant.78) | copy-start | bytes 7077892
  820.1 43.3 %all-to-all-start.10 = ((f32[2,24,24,768]{3,2,1,0:T(8,128)}), f32[2,24,24,768]{3,2,1,0:T(8,128)S(1)}, u32[]{:S(2)}, u32[]{:S(2)}) async-start(f32[2,24,24,768]{3,2,1,0:T(8,128)} %bitcast.169), calls=%async_computation.10 | async-start | bytes 7077888 | tf_op jit(solution)/shard_map/all_to_all | solution.py:112
  863.4 1.8 copy-start.2
  865.3 110.2 %all-to-all-start.11 = ((f32[16,24,24,96]{3,2,1,0:T(8,128)}), f32[16,24,24,96]{3,2,1,0:T(8,128)}, u32[]{:S(2)}, u32[]{:S(2)}) async-start(f32[16,24,24,96]{3,2,1,0:T(8,128)} %copy.36), calls=%async_computation.11 | async-start | bytes 9437184 | tf_op jit(solution)/shard_map/all_to_all | solution.py:117
  975.5 33.5 %slice-start = ((s8[14155776]{0:T(1024)(128)(4,1)}), s8[1572864]{0:T(1024)(128)(4,1)S(1)}, s32[]{:S(2)}) async-start(s8[14155776]{0:T(1024)(128)(4,1)} %bitcast.164), calls=%async_computation.16 | async-start | bytes 3145728
  975.5 109.1 %all-to-all-start.8 = ((f32[16,24,24,96]{3,2,1,0:T(8,128)}), f32[16,24,24,96]{3,2,1,0:T(8,128)}, u32[]{:S(2)}, u32[]{:S(2)}) async-start(f32[16,24,24,96]{3,2,1,0:T(8,128)} %copy.32), calls=%async_computation.8 | async-start | bytes 9437184 | tf_op jit(solution)/shard_map/all_to_all | solution.py:101
  981.1 27.9 %slice-start.1 = ((s8[14155776]{0:T(1024)(128)(4,1)}), s8[4194304]{0:T(1024)(128)(4,1)S(1)}, s32[]{:S(2)}) async-start(s8[14155776]{0:T(1024)(128)(4,1)} %bitcast.164), calls=%async_computation.17 | async-start | bytes 8388608
  981.1 27.9 %slice-start.2 = ((s8[14155776]{0:T(1024)(128)(4,1)}), s8[4194304]{0:T(1024)(128)(4,1)S(1)}, s32[]{:S(2)}) async-start(s8[14155776]{0:T(1024)(128)(4,1)} %bitcast.164), calls=%async_computation.18 | async-start | bytes 8388608
  981.1 27.9 %slice-start.3 = ((s8[14155776]{0:T(1024)(128)(4,1)}), s8[4194304]{0:T(1024)(128)(4,1)S(1)}, s32[]{:S(2)}) async-start(s8[14155776]{0:T(1024)(128)(4,1)} %bitcast.164), calls=%async_computation.19 | async-start | bytes 8388608
  981.1 27.9 %copy-start.4 = (f32[16,24,1536,1]{2,1,3,0:T(8,128)S(1)}, f32[16,24,1536,1]{2,1,3,0:T(8,128)}, u32[]{:S(2)}) copy-start(f32[16,24,1536,1]{2,1,3,0:T(8,128)} %constant.80) | copy-start | bytes 7077892
  1173.1 43.3 %all-to-all-start.13 = ((f32[2,24,24,768]{3,2,1,0:T(8,128)}), f32[2,24,24,768]{3,2,1,0:T(8,128)S(1)}, u32[]{:S(2)}, u32[]{:S(2)}) async-start(f32[2,24,24,768]{3,2,1,0:T(8,128)} %bitcast.170), calls=%async_computation.13 | async-start | bytes 7077888 | tf_op jit(solution)/shard_map/all_to_all | solution.py:112
  1216.4 110.2 %all-to-all-start.14 = ((f32[16,24,24,96]{3,2,1,0:T(8,128)}), f32[16,24,24,96]{3,2,1,0:T(8,128)}, u32[]{:S(2)}, u32[]{:S(2)}) async-start(f32[16,24,24,96]{3,2,1,0:T(8,128)} %copy.41), calls=%async_computation.14 | async-start | bytes 9437184 | tf_op jit(solution)/shard_map/all_to_all | solution.py:117
  1326.6 28.8 %copy-start.1 = (f32[16,24,24,96]{3,2,0,1:T(8,128)S(1)}, f32[16,24,24,96]{3,2,0,1:T(8,128)}, u32[]{:S(2)}) copy-start(f32[16,24,24,96]{3,2,0,1:T(8,128)} %fusion.34) | copy-start | bytes 10616836
  1355.9 108.5 %copy-start.3 = (f32[16,24,1536,1]{2,1,3,0:T(8,128)S(1)}, f32[16,24,1536,1]{2,1,3,0:T(8,128)}, u32[]{:S(2)}) copy-start(f32[16,24,1536,1]{2,1,3,0:T(8,128)} %constant.82) | copy-start | bytes 7077892

commit v5 on v4

--- a/solution.py
+++ b/solution.py
@@ -75,6 +75,24 @@
     )(lower_coef, upper_coef, eigen_sum, pinned.astype(jnp.float32), spectra)
 
 
+def exchange(pieces, axis_name):
+    count = pieces.shape[0]
+    here = lax.axis_index(axis_name)
+    arrived = [lax.dynamic_index_in_dim(pieces, here, keepdims=False)]
+    for shift in range(1, count):
+        outgoing = lax.dynamic_index_in_dim(pieces, (here + shift) % count, keepdims=False)
+        perm = [(device, (device + shift) % count) for device in range(count)]
+        arrived.append(lax.ppermute(outgoing, axis_name, perm))
+    placed = []
+    for source in range(count):
+        distance = (here - source) % count
+        piece = arrived[0]
+        for shift in range(1, count):
+            piece = jnp.where(distance == shift, arrived[shift], piece)
+        placed.append(piece)
+    return jnp.stack(placed)
+
+
 def body(source, lower_coef, upper_coef, chunks=4):
     highest = lax.Precision.HIGHEST
     slab_levels, slab_rows, full_x = source.shape
@@ -102,14 +120,14 @@
 
     def middle(chunk, gathered):
         spectra = jnp.einsum("sziy,syhj->hzij", gathered, forward_y, precision=highest)
-        columns = lax.all_to_all(spectra, "row", 0, 0, tiled=True)
+        columns = exchange(spectra, "row")
         columns = columns.reshape(row_count * slab_levels, chunk_x, part_y)
         wave_x = lax.axis_index("col") * part_x + chunk * chunk_x + lax.iota(jnp.int32, chunk_x)
         eigen_sum = eigen_values(wave_x, full_x)[:, None] + eigen_values(wave_y, full_y)[None, :]
         pinned = (wave_x == 0)[:, None] & (wave_y == 0)[None, :]
         solved = vertical_solve(columns, lower_coef, upper_coef, eigen_sum, pinned)
         solved = solved.reshape(row_count, slab_levels, chunk_x, part_y)
-        returned = lax.all_to_all(solved, "row", 0, 0, tiled=True)
+        returned = exchange(solved, "row")
         return jnp.einsum("hzij,hjsy->sziy", returned, inverse_y, precision=highest)
 
     def back_x(chunk, back_y):

time: 1500 us -> 1200 us (0.80)
  blocking collectives: 351 us -> 111 us
  waiting for transfers between devices: 549 us -> 490 us
  starting transfers between devices: 63.3 us -> 46 us
    ppermute x0 -> x8, waiting for transfers between devices: none -> 274 us  [exchange(): arrived.append(lax.ppermute(outgoing, axis_name, perm))]
    all_to_all x4 -> x0, blocking collectives: 243 us -> none  [the longest x3 133 us: middle(): columns = lax.all_to_all(spectra, 'row', 0, 0, tiled=True)]
    all_to_all x5 -> x0, waiting for transfers between devices: 146 us -> none  [the longest x4 109 us: middle(): returned = lax.all_to_all(solved, 'row', 0, 0, tiled=True)]
    all_to_all x3, waiting for transfers between devices: 227 us -> 113 us  [back_x(): scattered = lax.all_to_all(back_y, 'col', 0, 0, tiled=True)]
    all_to_all x3 -> x4, waiting for transfers between devices: 176 us -> 104 us  [along_x(): return lax.all_to_all(spread, 'col', 0, 0, tiled=True)]
    all_to_all x5 -> x0, starting transfers between devices: 25 us -> none  [the longest x4 20.8 us: middle(): returned = lax.all_to_all(solved, 'row', 0, 0, tiled=True)]
  transfers between devices with their start and end apart: 11 -> 15, of which waited for: 11 -> 10; matrix products, arithmetic and copies ran while one was open for 18% -> 33% of each run, Pallas kernels for 0% -> 2%
where the time goes in v5:
time: 1200 us; the launch traced here: 1190 us
  waiting for transfers between devices  490 us (41%)
  matrix products  468 us (39%)
  blocking collectives  111 us (9%)
  starting transfers between devices  46 us (4%)
  local copies, waits for them, and re-layouts  34.1 us (3%)
  Pallas kernels  26 us (2%)
  other arithmetic  15.2 us (1%)
    ppermute x8, waiting for transfers between devices, exchange(): arrived.append(lax.ppermute(outgoing, axis_name, perm))  274 us
    dot_general x4, matrix products, middle(): jnp.einsum('sziy,syhj->hzij', gathered, forward_y, precision=highest)  148 us
    all_to_all x3, waiting for transfers between devices, back_x(): scattered = lax.all_to_all(back_y, 'col', 0, 0, tiled=True)  113 us
    all_to_all x1, blocking collectives, back_x(): scattered = lax.all_to_all(back_y, 'col', 0, 0, tiled=True)  111 us
    dot_general x4, matrix products, middle(): return jnp.einsum('hzij,hjsy->sziy', returned, inverse_y, precision=highest)  109 us
    dot_general x4, matrix products, back_x(): return jnp.einsum('dziy,din->zyn', scattered, table_back, precision=highest)  108 us
    all_to_all x4, waiting for transfers between devices, along_x(): return lax.all_to_all(spread, 'col', 0, 0, tiled=True)  104 us
    dot_general x4, matrix products, along_x(): spread = jnp.einsum('zyx,xdi->dziy', slab, table_chunk, precision=highest)  103 us
  transfers between devices with their start and end apart: 15, of which 10 were waited for; matrix products, arithmetic and copies ran while one was open for 33% of the time, Pallas kernels for 2%

profile of v5, /device:TPU:15, one launch (start us, length us, event | category | flops | bytes accessed | tf_op | source)
XLA Modules:
  0.0 1191.8 jit_solution(15345125707778754701)
XLA Ops:
  0.0 27.8 %fusion.36 = f32[16,24,24,96]{3,2,1,0:T(8,128)} fusion(f32[1536,16,24,1]{0,2,3,1:T(8,128)} %constant.172, f32[24,96,1536]{2,1,0:T(8,128)} %param.12), kind=kOutput, calls=%fused_computation.42 | convolution fusion | flops 16307453952 | bytes 20054016 | tf_op jit(solution)/shard_map/zyx,xdi->dziy/dot_general | solution.py:118
  27.8 7.0 all-to-all-start
  34.9 103.5 %all-to-all-done = f32[16,24,24,96]{3,2,1,0:T(8,128)} async-done(((f32[16,24,24,96]{3,2,1,0:T(8,128)}), f32[16,24,24,96]{3,2,1,0:T(8,128)}, u32[]{:S(2)}, u32[]{:S(2)}) %all-to-all-start) | async-done | bytes 3538976 | tf_op jit(solution)/shard_map/all_to_all | solution.py:119
  138.4 25.1 %fusion.39 = f32[16,24,24,96]{3,2,0,1:T(8,128)S(1)} fusion(f32[1536,16,24,1]{0,2,1,3:T(8,128)S(1)} %copy-done.11, f32[24,96,1536]{2,1,0:T(8,128)} %param.12), kind=kOutput, calls=%fused_computation.43 | convolution fusion | flops 16307453952 | bytes 20054016 | tf_op jit(solution)/shard_map/zyx,xdi->dziy/dot_general | solution.py:118
  171.5 36.4 %fusion.48 = f32[24,24,2,768]{3,1,2,0:T(8,128)S(1)} fusion(f32[16,96,2,768,1]{3,1,0,2,4:T(8,128)} %constant.174, f32[16,24,24,96]{3,2,1,0:T(8,128)} %all-to-all-done), kind=kOutput, calls=%fused_computation.46 | convolution fusion | flops 16307453952 | bytes 16515072 | tf_op jit(solution)/shard_map/sziy,syhj->hzij/dot_general | solution.py:122
  211.3 38.1 %collective-permute-done = f32[24,24,768]{2,1,0:T(8,128)} collective-permute-done((f32[24,24,768]{2,1,0:T(8,128)}, f32[24,24,768]{2,1,0:T(8,128)}, u32[]{:S(2)}, u32[]{:S(2)}) %collective-permute-start) | collective-permute-done | bytes 1769504 | tf_op jit(solution)/shard_map/ppermute | solution.py:85
  261.7 38.7 %collective-permute-done.1 = f32[24,24,768]{2,1,0:T(8,128)S(1)} collective-permute-done((f32[24,24,768]{2,1,0:T(8,128)S(1)}, f32[24,24,768]{2,1,0:T(8,128)S(1)}, u32[]{:S(2)}, u32[]{:S(2)}) %collective-permute-start.1) | collective-permute-done | bytes 1769504 | tf_op jit(solution)/shard_map/ppermute | solution.py:85
  300.7 27.2 %fusion.35 = f32[16,24,24,96]{3,2,0,1:T(8,128)} fusion(f32[2,768,16,96,1]{1,3,0,2,4:T(8,128)} %constant.175, f32[1,24,24,768]{3,2,0,1:T(8,128)S(1)} %get-tuple-element.46, f32[1,24,24,768]{3,2,0,1:T(8,128)S(1)} %get-tuple-element.45), kind=kOutput, calls=%fused_computation.41 | convolution fusion | flops 16308338688 | bytes 16515072 | tf_op jit(solution)/shard_map/hzij,hjsy->sziy/dot_general | solution.py:131
  332.9 7.9 all-to-all-start.3
  340.8 25.1 %fusion.42 = f32[16,24,24,96]{3,2,0,1:T(8,128)S(1)} fusion(f32[1536,16,24,1]{0,2,1,3:T(8,128)S(1)} %copy-done.10, f32[24,96,1536]{2,1,0:T(8,128)} %param.12), kind=kOutput, calls=%fused_computation.44 | convolution fusion | flops 16307453952 | bytes 20054016 | tf_op jit(solution)/shard_map/zyx,xdi->dziy/dot_general | solution.py:118
  368.5 76.0 %all-to-all-done.3 = f32[16,24,24,96]{3,2,1,0:T(8,128)} async-done(((f32[16,24,24,96]{3,2,1,0:T(8,128)}), f32[16,24,24,96]{3,2,1,0:T(8,128)}, u32[]{:S(2)}, u32[]{:S(2)}) %all-to-all-start.3) | async-done | bytes 3538976 | tf_op jit(solution)/shard_map/all_to_all | solution.py:135
  449.4 37.5 %fusion.51 = f32[24,24,2,768]{3,1,2,0:T(8,128)S(1)} fusion(f32[16,96,2,768,1]{3,1,0,2,4:T(8,128)} %constant.174, f32[16,24,24,96]{3,2,1,0:T(8,128)} %all-to-all-done.1), kind=kOutput, calls=%fused_computation.47 | convolution fusion | flops 16307453952 | bytes 16515072 | tf_op jit(solution)/shard_map/sziy,syhj->hzij/dot_general | solution.py:122
  487.3 39.7 %collective-permute-done.2 = f32[24,24,768]{2,1,0:T(8,128)S(1)} collective-permute-done((f32[24,24,768]{2,1,0:T(8,128)S(1)}, f32[24,24,768]{2,1,0:T(8,128)S(1)}, u32[]{:S(2)}, u32[]{:S(2)}) %collective-permute-start.2) | collective-permute-done | bytes 1769504 | tf_op jit(solution)/shard_map/ppermute | solution.py:85
  537.9 38.9 %collective-permute-done.3 = f32[24,24,768]{2,1,0:T(8,128)S(1)} collective-permute-done((f32[24,24,768]{2,1,0:T(8,128)S(1)}, f32[24,24,768]{2,1,0:T(8,128)S(1)}, u32[]{:S(2)}, u32[]{:S(2)}) %collective-permute-start.3) | collective-permute-done | bytes 1769504 | tf_op jit(solution)/shard_map/ppermute | solution.py:85
  577.0 27.2 %fusion.26 = f32[16,24,24,96]{3,2,0,1:T(8,128)} fusion(f32[2,768,16,96,1]{1,3,0,2,4:T(8,128)} %constant.175, f32[1,24,24,768]{3,2,1,0:T(8,128)S(1)} %get-tuple-element.42, f32[1,24,24,768]{3,2,1,0:T(8,128)S(1)} %get-tuple-element.41), kind=kOutput, calls=%fused_computation.38 | convolution fusion | flops 16308338688 | bytes 16515072 | tf_op jit(solution)/shard_map/hzij,hjsy->sziy/dot_general | solution.py:131
  604.3 26.8 %convolution_bitcast_fusion = f32[24,96,1536]{2,1,0:T(8,128)} fusion(f32[16,24,24,96]{3,2,1,0:T(8,128)} %all-to-all-done.3, f32[16,24,1536,1]{2,1,3,0:T(8,128)S(1)} %copy-done.8), kind=kOutput, calls=%fused_computation.12 | convolution fusion | flops 16307453952 | bytes 20054016 | tf_op jit(solution)/shard_map/dziy,din->zyn/dot_general | solution.py:136
  636.0 7.7 all-to-all-start.5
  643.6 36.4 %fusion.54 = f32[24,24,2,768]{3,1,2,0:T(8,128)S(1)} fusion(f32[16,96,2,768,1]{3,1,0,2,4:T(8,128)} %constant.174, f32[16,24,24,96]{3,2,1,0:T(8,128)} %all-to-all-done.2), kind=kOutput, calls=%fused_computation.48 | convolution fusion | flops 16307453952 | bytes 16515072 | tf_op jit(solution)/shard_map/sziy,syhj->hzij/dot_general | solution.py:122
  682.4 25.5 %fusion.45 = f32[16,24,24,96]{3,2,0,1:T(8,128)S(1)} fusion(f32[1536,16,24,1]{0,2,1,3:T(8,128)S(1)} %copy-done.9, f32[24,96,1536]{2,1,0:T(8,128)} %param.12), kind=kOutput, calls=%fused_computation.45 | convolution fusion | flops 16307453952 | bytes 20054016 | tf_op jit(solution)/shard_map/zyx,xdi->dziy/dot_general | solution.py:118
  710.6 36.7 %all-to-all-done.5 = f32[16,24,24,96]{3,2,1,0:T(8,128)} async-done(((f32[16,24,24,96]{3,2,1,0:T(8,128)}), f32[16,24,24,96]{3,2,1,0:T(8,128)}, u32[]{:S(2)}, u32[]{:S(2)}) %all-to-all-start.5) | async-done | bytes 3538976 | tf_op jit(solution)/shard_map/all_to_all | solution.py:135
  756.1 6.5 shard_map.120
  764.5 39.8 %collective-permute-done.5 = f32[24,24,768]{2,1,0:T(8,128)S(1)} collective-permute-done((f32[24,24,768]{2,1,0:T(8,128)S(1)}, f32[24,24,768]{2,1,0:T(8,128)S(1)}, u32[]{:S(2)}, u32[]{:S(2)}) %collective-permute-start.5) | collective-permute-done | bytes 1769504 | tf_op jit(solution)/shard_map/ppermute | solution.py:85
  804.7 27.5 %fusion.29 = f32[16,24,24,96]{3,2,0,1:T(8,128)} fusion(f32[2,768,16,96,1]{1,3,0,2,4:T(8,128)} %constant.175, f32[1,24,24,768]{3,2,1,0:T(8,128)S(1)} %get-tuple-element.38, f32[1,24,24,768]{3,2,1,0:T(8,128)S(1)} %get-tuple-element.37), kind=kOutput, calls=%fused_computation.39 | convolution fusion | flops 16308338688 | bytes 16515072 | tf_op jit(solution)/shard_map/hzij,hjsy->sziy/dot_general | solution.py:131
  832.2 27.2 %bitcast_add_fusion.2 = f32[24,96,1536]{2,1,0:T(8,128)} fusion(f32[24,96,1536]{2,1,0:T(8,128)S(1)} %bitcast.266, f32[16,24,24,96]{3,2,1,0:T(8,128)} %all-to-all-done.5, f32[16,24,1536,1]{2,1,3,0:T(8,128)S(1)} %copy-done.7), kind=kOutput, calls=%fused_computation.9 | convolution fusion | flops 16310992896 | bytes 34209792 | tf_op jit(solution)/shard_map/dziy,din->zyn/dot_general | solution.py:136
  864.4 6.7 all-to-all-start.6
  871.1 37.5 %fusion.57 = f32[24,24,2,768]{3,1,2,0:T(8,128)S(1)} fusion(f32[16,96,2,768,1]{3,1,0,2,4:T(8,128)} %constant.174, f32[16,24,24,96]{3,2,1,0:T(8,128)} %all-to-all-done.4), kind=kOutput, calls=%fused_computation.49 | convolution fusion | flops 16307453952 | bytes 16515072 | tf_op jit(solution)/shard_map/sziy,syhj->hzij/dot_general | solution.py:122
  908.9 39.8 %collective-permute-done.6 = f32[24,24,768]{2,1,0:T(8,128)S(1)} collective-permute-done((f32[24,24,768]{2,1,0:T(8,128)S(1)}, f32[24,24,768]{2,1,0:T(8,128)S(1)}, u32[]{:S(2)}, u32[]{:S(2)}) %collective-permute-start.6) | collective-permute-done | bytes 1769504 | tf_op jit(solution)/shard_map/ppermute | solution.py:85
  959.5 39.0 %collective-permute-done.7 = f32[24,24,768]{2,1,0:T(8,128)S(1)} collective-permute-done((f32[24,24,768]{2,1,0:T(8,128)S(1)}, f32[24,24,768]{2,1,0:T(8,128)S(1)}, u32[]{:S(2)}, u32[]{:S(2)}) %collective-permute-start.7) | collective-permute-done | bytes 1769504 | tf_op jit(solution)/shard_map/ppermute | solution.py:85
  998.8 26.9 %fusion.32 = f32[16,24,24,96]{3,2,0,1:T(8,128)} fusion(f32[2,768,16,96,1]{1,3,0,2,4:T(8,128)} %constant.175, f32[1,24,24,768]{3,2,1,0:T(8,128)S(1)} %get-tuple-element.34, f32[1,24,24,768]{3,2,1,0:T(8,128)S(1)} %get-tuple-element.33), kind=kOutput, calls=%fused_computation.40 | convolution fusion | flops 16308338688 | bytes 16515072 | tf_op jit(solution)/shard_map/hzij,hjsy->sziy/dot_general | solution.py:131
  1025.7 28.1 %bitcast_add_fusion.1 = f32[24,96,1536]{2,1,0:T(8,128)S(1)} fusion(f32[24,96,1536]{2,1,0:T(8,128)} %bitcast_add_fusion.2, f32[16,24,24,96]{3,2,1,0:T(8,128)} %all-to-all-done.6, f32[16,24,1536,1]{2,1,3,0:T(8,128)S(1)} %copy-done.6), kind=kOutput, calls=%fused_computation.8 | convolution fusion | flops 16310992896 | bytes 34209792 | tf_op jit(solution)/shard_map/dziy,din->zyn/dot_general | solution.py:136
  1054.3 111.3 %all_to_all.40 = f32[16,24,24,96]{3,2,1,0:T(8,128)S(1)} all-to-all(f32[16,24,24,96]{3,2,1,0:T(8,128)S(1)} %copy.35), channel_id=1, replica_groups=mesh['row'=2,'col'=16] {'col'}, dimensions={0} | all-to-all | bytes 7077888 | tf_op jit(solution)/shard_map/all_to_all | solution.py:135
  1165.6 26.0 %fusion.6 = f32[24,96,1536]{2,1,0:T(8,128)} fusion(f32[24,96,1536]{2,1,0:T(8,128)S(1)} %bitcast_add_fusion.1, f32[16,24,24,96]{3,2,1,0:T(8,128)S(1)} %all_to_all.40, f32[16,24,1536,1]{2,1,3,0:T(8,128)S(1)} %copy-done.5), kind=kOutput, calls=%fused_computation.7 | convolution fusion | flops 16314531840 | bytes 34209792 | tf_op jit(solution)/shard_map/dziy,din->zyn/dot_general | solution.py:136
  (87 shorter events, 85.5 us)
Async XLA Ops:
  27.8 110.6 %copy-start.11 = (f32[1536,16,24,1]{0,2,1,3:T(8,128)S(1)}, f32[1536,16,24,1]{0,2,1,3:T(8,128)}, u32[]{:S(2)}) copy-start(f32[1536,16,24,1]{0,2,1,3:T(8,128)} %constant.173) | copy-start | bytes 7077892
  27.8 110.6 %all-to-all-start = ((f32[16,24,24,96]{3,2,1,0:T(8,128)}), f32[16,24,24,96]{3,2,1,0:T(8,128)}, u32[]{:S(2)}, u32[]{:S(2)}) async-start(f32[16,24,24,96]{3,2,1,0:T(8,128)} %fusion.36), calls=%async_computation | async-start | bytes 9437184 | tf_op jit(solution)/shard_map/all_to_all | solution.py:119
  166.2 161.7 %all-to-all-start.1 = ((f32[16,24,24,96]{3,2,1,0:T(8,128)}), f32[16,24,24,96]{3,2,1,0:T(8,128)}, u32[]{:S(2)}, u32[]{:S(2)}) async-start(f32[16,24,24,96]{3,2,1,0:T(8,128)} %copy.18), calls=%async_computation.1 | async-start | bytes 9437184 | tf_op jit(solution)/shard_map/all_to_all | solution.py:119
  209.2 40.1 %collective-permute-start = (f32[24,24,768]{2,1,0:T(8,128)}, f32[24,24,768]{2,1,0:T(8,128)}, u32[]{:S(2)}, u32[]{:S(2)}) collective-permute-start(f32[24,24,768]{2,1,0:T(8,128)} %dynamic-slice_bitcast_fusion.7), channel_id=1, source_target_pairs={{0,16},{16,0},{1,17},{17,1},{2,18},{18,2},{3,19},{19,3},{4,20},{20... | collective-permute-start | bytes 5308424 | tf_op jit(solution)/shard_map/ppermute | solution.py:85
  259.7 40.7 %copy-start.1 = (f32[48,24,768]{2,1,0:T(8,128)S(1)}, f32[48,24,768]{2,1,0:T(8,128)}, u32[]{:S(2)}) copy-start(f32[48,24,768]{2,1,0:T(8,128)} %shard_map.118) | copy-start | bytes 10616836
  261.4 39.0 %collective-permute-start.1 = (f32[24,24,768]{2,1,0:T(8,128)S(1)}, f32[24,24,768]{2,1,0:T(8,128)S(1)}, u32[]{:S(2)}, u32[]{:S(2)}) collective-permute-start(f32[24,24,768]{2,1,0:T(8,128)S(1)} %dynamic-slice_bitcast_fusion.6), channel_id=1, source_target_pairs={{0,16},{16,0},{1,17},{17,1},{2,18},{18,2},{3,19},{19,3},{4,20},{20... | collective-permute-start | bytes 5308424 | tf_op jit(solution)/shard_map/ppermute | solution.py:85
  332.9 7.9 copy-start.10
  332.9 111.6 %all-to-all-start.3 = ((f32[16,24,24,96]{3,2,1,0:T(8,128)}), f32[16,24,24,96]{3,2,1,0:T(8,128)}, u32[]{:S(2)}, u32[]{:S(2)}) async-start(f32[16,24,24,96]{3,2,1,0:T(8,128)} %copy.24), calls=%async_computation.3 | async-start | bytes 9437184 | tf_op jit(solution)/shard_map/all_to_all | solution.py:135
  444.5 186.5 %all-to-all-start.2 = ((f32[16,24,24,96]{3,2,1,0:T(8,128)}), f32[16,24,24,96]{3,2,1,0:T(8,128)}, u32[]{:S(2)}, u32[]{:S(2)}) async-start(f32[16,24,24,96]{3,2,1,0:T(8,128)} %copy.21), calls=%async_computation.2 | async-start | bytes 9437184 | tf_op jit(solution)/shard_map/all_to_all | solution.py:119
  487.1 40.0 %collective-permute-start.2 = (f32[24,24,768]{2,1,0:T(8,128)S(1)}, f32[24,24,768]{2,1,0:T(8,128)S(1)}, u32[]{:S(2)}, u32[]{:S(2)}) collective-permute-start(f32[24,24,768]{2,1,0:T(8,128)S(1)} %dynamic-slice_bitcast_fusion.5), channel_id=1, source_target_pairs={{0,16},{16,0},{1,17},{17,1},{2,18},{18,2},{3,19},{19,3},{4,20},{20... | collective-permute-start | bytes 5308424 | tf_op jit(solution)/shard_map/ppermute | solution.py:85
  535.9 40.8 %copy-start.2 = (f32[48,24,768]{2,1,0:T(8,128)S(1)}, f32[48,24,768]{2,1,0:T(8,128)}, u32[]{:S(2)}) copy-start(f32[48,24,768]{2,1,0:T(8,128)} %shard_map.119) | copy-start | bytes 10616836
  537.7 39.1 %collective-permute-start.3 = (f32[24,24,768]{2,1,0:T(8,128)S(1)}, f32[24,24,768]{2,1,0:T(8,128)S(1)}, u32[]{:S(2)}, u32[]{:S(2)}) collective-permute-start(f32[24,24,768]{2,1,0:T(8,128)S(1)} %dynamic-slice_bitcast_fusion.4), channel_id=1, source_target_pairs={{0,16},{16,0},{1,17},{17,1},{2,18},{18,2},{3,19},{19,3},{4,20},{20... | collective-permute-start | bytes 5308424 | tf_op jit(solution)/shard_map/ppermute | solution.py:85
  577.0 27.3 %copy-start.8 = (f32[16,24,1536,1]{2,1,3,0:T(8,128)S(1)}, f32[16,24,1536,1]{2,1,3,0:T(8,128)}, u32[]{:S(2)}) copy-start(f32[16,24,1536,1]{2,1,3,0:T(8,128)} %constant.177) | copy-start | bytes 7077892
  636.0 111.4 %all-to-all-start.5 = ((f32[16,24,24,96]{3,2,1,0:T(8,128)}), f32[16,24,24,96]{3,2,1,0:T(8,128)}, u32[]{:S(2)}, u32[]{:S(2)}) async-start(f32[16,24,24,96]{3,2,1,0:T(8,128)} %copy.29), calls=%async_computation.5 | async-start | bytes 9437184 | tf_op jit(solution)/shard_map/all_to_all | solution.py:135
  680.1 2.3 copy-start.9
  681.4 70.8 %collective-permute-start.4 = (f32[24,24,768]{2,1,0:T(8,128)}, f32[24,24,768]{2,1,0:T(8,128)}, u32[]{:S(2)}, u32[]{:S(2)}) collective-permute-start(f32[24,24,768]{2,1,0:T(8,128)} %dynamic-slice_bitcast_fusion.3), channel_id=1, source_target_pairs={{0,16},{16,0},{1,17},{17,1},{2,18},{18,2},{3,19},{19,3},{4,20},{20... | collective-permute-start | bytes 5308424 | tf_op jit(solution)/shard_map/ppermute | solution.py:85
  747.3 112.1 %all-to-all-start.4 = ((f32[16,24,24,96]{3,2,1,0:T(8,128)}), f32[16,24,24,96]{3,2,1,0:T(8,128)}, u32[]{:S(2)}, u32[]{:S(2)}) async-start(f32[16,24,24,96]{3,2,1,0:T(8,128)} %copy.26), calls=%async_computation.4 | async-start | bytes 9437184 | tf_op jit(solution)/shard_map/all_to_all | solution.py:119
  762.6 41.8 %copy-start.3 = (f32[48,24,768]{2,1,0:T(8,128)S(1)}, f32[48,24,768]{2,1,0:T(8,128)}, u32[]{:S(2)}) copy-start(f32[48,24,768]{2,1,0:T(8,128)} %shard_map.120) | copy-start | bytes 10616836
  764.4 40.0 %collective-permute-start.5 = (f32[24,24,768]{2,1,0:T(8,128)S(1)}, f32[24,24,768]{2,1,0:T(8,128)S(1)}, u32[]{:S(2)}, u32[]{:S(2)}) collective-permute-start(f32[24,24,768]{2,1,0:T(8,128)S(1)} %dynamic-slice_bitcast_fusion.2), channel_id=1, source_target_pairs={{0,16},{16,0},{1,17},{17,1},{2,18},{18,2},{3,19},{19,3},{4,20},{20... | collective-permute-start | bytes 5308424 | tf_op jit(solution)/shard_map/ppermute | solution.py:85
  804.4 27.8 %slice-start = ((s8[14155776]{0:T(1024)(128)(4,1)}), s8[4194304]{0:T(1024)(128)(4,1)S(1)}, s32[]{:S(2)}) async-start(s8[14155776]{0:T(1024)(128)(4,1)} %bitcast.265), calls=%async_computation.8 | async-start | bytes 8388608
  804.6 27.5 %slice-start.1 = ((s8[14155776]{0:T(1024)(128)(4,1)}), s8[4194304]{0:T(1024)(128)(4,1)S(1)}, s32[]{:S(2)}) async-start(s8[14155776]{0:T(1024)(128)(4,1)} %bitcast.265), calls=%async_computation.9 | async-start | bytes 8388608
  804.6 27.5 %slice-start.2 = ((s8[14155776]{0:T(1024)(128)(4,1)}), s8[4194304]{0:T(1024)(128)(4,1)S(1)}, s32[]{:S(2)}) async-start(s8[14155776]{0:T(1024)(128)(4,1)} %bitcast.265), calls=%async_computation.10 | async-start | bytes 8388608
  804.7 27.5 %slice-start.3 = ((s8[14155776]{0:T(1024)(128)(4,1)}), s8[1572864]{0:T(1024)(128)(4,1)S(1)}, s32[]{:S(2)}) async-start(s8[14155776]{0:T(1024)(128)(4,1)} %bitcast.265), calls=%async_computation.11 | async-start | bytes 3145728
  804.7 27.5 %copy-start.7 = (f32[16,24,1536,1]{2,1,3,0:T(8,128)S(1)}, f32[16,24,1536,1]{2,1,3,0:T(8,128)}, u32[]{:S(2)}) copy-start(f32[16,24,1536,1]{2,1,3,0:T(8,128)} %constant.179) | copy-start | bytes 7077892
  864.4 161.3 %all-to-all-start.6 = ((f32[16,24,24,96]{3,2,1,0:T(8,128)}), f32[16,24,24,96]{3,2,1,0:T(8,128)}, u32[]{:S(2)}, u32[]{:S(2)}) async-start(f32[16,24,24,96]{3,2,1,0:T(8,128)} %copy.33), calls=%async_computation.6 | async-start | bytes 9437184 | tf_op jit(solution)/shard_map/all_to_all | solution.py:135
  908.8 40.0 %collective-permute-start.6 = (f32[24,24,768]{2,1,0:T(8,128)S(1)}, f32[24,24,768]{2,1,0:T(8,128)S(1)}, u32[]{:S(2)}, u32[]{:S(2)}) collective-permute-start(f32[24,24,768]{2,1,0:T(8,128)S(1)} %dynamic-slice_bitcast_fusion.1), channel_id=1, source_target_pairs={{0,16},{16,0},{1,17},{17,1},{2,18},{18,2},{3,19},{19,3},{4,20},{20... | collective-permute-start | bytes 5308424 | tf_op jit(solution)/shard_map/ppermute | solution.py:85
  957.7 40.8 %copy-start = (f32[48,24,768]{2,1,0:T(8,128)S(1)}, f32[48,24,768]{2,1,0:T(8,128)}, u32[]{:S(2)}) copy-start(f32[48,24,768]{2,1,0:T(8,128)} %shard_map.121) | copy-start | bytes 10616836
  959.4 39.1 %collective-permute-start.7 = (f32[24,24,768]{2,1,0:T(8,128)S(1)}, f32[24,24,768]{2,1,0:T(8,128)S(1)}, u32[]{:S(2)}, u32[]{:S(2)}) collective-permute-start(f32[24,24,768]{2,1,0:T(8,128)S(1)} %dynamic-slice_bitcast_fusion), channel_id=1, source_target_pairs={{0,16},{16,0},{1,17},{17,1},{2,18},{18,2},{3,19},{19,3},{4,20},{20... | collective-permute-start | bytes 5308424 | tf_op jit(solution)/shard_map/ppermute | solution.py:85
  998.8 26.9 %copy-start.6 = (f32[16,24,1536,1]{2,1,3,0:T(8,128)S(1)}, f32[16,24,1536,1]{2,1,3,0:T(8,128)}, u32[]{:S(2)}) copy-start(f32[16,24,1536,1]{2,1,3,0:T(8,128)} %constant.180) | copy-start | bytes 7077892
  1025.7 28.1 %copy-start.4 = (f32[16,24,24,96]{3,2,0,1:T(8,128)S(1)}, f32[16,24,24,96]{3,2,0,1:T(8,128)}, u32[]{:S(2)}) copy-start(f32[16,24,24,96]{3,2,0,1:T(8,128)} %fusion.32) | copy-start | bytes 10616836
  1054.3 111.3 %copy-start.5 = (f32[16,24,1536,1]{2,1,3,0:T(8,128)S(1)}, f32[16,24,1536,1]{2,1,3,0:T(8,128)}, u32[]{:S(2)}) copy-start(f32[16,24,1536,1]{2,1,3,0:T(8,128)} %constant.181) | copy-start | bytes 7077892

commit v6 on v5

--- a/solution.py
+++ b/solution.py
@@ -136,7 +136,7 @@
         return jnp.einsum("dziy,din->zyn", scattered, table_back, precision=highest)
 
     gathered = along_x(0, source)
-    gathered, source = lax.optimization_barrier((gathered, source))
+    pass
     pressure = None
     back_y = None
     for chunk in range(chunks):
@@ -146,7 +146,7 @@
             pressure = part if pressure is None else pressure + part
         back_y = middle(chunk, gathered)
         gathered = gathered_next
-        gathered, back_y, pressure, source = lax.optimization_barrier((gathered, back_y, pressure, source))
+        pass
     part = back_x(chunks - 1, back_y)
     pressure = part if pressure is None else pressure + part
     return pressure * scale

time: 1200 us -> 1180 us (0.983)
  blocking collectives: 111 us -> 0 us
  waiting for transfers between devices: 490 us -> 565 us
  matrix products: 468 us -> 499 us
  local copies, waits for them, and re-layouts: 34.1 us -> 8.72 us
    all_to_all x4, waiting for transfers between devices: 104 us -> 229 us  [along_x(): return lax.all_to_all(spread, 'col', 0, 0, tiled=True)]
    all_to_all x1 -> x0, blocking collectives: 111 us -> none  [back_x(): scattered = lax.all_to_all(back_y, 'col', 0, 0, tiled=True)]
    all_to_all x3 -> x4, waiting for transfers between devices: 113 us -> 22.8 us  [back_x(): scattered = lax.all_to_all(back_y, 'col', 0, 0, tiled=True)]
    ppermute x8, waiting for transfers between devices: 274 us -> 313 us  [exchange(): arrived.append(lax.ppermute(outgoing, axis_name, perm))]
    dot_general x4, matrix products: 108 us -> 134 us  [back_x(): return jnp.einsum('dziy,din->zyn', scattered, table_back, precision=highest)]
    optimization_barrier x4 -> x0, local copies, waits for them, and re-layouts: 15.4 us -> none  [body(): lax.optimization_barrier((gathered, back_y, pressure, source))]
    all_to_all x3 -> x4, starting transfers between devices: 22.3 us -> 32.2 us  [back_x(): scattered = lax.all_to_all(back_y, 'col', 0, 0, tiled=True)]
  transfers between devices with their start and end apart: 15 -> 16, of which waited for: 10 -> 12; matrix products, arithmetic and copies ran while one was open for 33% -> 38% of each run, Pallas kernels for 2% -> 2%
where the time goes in v6:
time: 1180 us; the launch traced here: 1170 us
  waiting for transfers between devices  565 us (48%)
  matrix products  499 us (42%)
  starting transfers between devices  57 us (5%)
  Pallas kernels  25.9 us (2%)
  other arithmetic  13.7 us (1%)
    ppermute x8, waiting for transfers between devices, exchange(): arrived.append(lax.ppermute(outgoing, axis_name, perm))  313 us
    all_to_all x4, waiting for transfers between devices, along_x(): return lax.all_to_all(spread, 'col', 0, 0, tiled=True)  229 us
    dot_general x4, matrix products, middle(): jnp.einsum('sziy,syhj->hzij', gathered, forward_y, precision=highest)  149 us
    dot_general x4, matrix products, back_x(): return jnp.einsum('dziy,din->zyn', scattered, table_back, precision=highest)  134 us
    dot_general x4, matrix products, along_x(): spread = jnp.einsum('zyx,xdi->dziy', slab, table_chunk, precision=highest)  109 us
    dot_general x4, matrix products, middle(): return jnp.einsum('hzij,hjsy->sziy', returned, inverse_y, precision=highest)  107 us
    all_to_all x4, starting transfers between devices, back_x(): scattered = lax.all_to_all(back_y, 'col', 0, 0, tiled=True)  32.2 us
    pallas_call x4, Pallas kernels, vertical_solve(): pl.pallas_call(solve_kernel, grid=(part_x // block,), in_specs=[scalar_sp...  25.9 us
  transfers between devices with their start and end apart: 16, of which 12 were waited for; matrix products, arithmetic and copies ran while one was open for 38% of the time, Pallas kernels for 2%

profile of v6, /device:TPU:15, one launch (start us, length us, event | category | flops | bytes accessed | tf_op | source)
XLA Modules:
  0.0 1169.8 jit_solution(10819581667548331757)
XLA Ops:
  0.0 27.8 %fusion.39 = f32[16,24,24,96]{3,2,1,0:T(8,128)} fusion(f32[1536,16,24,1]{0,2,3,1:T(8,128)} %constant.172, f32[24,96,1536]{2,1,0:T(8,128)} %param.12), kind=kOutput, calls=%fused_computation.44 | convolution fusion | flops 16307453952 | bytes 20054016 | tf_op jit(solution)/shard_map/zyx,xdi->dziy/dot_general | solution.py:118
  35.0 27.1 %fusion.42 = f32[16,24,24,96]{3,2,1,0:T(8,128)} fusion(f32[1536,16,24,1]{0,2,3,1:T(8,128)S(1)} %copy-done.10, f32[24,96,1536]{2,1,0:T(8,128)} %param.12), kind=kOutput, calls=%fused_computation.45 | convolution fusion | flops 16307453952 | bytes 20054016 | tf_op jit(solution)/shard_map/zyx,xdi->dziy/dot_general | solution.py:118
  62.1 76.4 %all-to-all-done = f32[16,24,24,96]{3,2,1,0:T(8,128)} async-done(((f32[16,24,24,96]{3,2,1,0:T(8,128)}), f32[16,24,24,96]{3,2,1,0:T(8,128)}, u32[]{:S(2)}, u32[]{:S(2)}) %all-to-all-start) | async-done | bytes 3538976 | tf_op jit(solution)/shard_map/all_to_all | solution.py:119
  144.1 27.1 %fusion.45 = f32[16,24,24,96]{3,2,1,0:T(8,128)} fusion(f32[1536,16,24,1]{0,2,3,1:T(8,128)S(1)} %copy-done.9, f32[24,96,1536]{2,1,0:T(8,128)} %param.12), kind=kOutput, calls=%fused_computation.46 | convolution fusion | flops 16307453952 | bytes 20054016 | tf_op jit(solution)/shard_map/zyx,xdi->dziy/dot_general | solution.py:118
  171.2 76.5 %all-to-all-done.2 = f32[16,24,24,96]{3,2,1,0:T(8,128)} async-done(((f32[16,24,24,96]{3,2,1,0:T(8,128)}), f32[16,24,24,96]{3,2,1,0:T(8,128)}, u32[]{:S(2)}, u32[]{:S(2)}) %all-to-all-start.2) | async-done | bytes 3538976 | tf_op jit(solution)/shard_map/all_to_all | solution.py:119
  252.9 27.1 %fusion.48 = f32[16,24,24,96]{3,2,1,0:T(8,128)} fusion(f32[1536,16,24,1]{0,2,3,1:T(8,128)S(1)} %copy-done.8, f32[24,96,1536]{2,1,0:T(8,128)} %param.12), kind=kOutput, calls=%fused_computation.47 | convolution fusion | flops 16307453952 | bytes 20054016 | tf_op jit(solution)/shard_map/zyx,xdi->dziy/dot_general | solution.py:118
  280.0 76.4 %all-to-all-done.4 = f32[16,24,24,96]{3,2,1,0:T(8,128)} async-done(((f32[16,24,24,96]{3,2,1,0:T(8,128)}), f32[16,24,24,96]{3,2,1,0:T(8,128)}, u32[]{:S(2)}, u32[]{:S(2)}) %all-to-all-start.4) | async-done | bytes 3538976 | tf_op jit(solution)/shard_map/all_to_all | solution.py:119
  361.7 36.4 %fusion.51 = f32[24,24,2,768]{3,1,2,0:T(8,128)S(1)} fusion(f32[16,96,2,768,1]{3,1,0,2,4:T(8,128)} %constant.173, f32[16,24,24,96]{3,2,1,0:T(8,128)} %all-to-all-done), kind=kOutput, calls=%fused_computation.48 | convolution fusion | flops 16307453952 | bytes 16515072 | tf_op jit(solution)/shard_map/sziy,syhj->hzij/dot_general | solution.py:122
  401.5 38.1 %collective-permute-done = f32[24,24,768]{2,1,0:T(8,128)} collective-permute-done((f32[24,24,768]{2,1,0:T(8,128)}, f32[24,24,768]{2,1,0:T(8,128)}, u32[]{:S(2)}, u32[]{:S(2)}) %collective-permute-start) | collective-permute-done | bytes 1769504 | tf_op jit(solution)/shard_map/ppermute | solution.py:85
  451.9 38.7 %collective-permute-done.1 = f32[24,24,768]{2,1,0:T(8,128)S(1)} collective-permute-done((f32[24,24,768]{2,1,0:T(8,128)S(1)}, f32[24,24,768]{2,1,0:T(8,128)S(1)}, u32[]{:S(2)}, u32[]{:S(2)}) %collective-permute-start.1) | collective-permute-done | bytes 1769504 | tf_op jit(solution)/shard_map/ppermute | solution.py:85
  490.9 26.8 %fusion.38 = f32[16,24,24,96]{3,2,1,0:T(8,128)} fusion(f32[2,768,16,96,1]{1,3,0,4,2:T(8,128)} %constant.174, f32[1,24,24,768]{3,2,0,1:T(8,128)S(1)} %get-tuple-element.10, f32[1,24,24,768]{3,2,0,1:T(8,128)S(1)} %get-tuple-element.9), kind=kOutput, calls=%fused_computation.43 | convolution fusion | flops 16308338688 | bytes 16515072 | tf_op jit(solution)/shard_map/hzij,hjsy->sziy/dot_general | solution.py:131
  517.7 8.2 all-to-all-start.1
  525.9 37.5 %fusion.54 = f32[24,24,2,768]{3,1,2,0:T(8,128)S(1)} fusion(f32[16,96,2,768,1]{3,1,0,2,4:T(8,128)} %constant.173, f32[16,24,24,96]{3,2,1,0:T(8,128)} %all-to-all-done.2), kind=kOutput, calls=%fused_computation.49 | convolution fusion | flops 16307453952 | bytes 16515072 | tf_op jit(solution)/shard_map/sziy,syhj->hzij/dot_general | solution.py:122
  563.8 39.8 %collective-permute-done.2 = f32[24,24,768]{2,1,0:T(8,128)S(1)} collective-permute-done((f32[24,24,768]{2,1,0:T(8,128)S(1)}, f32[24,24,768]{2,1,0:T(8,128)S(1)}, u32[]{:S(2)}, u32[]{:S(2)}) %collective-permute-start.2) | collective-permute-done | bytes 1769504 | tf_op jit(solution)/shard_map/ppermute | solution.py:85
  614.4 38.9 %collective-permute-done.3 = f32[24,24,768]{2,1,0:T(8,128)S(1)} collective-permute-done((f32[24,24,768]{2,1,0:T(8,128)S(1)}, f32[24,24,768]{2,1,0:T(8,128)S(1)}, u32[]{:S(2)}, u32[]{:S(2)}) %collective-permute-start.3) | collective-permute-done | bytes 1769504 | tf_op jit(solution)/shard_map/ppermute | solution.py:85
  653.5 26.7 %fusion.29 = f32[16,24,24,96]{3,2,1,0:T(8,128)} fusion(f32[2,768,16,96,1]{1,3,0,4,2:T(8,128)} %constant.174, f32[1,24,24,768]{3,2,1,0:T(8,128)S(1)} %get-tuple-element.14, f32[1,24,24,768]{3,2,1,0:T(8,128)S(1)} %get-tuple-element.13), kind=kOutput, calls=%fused_computation.40 | convolution fusion | flops 16308338688 | bytes 16515072 | tf_op jit(solution)/shard_map/hzij,hjsy->sziy/dot_general | solution.py:131
  680.3 8.1 all-to-all-start.3
  688.3 37.5 %fusion.57 = f32[24,24,2,768]{3,1,2,0:T(8,128)S(1)} fusion(f32[16,96,2,768,1]{3,1,0,2,4:T(8,128)} %constant.173, f32[16,24,24,96]{3,2,1,0:T(8,128)} %all-to-all-done.4), kind=kOutput, calls=%fused_computation.50 | convolution fusion | flops 16307453952 | bytes 16515072 | tf_op jit(solution)/shard_map/sziy,syhj->hzij/dot_general | solution.py:122
  726.2 39.8 %collective-permute-done.4 = f32[24,24,768]{2,1,0:T(8,128)S(1)} collective-permute-done((f32[24,24,768]{2,1,0:T(8,128)S(1)}, f32[24,24,768]{2,1,0:T(8,128)S(1)}, u32[]{:S(2)}, u32[]{:S(2)}) %collective-permute-start.4) | collective-permute-done | bytes 1769504 | tf_op jit(solution)/shard_map/ppermute | solution.py:85
  776.8 38.9 %collective-permute-done.5 = f32[24,24,768]{2,1,0:T(8,128)S(1)} collective-permute-done((f32[24,24,768]{2,1,0:T(8,128)S(1)}, f32[24,24,768]{2,1,0:T(8,128)S(1)}, u32[]{:S(2)}, u32[]{:S(2)}) %collective-permute-start.5) | collective-permute-done | bytes 1769504 | tf_op jit(solution)/shard_map/ppermute | solution.py:85
  815.9 26.5 %fusion.32 = f32[16,24,24,96]{3,2,1,0:T(8,128)} fusion(f32[2,768,16,96,1]{1,3,0,4,2:T(8,128)} %constant.174, f32[1,24,24,768]{3,2,1,0:T(8,128)S(1)} %get-tuple-element.18, f32[1,24,24,768]{3,2,1,0:T(8,128)S(1)} %get-tuple-element.17), kind=kOutput, calls=%fused_computation.41 | convolution fusion | flops 16308338688 | bytes 16515072 | tf_op jit(solution)/shard_map/hzij,hjsy->sziy/dot_general | solution.py:131
  842.4 7.8 all-to-all-start.5
  850.3 37.5 %fusion.60 = f32[24,24,2,768]{3,1,2,0:T(8,128)S(1)} fusion(f32[16,96,2,768,1]{3,1,0,2,4:T(8,128)} %constant.173, f32[16,24,24,96]{3,2,1,0:T(8,128)} %all-to-all-done.6), kind=kOutput, calls=%fused_computation.51 | convolution fusion | flops 16307453952 | bytes 16515072 | tf_op jit(solution)/shard_map/sziy,syhj->hzij/dot_general | solution.py:122
  888.1 39.8 %collective-permute-done.6 = f32[24,24,768]{2,1,0:T(8,128)S(1)} collective-permute-done((f32[24,24,768]{2,1,0:T(8,128)S(1)}, f32[24,24,768]{2,1,0:T(8,128)S(1)}, u32[]{:S(2)}, u32[]{:S(2)}) %collective-permute-start.6) | collective-permute-done | bytes 1769504 | tf_op jit(solution)/shard_map/ppermute | solution.py:85
  938.6 38.9 %collective-permute-done.7 = f32[24,24,768]{2,1,0:T(8,128)S(1)} collective-permute-done((f32[24,24,768]{2,1,0:T(8,128)S(1)}, f32[24,24,768]{2,1,0:T(8,128)S(1)}, u32[]{:S(2)}, u32[]{:S(2)}) %collective-permute-start.7) | collective-permute-done | bytes 1769504 | tf_op jit(solution)/shard_map/ppermute | solution.py:85
  977.8 26.8 %fusion.35 = f32[16,24,24,96]{3,2,1,0:T(8,128)} fusion(f32[2,768,16,96,1]{1,3,0,4,2:T(8,128)} %constant.174, f32[1,24,24,768]{3,2,1,0:T(8,128)S(1)} %get-tuple-element.6, f32[1,24,24,768]{3,2,1,0:T(8,128)S(1)} %get-tuple-element.5), kind=kOutput, calls=%fused_computation.42 | convolution fusion | flops 16308338688 | bytes 16515072 | tf_op jit(solution)/shard_map/hzij,hjsy->sziy/dot_general | solution.py:131
  1004.6 8.0 all-to-all-start.7
  1012.6 26.7 %fusion.87 = f32[24,96,1536,1]{2,1,0,3:T(8,128)} fusion(f32[16,24,24,96]{3,2,1,0:T(8,128)} %all-to-all-done.5, f32[16,24,1536,1]{2,1,3,0:T(8,128)S(1)} %copy-done.7), kind=kOutput, calls=%fused_computation.118 | convolution fusion | flops 16307453952 | bytes 20054016 | tf_op jit(solution)/shard_map/dziy,din->zyn/dot_general | solution.py:136
  1039.4 27.3 %fusion.86 = f32[24,96,1536,1]{2,1,0,3:T(8,128)} fusion(f32[16,24,24,96]{3,2,1,0:T(8,128)} %all-to-all-done.3, f32[16,24,1536,1]{2,1,3,0:T(8,128)S(1)} %copy-done.6), kind=kOutput, calls=%fused_computation.117 | convolution fusion | flops 16307453952 | bytes 20054016 | tf_op jit(solution)/shard_map/dziy,din->zyn/dot_general | solution.py:136
  1066.7 26.9 %fusion.85 = f32[24,96,1536,1]{2,1,0,3:T(8,128)} fusion(f32[16,24,24,96]{3,2,1,0:T(8,128)} %all-to-all-done.1, f32[16,24,1536,1]{2,1,3,0:T(8,128)S(1)} %copy-done.5), kind=kOutput, calls=%fused_computation.116 | convolution fusion | flops 16307453952 | bytes 20054016 | tf_op jit(solution)/shard_map/dziy,din->zyn/dot_general | solution.py:136
  1093.6 22.8 %all-to-all-done.7 = f32[16,24,24,96]{3,2,1,0:T(8,128)} async-done(((f32[16,24,24,96]{3,2,1,0:T(8,128)}), f32[16,24,24,96]{3,2,1,0:T(8,128)}, u32[]{:S(2)}, u32[]{:S(2)}) %all-to-all-start.7) | async-done | bytes 3538976 | tf_op jit(solution)/shard_map/all_to_all | solution.py:135
  1116.3 53.3 %fusion = f32[24,96,1536]{2,1,0:T(8,128)} fusion(f32[24,96,1536,1]{2,1,0,3:T(8,128)} %fusion.87, f32[24,96,1536,1]{2,1,0,3:T(8,128)} %fusion.86, f32[24,96,1536,1]{2,1,0,3:T(8,128)} %fusion.85, f32[16,24,24,96]{3,2,1,0:T(8,128)} %all-to-all-done.7, f32[16,24,1536,1]{2,1,3,0:T(8,128)S(1)} %copy-done.4), kind=kOutput, calls=%fused_computation.1 | convolution fusion | flops 16321609728 | bytes 62521344 | tf_op jit(solution)/shard_map/dziy,din->zyn/dot_general | solution.py:136
  (70 shorter events, 73.2 us)
Async XLA Ops:
  27.8 7.1 copy-start.10
  27.8 110.7 %all-to-all-start = ((f32[16,24,24,96]{3,2,1,0:T(8,128)}), f32[16,24,24,96]{3,2,1,0:T(8,128)}, u32[]{:S(2)}, u32[]{:S(2)}) async-start(f32[16,24,24,96]{3,2,1,0:T(8,128)} %fusion.39), calls=%async_computation | async-start | bytes 9437184 | tf_op jit(solution)/shard_map/all_to_all | solution.py:119
  62.1 82.0 %copy-start.9 = (f32[1536,16,24,1]{0,2,3,1:T(8,128)S(1)}, f32[1536,16,24,1]{0,2,3,1:T(8,128)}, u32[]{:S(2)}) copy-start(f32[1536,16,24,1]{0,2,3,1:T(8,128)} %constant.178) | copy-start | bytes 7077892
  138.5 109.1 %all-to-all-start.2 = ((f32[16,24,24,96]{3,2,1,0:T(8,128)}), f32[16,24,24,96]{3,2,1,0:T(8,128)}, u32[]{:S(2)}, u32[]{:S(2)}) async-start(f32[16,24,24,96]{3,2,1,0:T(8,128)} %fusion.42), calls=%async_computation.2 | async-start | bytes 9437184 | tf_op jit(solution)/shard_map/all_to_all | solution.py:119
  171.2 81.7 %copy-start.8 = (f32[1536,16,24,1]{0,2,3,1:T(8,128)S(1)}, f32[1536,16,24,1]{0,2,3,1:T(8,128)}, u32[]{:S(2)}) copy-start(f32[1536,16,24,1]{0,2,3,1:T(8,128)} %constant.180) | copy-start | bytes 7077892
  247.6 108.8 %all-to-all-start.4 = ((f32[16,24,24,96]{3,2,1,0:T(8,128)}), f32[16,24,24,96]{3,2,1,0:T(8,128)}, u32[]{:S(2)}, u32[]{:S(2)}) async-start(f32[16,24,24,96]{3,2,1,0:T(8,128)} %fusion.45), calls=%async_computation.4 | async-start | bytes 9437184 | tf_op jit(solution)/shard_map/all_to_all | solution.py:119
  356.4 161.2 %all-to-all-start.6 = ((f32[16,24,24,96]{3,2,1,0:T(8,128)}), f32[16,24,24,96]{3,2,1,0:T(8,128)}, u32[]{:S(2)}, u32[]{:S(2)}) async-start(f32[16,24,24,96]{3,2,1,0:T(8,128)} %fusion.48), calls=%async_computation.6 | async-start | bytes 9437184 | tf_op jit(solution)/shard_map/all_to_all | solution.py:119
  399.4 40.1 %collective-permute-start = (f32[24,24,768]{2,1,0:T(8,128)}, f32[24,24,768]{2,1,0:T(8,128)}, u32[]{:S(2)}, u32[]{:S(2)}) collective-permute-start(f32[24,24,768]{2,1,0:T(8,128)} %dynamic-slice_bitcast_fusion.7), channel_id=1, source_target_pairs={{0,16},{16,0},{1,17},{17,1},{2,18},{18,2},{3,19},{19,3},{4,20},{20... | collective-permute-start | bytes 5308424 | tf_op jit(solution)/shard_map/ppermute | solution.py:85
  449.9 40.7 %copy-start.1 = (f32[48,24,768]{2,1,0:T(8,128)S(1)}, f32[48,24,768]{2,1,0:T(8,128)}, u32[]{:S(2)}) copy-start(f32[48,24,768]{2,1,0:T(8,128)} %shard_map.118) | copy-start | bytes 10616836
  451.6 39.0 %collective-permute-start.1 = (f32[24,24,768]{2,1,0:T(8,128)S(1)}, f32[24,24,768]{2,1,0:T(8,128)S(1)}, u32[]{:S(2)}, u32[]{:S(2)}) collective-permute-start(f32[24,24,768]{2,1,0:T(8,128)S(1)} %dynamic-slice_bitcast_fusion.6), channel_id=1, source_target_pairs={{0,16},{16,0},{1,17},{17,1},{2,18},{18,2},{3,19},{19,3},{4,20},{20... | collective-permute-start | bytes 5308424 | tf_op jit(solution)/shard_map/ppermute | solution.py:85
  517.7 162.6 %all-to-all-start.1 = ((f32[16,24,24,96]{3,2,1,0:T(8,128)}), f32[16,24,24,96]{3,2,1,0:T(8,128)}, u32[]{:S(2)}, u32[]{:S(2)}) async-start(f32[16,24,24,96]{3,2,1,0:T(8,128)} %fusion.38), calls=%async_computation.1 | async-start | bytes 9437184 | tf_op jit(solution)/shard_map/all_to_all | solution.py:135
  563.5 40.0 %collective-permute-start.2 = (f32[24,24,768]{2,1,0:T(8,128)S(1)}, f32[24,24,768]{2,1,0:T(8,128)S(1)}, u32[]{:S(2)}, u32[]{:S(2)}) collective-permute-start(f32[24,24,768]{2,1,0:T(8,128)S(1)} %dynamic-slice_bitcast_fusion.5), channel_id=1, source_target_pairs={{0,16},{16,0},{1,17},{17,1},{2,18},{18,2},{3,19},{19,3},{4,20},{20... | collective-permute-start | bytes 5308424 | tf_op jit(solution)/shard_map/ppermute | solution.py:85
  612.4 40.8 %copy-start.2 = (f32[48,24,768]{2,1,0:T(8,128)S(1)}, f32[48,24,768]{2,1,0:T(8,128)}, u32[]{:S(2)}) copy-start(f32[48,24,768]{2,1,0:T(8,128)} %shard_map.119) | copy-start | bytes 10616836
  614.2 39.1 %collective-permute-start.3 = (f32[24,24,768]{2,1,0:T(8,128)S(1)}, f32[24,24,768]{2,1,0:T(8,128)S(1)}, u32[]{:S(2)}, u32[]{:S(2)}) collective-permute-start(f32[24,24,768]{2,1,0:T(8,128)S(1)} %dynamic-slice_bitcast_fusion.4), channel_id=1, source_target_pairs={{0,16},{16,0},{1,17},{17,1},{2,18},{18,2},{3,19},{19,3},{4,20},{20... | collective-permute-start | bytes 5308424 | tf_op jit(solution)/shard_map/ppermute | solution.py:85
  680.3 162.2 %all-to-all-start.3 = ((f32[16,24,24,96]{3,2,1,0:T(8,128)}), f32[16,24,24,96]{3,2,1,0:T(8,128)}, u32[]{:S(2)}, u32[]{:S(2)}) async-start(f32[16,24,24,96]{3,2,1,0:T(8,128)} %fusion.29), calls=%async_computation.3 | async-start | bytes 9437184 | tf_op jit(solution)/shard_map/all_to_all | solution.py:135
  726.0 40.0 %collective-permute-start.4 = (f32[24,24,768]{2,1,0:T(8,128)S(1)}, f32[24,24,768]{2,1,0:T(8,128)S(1)}, u32[]{:S(2)}, u32[]{:S(2)}) collective-permute-start(f32[24,24,768]{2,1,0:T(8,128)S(1)} %dynamic-slice_bitcast_fusion.3), channel_id=1, source_target_pairs={{0,16},{16,0},{1,17},{17,1},{2,18},{18,2},{3,19},{19,3},{4,20},{20... | collective-permute-start | bytes 5308424 | tf_op jit(solution)/shard_map/ppermute | solution.py:85
  774.8 40.8 %copy-start.3 = (f32[48,24,768]{2,1,0:T(8,128)S(1)}, f32[48,24,768]{2,1,0:T(8,128)}, u32[]{:S(2)}) copy-start(f32[48,24,768]{2,1,0:T(8,128)} %shard_map.120) | copy-start | bytes 10616836
  776.6 39.1 %collective-permute-start.5 = (f32[24,24,768]{2,1,0:T(8,128)S(1)}, f32[24,24,768]{2,1,0:T(8,128)S(1)}, u32[]{:S(2)}, u32[]{:S(2)}) collective-permute-start(f32[24,24,768]{2,1,0:T(8,128)S(1)} %dynamic-slice_bitcast_fusion.2), channel_id=1, source_target_pairs={{0,16},{16,0},{1,17},{17,1},{2,18},{18,2},{3,19},{19,3},{4,20},{20... | collective-permute-start | bytes 5308424 | tf_op jit(solution)/shard_map/ppermute | solution.py:85
  842.4 162.1 %all-to-all-start.5 = ((f32[16,24,24,96]{3,2,1,0:T(8,128)}), f32[16,24,24,96]{3,2,1,0:T(8,128)}, u32[]{:S(2)}, u32[]{:S(2)}) async-start(f32[16,24,24,96]{3,2,1,0:T(8,128)} %fusion.32), calls=%async_computation.5 | async-start | bytes 9437184 | tf_op jit(solution)/shard_map/all_to_all | solution.py:135
  887.9 40.0 %collective-permute-start.6 = (f32[24,24,768]{2,1,0:T(8,128)S(1)}, f32[24,24,768]{2,1,0:T(8,128)S(1)}, u32[]{:S(2)}, u32[]{:S(2)}) collective-permute-start(f32[24,24,768]{2,1,0:T(8,128)S(1)} %dynamic-slice_bitcast_fusion.1), channel_id=1, source_target_pairs={{0,16},{16,0},{1,17},{17,1},{2,18},{18,2},{3,19},{19,3},{4,20},{20... | collective-permute-start | bytes 5308424 | tf_op jit(solution)/shard_map/ppermute | solution.py:85
  936.7 40.8 %copy-start = (f32[48,24,768]{2,1,0:T(8,128)S(1)}, f32[48,24,768]{2,1,0:T(8,128)}, u32[]{:S(2)}) copy-start(f32[48,24,768]{2,1,0:T(8,128)} %shard_map.121) | copy-start | bytes 10616836
  938.4 39.1 %collective-permute-start.7 = (f32[24,24,768]{2,1,0:T(8,128)S(1)}, f32[24,24,768]{2,1,0:T(8,128)S(1)}, u32[]{:S(2)}, u32[]{:S(2)}) collective-permute-start(f32[24,24,768]{2,1,0:T(8,128)S(1)} %dynamic-slice_bitcast_fusion), channel_id=1, source_target_pairs={{0,16},{16,0},{1,17},{17,1},{2,18},{18,2},{3,19},{19,3},{4,20},{20... | collective-permute-start | bytes 5308424 | tf_op jit(solution)/shard_map/ppermute | solution.py:85
  1004.6 8.1 copy-start.7
  1004.6 111.7 %all-to-all-start.7 = ((f32[16,24,24,96]{3,2,1,0:T(8,128)}), f32[16,24,24,96]{3,2,1,0:T(8,128)}, u32[]{:S(2)}, u32[]{:S(2)}) async-start(f32[16,24,24,96]{3,2,1,0:T(8,128)} %fusion.35), calls=%async_computation.7 | async-start | bytes 9437184 | tf_op jit(solution)/shard_map/all_to_all | solution.py:135
  1012.6 26.8 %copy-start.6 = (f32[16,24,1536,1]{2,1,3,0:T(8,128)S(1)}, f32[16,24,1536,1]{2,1,3,0:T(8,128)}, u32[]{:S(2)}) copy-start(f32[16,24,1536,1]{2,1,3,0:T(8,128)} %constant.177) | copy-start | bytes 7077892
  1039.4 27.3 %copy-start.5 = (f32[16,24,1536,1]{2,1,3,0:T(8,128)S(1)}, f32[16,24,1536,1]{2,1,3,0:T(8,128)}, u32[]{:S(2)}) copy-start(f32[16,24,1536,1]{2,1,3,0:T(8,128)} %constant.175) | copy-start | bytes 7077892
  1066.7 49.6 %copy-start.4 = (f32[16,24,1536,1]{2,1,3,0:T(8,128)S(1)}, f32[16,24,1536,1]{2,1,3,0:T(8,128)}, u32[]{:S(2)}) copy-start(f32[16,24,1536,1]{2,1,3,0:T(8,128)} %constant.181) | copy-start | bytes 7077892

commit v7 on v6

--- a/solution.py
+++ b/solution.py
@@ -113,13 +113,14 @@
         return (np.arange(col_count)[:, None] * part_x + chunk * chunk_x
                 + np.arange(chunk_x)[None, :]).reshape(-1)
 
-    def along_x(chunk, slab):
+    def spread_x(chunk):
         table_chunk = cas_constant(index_x, chunk_waves(chunk), full_x).reshape(full_x, col_count, chunk_x)
-        spread = jnp.einsum("zyx,xdi->dziy", slab, table_chunk, precision=highest)
-        return lax.all_to_all(spread, "col", 0, 0, tiled=True)
+        return jnp.einsum("zyx,xdi->dziy", source, table_chunk, precision=highest)
 
-    def middle(chunk, gathered):
-        spectra = jnp.einsum("sziy,syhj->hzij", gathered, forward_y, precision=highest)
+    def spectra_y(gathered):
+        return jnp.einsum("sziy,syhj->hzij", gathered, forward_y, precision=highest)
+
+    def middle(chunk, spectra):
         columns = exchange(spectra, "row")
         columns = columns.reshape(row_count * slab_levels, chunk_x, part_y)
         wave_x = lax.axis_index("col") * part_x + chunk * chunk_x + lax.iota(jnp.int32, chunk_x)
@@ -135,20 +136,16 @@
         scattered = lax.all_to_all(back_y, "col", 0, 0, tiled=True)
         return jnp.einsum("dziy,din->zyn", scattered, table_back, precision=highest)
 
-    gathered = along_x(0, source)
-    pass
+    lead = min(2, chunks)
+    gathered = [lax.all_to_all(spread_x(chunk), "col", 0, 0, tiled=True) for chunk in range(lead)]
     pressure = None
-    back_y = None
     for chunk in range(chunks):
-        gathered_next = along_x(chunk + 1, source) if chunk + 1 < chunks else None
-        if back_y is not None:
-            part = back_x(chunk - 1, back_y)
-            pressure = part if pressure is None else pressure + part
-        back_y = middle(chunk, gathered)
-        gathered = gathered_next
-        pass
-    part = back_x(chunks - 1, back_y)
-    pressure = part if pressure is None else pressure + part
+        spectra = spectra_y(gathered[chunk])
+        if chunk + lead < chunks:
+            spread, spectra = lax.optimization_barrier((spread_x(chunk + lead), spectra))
+            gathered.append(lax.all_to_all(spread, "col", 0, 0, tiled=True))
+        part = back_x(chunk, middle(chunk, spectra))
+        pressure = part if pressure is None else pressure + part
     return pressure * scale
 
 

time: 1180 us -> 1100 us (0.932)
  waiting for transfers between devices: 565 us -> 489 us
    all_to_all x4, waiting for transfers between devices: 229 us -> 155 us  [the longest x2 115 us: body(): lax.all_to_all(spread_x(chunk), 'col', 0, 0, tiled=True)]
  transfers between devices with their start and end apart: 16 -> 16, of which waited for: 12 -> 12; matrix products, arithmetic and copies ran while one was open for 38% -> 40% of each run, Pallas kernels for 2% -> 2%
where the time goes in v7:
time: 1100 us
  matrix products  500 us (45%)
  waiting for transfers between devices  489 us (44%)
  starting transfers between devices  57.4 us (5%)
  Pallas kernels  26.1 us (2%)
  other arithmetic  14.2 us (1%)
    ppermute x8, waiting for transfers between devices, exchange(): arrived.append(lax.ppermute(outgoing, axis_name, perm))  312 us
    dot_general x4, matrix products, spectra_y(): return jnp.einsum('sziy,syhj->hzij', gathered, forward_y, precision=highest)  149 us
    dot_general x4, matrix products, back_x(): return jnp.einsum('dziy,din->zyn', scattered, table_back, precision=highest)  134 us
    all_to_all x2, waiting for transfers between devices, body(): lax.all_to_all(spread_x(chunk), 'col', 0, 0, tiled=True)  115 us
    dot_general x4, matrix products, spread_x(): return jnp.einsum('zyx,xdi->dziy', source, table_chunk, precision=highest)  109 us
    dot_general x4, matrix products, middle(): return jnp.einsum('hzij,hjsy->sziy', returned, inverse_y, precision=highest)  107 us
    all_to_all x2, waiting for transfers between devices, body(): gathered.append(lax.all_to_all(spread, 'col', 0, 0, tiled=True))  39.7 us
    all_to_all x4, starting transfers between devices, back_x(): scattered = lax.all_to_all(back_y, 'col', 0, 0, tiled=True)  32 us
  transfers between devices with their start and end apart: 16, of which 12 were waited for; matrix products, arithmetic and copies ran while one was open for 40% of the time, Pallas kernels for 2%

profile of v7, /device:TPU:15, one launch (start us, length us, event | category | flops | bytes accessed | tf_op | source)
XLA Modules:
  0.0 1097.4 jit_solution(9373048760422671371)
XLA Ops:
  0.0 27.8 %fusion.42 = f32[16,24,24,96]{3,2,1,0:T(8,128)} fusion(f32[1536,16,24,1]{0,2,3,1:T(8,128)} %constant.173, f32[24,96,1536]{2,1,0:T(8,128)} %param.12), kind=kOutput, calls=%fused_computation.45 | convolution fusion | flops 16307453952 | bytes 20054016 | tf_op jit(solution)/shard_map/zyx,xdi->dziy/dot_general | solution.py:118
  35.0 27.2 %fusion.48 = f32[16,24,24,96]{3,2,1,0:T(8,128)} fusion(f32[1536,16,24,1]{0,2,3,1:T(8,128)S(1)} %copy-done.10, f32[24,96,1536]{2,1,0:T(8,128)} %param.12), kind=kOutput, calls=%fused_computation.47 | convolution fusion | flops 16307453952 | bytes 20054016 | tf_op jit(solution)/shard_map/zyx,xdi->dziy/dot_general | solution.py:118
  62.1 76.4 %all-to-all-done = f32[16,24,24,96]{3,2,1,0:T(8,128)} async-done(((f32[16,24,24,96]{3,2,1,0:T(8,128)}), f32[16,24,24,96]{3,2,1,0:T(8,128)}, u32[]{:S(2)}, u32[]{:S(2)}) %all-to-all-start) | async-done | bytes 3538976 | tf_op jit(solution)/shard_map/all_to_all | solution.py:140
  144.2 27.2 %fusion.39 = f32[16,24,24,96]{3,2,1,0:T(8,128)} fusion(f32[1536,16,24,1]{0,2,3,1:T(8,128)S(1)} %copy-done.9, f32[24,96,1536]{2,1,0:T(8,128)} %param.12), kind=kOutput, calls=%fused_computation.44 | convolution fusion | flops 16307453952 | bytes 20054016 | tf_op jit(solution)/shard_map/zyx,xdi->dziy/dot_general | solution.py:118
  171.5 37.6 %fusion.51 = f32[2,24,24,768]{3,2,0,1:T(8,128)} fusion(f32[16,96,2,768,1]{3,1,0,2,4:T(8,128)S(1)} %bitcast.286, f32[16,24,24,96]{3,2,1,0:T(8,128)} %all-to-all-done), kind=kOutput, calls=%fused_computation.48 | convolution fusion | flops 16307453952 | bytes 16515072 | tf_op jit(solution)/shard_map/sziy,syhj->hzij/dot_general | solution.py:121
  209.1 38.7 %all-to-all-done.2 = f32[16,24,24,96]{3,2,1,0:T(8,128)} async-done(((f32[16,24,24,96]{3,2,1,0:T(8,128)}), f32[16,24,24,96]{3,2,1,0:T(8,128)}, u32[]{:S(2)}, u32[]{:S(2)}) %all-to-all-start.2) | async-done | bytes 3538976 | tf_op jit(solution)/shard_map/all_to_all | solution.py:140
  253.0 27.2 %fusion.45 = f32[16,24,24,96]{3,2,1,0:T(8,128)} fusion(f32[1536,16,24,1]{0,2,3,1:T(8,128)S(1)} %copy-done.8, f32[24,96,1536]{2,1,0:T(8,128)} %param.12), kind=kOutput, calls=%fused_computation.46 | convolution fusion | flops 16307453952 | bytes 20054016 | tf_op jit(solution)/shard_map/zyx,xdi->dziy/dot_general | solution.py:118
  280.2 36.6 %fusion.54 = f32[2,24,24,768]{3,2,0,1:T(8,128)S(1)} fusion(f32[16,96,2,768,1]{3,1,0,2,4:T(8,128)} %constant.174, f32[16,24,24,96]{3,2,1,0:T(8,128)} %all-to-all-done.2), kind=kOutput, calls=%fused_computation.49 | convolution fusion | flops 16307453952 | bytes 16515072 | tf_op jit(solution)/shard_map/sziy,syhj->hzij/dot_general | solution.py:121
  316.8 39.7 %all-to-all-done.4 = f32[16,24,24,96]{3,2,1,0:T(8,128)} async-done(((f32[16,24,24,96]{3,2,1,0:T(8,128)}), f32[16,24,24,96]{3,2,1,0:T(8,128)}, u32[]{:S(2)}, u32[]{:S(2)}) %all-to-all-start.4) | async-done | bytes 3538976 | tf_op jit(solution)/shard_map/all_to_all | solution.py:146
  366.3 38.1 %collective-permute-done = f32[24,24,768]{2,1,0:T(8,128)} collective-permute-done((f32[24,24,768]{2,1,0:T(8,128)}, f32[24,24,768]{2,1,0:T(8,128)}, u32[]{:S(2)}, u32[]{:S(2)}) %collective-permute-start) | collective-permute-done | bytes 1769504 | tf_op jit(solution)/shard_map/ppermute | solution.py:85
  417.2 38.7 %collective-permute-done.1 = f32[24,24,768]{2,1,0:T(8,128)S(1)} collective-permute-done((f32[24,24,768]{2,1,0:T(8,128)S(1)}, f32[24,24,768]{2,1,0:T(8,128)S(1)}, u32[]{:S(2)}, u32[]{:S(2)}) %collective-permute-start.1) | collective-permute-done | bytes 1769504 | tf_op jit(solution)/shard_map/ppermute | solution.py:85
  456.2 27.0 %fusion.38 = f32[16,24,24,96]{3,2,1,0:T(8,128)} fusion(f32[2,768,16,96,1]{1,3,0,4,2:T(8,128)} %constant.175, f32[1,24,24,768]{3,2,0,1:T(8,128)S(1)} %get-tuple-element.18, f32[1,24,24,768]{3,2,0,1:T(8,128)S(1)} %get-tuple-element.17), kind=kOutput, calls=%fused_computation.43 | convolution fusion | flops 16308338688 | bytes 16515072 | tf_op jit(solution)/shard_map/hzij,hjsy->sziy/dot_general | solution.py:132
  483.2 7.9 all-to-all-start.1
  491.6 39.6 %collective-permute-done.2 = f32[24,24,768]{2,1,0:T(8,128)S(1)} collective-permute-done((f32[24,24,768]{2,1,0:T(8,128)S(1)}, f32[24,24,768]{2,1,0:T(8,128)S(1)}, u32[]{:S(2)}, u32[]{:S(2)}) %collective-permute-start.2) | collective-permute-done | bytes 1769504 | tf_op jit(solution)/shard_map/ppermute | solution.py:85
  542.1 38.6 %collective-permute-done.3 = f32[24,24,768]{2,1,0:T(8,128)S(1)} collective-permute-done((f32[24,24,768]{2,1,0:T(8,128)S(1)}, f32[24,24,768]{2,1,0:T(8,128)S(1)}, u32[]{:S(2)}, u32[]{:S(2)}) %collective-permute-start.3) | collective-permute-done | bytes 1769504 | tf_op jit(solution)/shard_map/ppermute | solution.py:85
  581.1 26.5 %fusion.29 = f32[16,24,24,96]{3,2,1,0:T(8,128)} fusion(f32[2,768,16,96,1]{1,3,0,4,2:T(8,128)} %constant.175, f32[1,24,24,768]{3,2,1,0:T(8,128)S(1)} %get-tuple-element.22, f32[1,24,24,768]{3,2,1,0:T(8,128)S(1)} %get-tuple-element.21), kind=kOutput, calls=%fused_computation.40 | convolution fusion | flops 16308338688 | bytes 16515072 | tf_op jit(solution)/shard_map/hzij,hjsy->sziy/dot_general | solution.py:132
  607.6 8.2 all-to-all-start.3
  615.8 37.5 %fusion.57 = f32[24,24,2,768]{3,1,2,0:T(8,128)S(1)} fusion(f32[16,96,2,768,1]{3,1,0,2,4:T(8,128)} %constant.174, f32[16,24,24,96]{3,2,1,0:T(8,128)} %all-to-all-done.4), kind=kOutput, calls=%fused_computation.50 | convolution fusion | flops 16307453952 | bytes 16515072 | tf_op jit(solution)/shard_map/sziy,syhj->hzij/dot_general | solution.py:121
  653.7 39.7 %collective-permute-done.4 = f32[24,24,768]{2,1,0:T(8,128)S(1)} collective-permute-done((f32[24,24,768]{2,1,0:T(8,128)S(1)}, f32[24,24,768]{2,1,0:T(8,128)S(1)}, u32[]{:S(2)}, u32[]{:S(2)}) %collective-permute-start.4) | collective-permute-done | bytes 1769504 | tf_op jit(solution)/shard_map/ppermute | solution.py:85
  704.4 38.8 %collective-permute-done.5 = f32[24,24,768]{2,1,0:T(8,128)S(1)} collective-permute-done((f32[24,24,768]{2,1,0:T(8,128)S(1)}, f32[24,24,768]{2,1,0:T(8,128)S(1)}, u32[]{:S(2)}, u32[]{:S(2)}) %collective-permute-start.5) | collective-permute-done | bytes 1769504 | tf_op jit(solution)/shard_map/ppermute | solution.py:85
  743.4 26.5 %fusion.32 = f32[16,24,24,96]{3,2,1,0:T(8,128)} fusion(f32[2,768,16,96,1]{1,3,0,4,2:T(8,128)} %constant.175, f32[1,24,24,768]{3,2,1,0:T(8,128)S(1)} %get-tuple-element.26, f32[1,24,24,768]{3,2,1,0:T(8,128)S(1)} %get-tuple-element.25), kind=kOutput, calls=%fused_computation.41 | convolution fusion | flops 16308338688 | bytes 16515072 | tf_op jit(solution)/shard_map/hzij,hjsy->sziy/dot_general | solution.py:132
  770.0 7.8 all-to-all-start.5
  777.8 37.5 %fusion.60 = f32[24,24,2,768]{3,1,2,0:T(8,128)S(1)} fusion(f32[16,96,2,768,1]{3,1,0,2,4:T(8,128)} %constant.174, f32[16,24,24,96]{3,2,1,0:T(8,128)} %all-to-all-done.6), kind=kOutput, calls=%fused_computation.51 | convolution fusion | flops 16307453952 | bytes 16515072 | tf_op jit(solution)/shard_map/sziy,syhj->hzij/dot_general | solution.py:121
  815.7 39.7 %collective-permute-done.6 = f32[24,24,768]{2,1,0:T(8,128)S(1)} collective-permute-done((f32[24,24,768]{2,1,0:T(8,128)S(1)}, f32[24,24,768]{2,1,0:T(8,128)S(1)}, u32[]{:S(2)}, u32[]{:S(2)}) %collective-permute-start.6) | collective-permute-done | bytes 1769504 | tf_op jit(solution)/shard_map/ppermute | solution.py:85
  866.4 38.8 %collective-permute-done.7 = f32[24,24,768]{2,1,0:T(8,128)S(1)} collective-permute-done((f32[24,24,768]{2,1,0:T(8,128)S(1)}, f32[24,24,768]{2,1,0:T(8,128)S(1)}, u32[]{:S(2)}, u32[]{:S(2)}) %collective-permute-start.7) | collective-permute-done | bytes 1769504 | tf_op jit(solution)/shard_map/ppermute | solution.py:85
  905.4 26.8 %fusion.35 = f32[16,24,24,96]{3,2,1,0:T(8,128)} fusion(f32[2,768,16,96,1]{1,3,0,4,2:T(8,128)} %constant.175, f32[1,24,24,768]{3,2,1,0:T(8,128)S(1)} %get-tuple-element.14, f32[1,24,24,768]{3,2,1,0:T(8,128)S(1)} %get-tuple-element.13), kind=kOutput, calls=%fused_computation.42 | convolution fusion | flops 16308338688 | bytes 16515072 | tf_op jit(solution)/shard_map/hzij,hjsy->sziy/dot_general | solution.py:132
  932.2 8.1 all-to-all-start.7
  940.3 26.8 %fusion.86 = f32[24,96,1536,1]{2,1,0,3:T(8,128)} fusion(f32[16,24,24,96]{3,2,1,0:T(8,128)} %all-to-all-done.3, f32[16,24,1536,1]{2,1,3,0:T(8,128)S(1)} %copy-done.7), kind=kOutput, calls=%fused_computation.117 | convolution fusion | flops 16307453952 | bytes 20054016 | tf_op jit(solution)/shard_map/dziy,din->zyn/dot_general | solution.py:137
  967.1 27.3 %fusion.85 = f32[24,96,1536,1]{2,1,0,3:T(8,128)} fusion(f32[16,24,24,96]{3,2,1,0:T(8,128)} %all-to-all-done.1, f32[16,24,1536,1]{2,1,3,0:T(8,128)S(1)} %copy-done.6), kind=kOutput, calls=%fused_computation.116 | convolution fusion | flops 16307453952 | bytes 20054016 | tf_op jit(solution)/shard_map/dziy,din->zyn/dot_general | solution.py:137
  994.4 26.9 %fusion.87 = f32[24,96,1536,1]{2,1,0,3:T(8,128)} fusion(f32[16,24,24,96]{3,2,1,0:T(8,128)} %all-to-all-done.5, f32[16,24,1536,1]{2,1,3,0:T(8,128)S(1)} %copy-done.5), kind=kOutput, calls=%fused_computation.118 | convolution fusion | flops 16307453952 | bytes 20054016 | tf_op jit(solution)/shard_map/dziy,din->zyn/dot_general | solution.py:137
  1021.3 22.7 %all-to-all-done.7 = f32[16,24,24,96]{3,2,1,0:T(8,128)} async-done(((f32[16,24,24,96]{3,2,1,0:T(8,128)}), f32[16,24,24,96]{3,2,1,0:T(8,128)}, u32[]{:S(2)}, u32[]{:S(2)}) %all-to-all-start.7) | async-done | bytes 3538976 | tf_op jit(solution)/shard_map/all_to_all | solution.py:136
  1044.0 53.2 %fusion = f32[24,96,1536]{2,1,0:T(8,128)} fusion(f32[24,96,1536,1]{2,1,0,3:T(8,128)} %fusion.87, f32[24,96,1536,1]{2,1,0,3:T(8,128)} %fusion.86, f32[24,96,1536,1]{2,1,0,3:T(8,128)} %fusion.85, f32[16,24,24,96]{3,2,1,0:T(8,128)} %all-to-all-done.7, f32[16,24,1536,1]{2,1,3,0:T(8,128)S(1)} %copy-done.4), kind=kOutput, calls=%fused_computation.1 | convolution fusion | flops 16321609728 | bytes 62521344 | tf_op jit(solution)/shard_map/dziy,din->zyn/dot_general | solution.py:137
  (77 shorter events, 75.8 us)
Async XLA Ops:
  27.8 7.1 copy-start.10
  27.8 110.7 %all-to-all-start = ((f32[16,24,24,96]{3,2,1,0:T(8,128)}), f32[16,24,24,96]{3,2,1,0:T(8,128)}, u32[]{:S(2)}, u32[]{:S(2)}) async-start(f32[16,24,24,96]{3,2,1,0:T(8,128)} %fusion.42), calls=%async_computation | async-start | bytes 9437184 | tf_op jit(solution)/shard_map/all_to_all | solution.py:140
  62.1 82.1 %copy-start.9 = (f32[1536,16,24,1]{0,2,3,1:T(8,128)S(1)}, f32[1536,16,24,1]{0,2,3,1:T(8,128)}, u32[]{:S(2)}) copy-start(f32[1536,16,24,1]{0,2,3,1:T(8,128)} %constant.172) | copy-start | bytes 7077892
  138.5 33.0 %slice-start = ((s8[9437184]{0:T(1024)(128)(4,1)}), s8[1048576]{0:T(1024)(128)(4,1)S(1)}, s32[]{:S(2)}) async-start(s8[9437184]{0:T(1024)(128)(4,1)} %bitcast.285), calls=%async_computation.8 | async-start | bytes 2097152
  138.5 109.3 %all-to-all-start.2 = ((f32[16,24,24,96]{3,2,1,0:T(8,128)}), f32[16,24,24,96]{3,2,1,0:T(8,128)}, u32[]{:S(2)}, u32[]{:S(2)}) async-start(f32[16,24,24,96]{3,2,1,0:T(8,128)} %fusion.48), calls=%async_computation.2 | async-start | bytes 9437184 | tf_op jit(solution)/shard_map/all_to_all | solution.py:140
  144.2 27.3 %slice-start.1 = ((s8[9437184]{0:T(1024)(128)(4,1)}), s8[4194304]{0:T(1024)(128)(4,1)S(1)}, s32[]{:S(2)}) async-start(s8[9437184]{0:T(1024)(128)(4,1)} %bitcast.285), calls=%async_computation.9 | async-start | bytes 8388608
  144.2 27.3 %slice-start.2 = ((s8[9437184]{0:T(1024)(128)(4,1)}), s8[4194304]{0:T(1024)(128)(4,1)S(1)}, s32[]{:S(2)}) async-start(s8[9437184]{0:T(1024)(128)(4,1)} %bitcast.285), calls=%async_computation.10 | async-start | bytes 8388608
  209.1 43.9 %copy-start.8 = (f32[1536,16,24,1]{0,2,3,1:T(8,128)S(1)}, f32[1536,16,24,1]{0,2,3,1:T(8,128)}, u32[]{:S(2)}) copy-start(f32[1536,16,24,1]{0,2,3,1:T(8,128)} %constant.177) | copy-start | bytes 7077892
  247.8 108.8 %all-to-all-start.4 = ((f32[16,24,24,96]{3,2,1,0:T(8,128)}), f32[16,24,24,96]{3,2,1,0:T(8,128)}, u32[]{:S(2)}, u32[]{:S(2)}) async-start(f32[16,24,24,96]{3,2,1,0:T(8,128)} %fusion.39), calls=%async_computation.4 | async-start | bytes 9437184 | tf_op jit(solution)/shard_map/all_to_all | solution.py:146
  356.6 126.6 %all-to-all-start.6 = ((f32[16,24,24,96]{3,2,1,0:T(8,128)}), f32[16,24,24,96]{3,2,1,0:T(8,128)}, u32[]{:S(2)}, u32[]{:S(2)}) async-start(f32[16,24,24,96]{3,2,1,0:T(8,128)} %fusion.45), calls=%async_computation.6 | async-start | bytes 9437184 | tf_op jit(solution)/shard_map/all_to_all | solution.py:146
  364.3 40.1 %collective-permute-start = (f32[24,24,768]{2,1,0:T(8,128)}, f32[24,24,768]{2,1,0:T(8,128)}, u32[]{:S(2)}, u32[]{:S(2)}) collective-permute-start(f32[24,24,768]{2,1,0:T(8,128)} %dynamic-slice_bitcast_fusion.7), channel_id=1, source_target_pairs={{0,16},{16,0},{1,17},{17,1},{2,18},{18,2},{3,19},{19,3},{4,20},{20... | collective-permute-start | bytes 5308424 | tf_op jit(solution)/shard_map/ppermute | solution.py:85
  415.2 40.7 %copy-start.1 = (f32[48,24,768]{2,1,0:T(8,128)S(1)}, f32[48,24,768]{2,1,0:T(8,128)}, u32[]{:S(2)}) copy-start(f32[48,24,768]{2,1,0:T(8,128)} %shard_map.118) | copy-start | bytes 10616836
  416.9 39.0 %collective-permute-start.1 = (f32[24,24,768]{2,1,0:T(8,128)S(1)}, f32[24,24,768]{2,1,0:T(8,128)S(1)}, u32[]{:S(2)}, u32[]{:S(2)}) collective-permute-start(f32[24,24,768]{2,1,0:T(8,128)S(1)} %dynamic-slice_bitcast_fusion.6), channel_id=1, source_target_pairs={{0,16},{16,0},{1,17},{17,1},{2,18},{18,2},{3,19},{19,3},{4,20},{20... | collective-permute-start | bytes 5308424 | tf_op jit(solution)/shard_map/ppermute | solution.py:85
  483.2 124.4 %all-to-all-start.1 = ((f32[16,24,24,96]{3,2,1,0:T(8,128)}), f32[16,24,24,96]{3,2,1,0:T(8,128)}, u32[]{:S(2)}, u32[]{:S(2)}) async-start(f32[16,24,24,96]{3,2,1,0:T(8,128)} %fusion.38), calls=%async_computation.1 | async-start | bytes 9437184 | tf_op jit(solution)/shard_map/all_to_all | solution.py:136
  491.2 39.9 %collective-permute-start.2 = (f32[24,24,768]{2,1,0:T(8,128)S(1)}, f32[24,24,768]{2,1,0:T(8,128)S(1)}, u32[]{:S(2)}, u32[]{:S(2)}) collective-permute-start(f32[24,24,768]{2,1,0:T(8,128)S(1)} %dynamic-slice_bitcast_fusion.5), channel_id=1, source_target_pairs={{0,16},{16,0},{1,17},{17,1},{2,18},{18,2},{3,19},{19,3},{4,20},{20... | collective-permute-start | bytes 5308424 | tf_op jit(solution)/shard_map/ppermute | solution.py:85
  540.1 40.7 %copy-start.2 = (f32[48,24,768]{2,1,0:T(8,128)S(1)}, f32[48,24,768]{2,1,0:T(8,128)}, u32[]{:S(2)}) copy-start(f32[48,24,768]{2,1,0:T(8,128)} %shard_map.119) | copy-start | bytes 10616836
  541.8 39.0 %collective-permute-start.3 = (f32[24,24,768]{2,1,0:T(8,128)S(1)}, f32[24,24,768]{2,1,0:T(8,128)S(1)}, u32[]{:S(2)}, u32[]{:S(2)}) collective-permute-start(f32[24,24,768]{2,1,0:T(8,128)S(1)} %dynamic-slice_bitcast_fusion.4), channel_id=1, source_target_pairs={{0,16},{16,0},{1,17},{17,1},{2,18},{18,2},{3,19},{19,3},{4,20},{20... | collective-permute-start | bytes 5308424 | tf_op jit(solution)/shard_map/ppermute | solution.py:85
  607.6 162.3 %all-to-all-start.3 = ((f32[16,24,24,96]{3,2,1,0:T(8,128)}), f32[16,24,24,96]{3,2,1,0:T(8,128)}, u32[]{:S(2)}, u32[]{:S(2)}) async-start(f32[16,24,24,96]{3,2,1,0:T(8,128)} %fusion.29), calls=%async_computation.3 | async-start | bytes 9437184 | tf_op jit(solution)/shard_map/all_to_all | solution.py:136
  653.4 40.0 %collective-permute-start.4 = (f32[24,24,768]{2,1,0:T(8,128)S(1)}, f32[24,24,768]{2,1,0:T(8,128)S(1)}, u32[]{:S(2)}, u32[]{:S(2)}) collective-permute-start(f32[24,24,768]{2,1,0:T(8,128)S(1)} %dynamic-slice_bitcast_fusion.3), channel_id=1, source_target_pairs={{0,16},{16,0},{1,17},{17,1},{2,18},{18,2},{3,19},{19,3},{4,20},{20... | collective-permute-start | bytes 5308424 | tf_op jit(solution)/shard_map/ppermute | solution.py:85
  702.3 40.8 %copy-start.3 = (f32[48,24,768]{2,1,0:T(8,128)S(1)}, f32[48,24,768]{2,1,0:T(8,128)}, u32[]{:S(2)}) copy-start(f32[48,24,768]{2,1,0:T(8,128)} %shard_map.120) | copy-start | bytes 10616836
  704.1 39.1 %collective-permute-start.5 = (f32[24,24,768]{2,1,0:T(8,128)S(1)}, f32[24,24,768]{2,1,0:T(8,128)S(1)}, u32[]{:S(2)}, u32[]{:S(2)}) collective-permute-start(f32[24,24,768]{2,1,0:T(8,128)S(1)} %dynamic-slice_bitcast_fusion.2), channel_id=1, source_target_pairs={{0,16},{16,0},{1,17},{17,1},{2,18},{18,2},{3,19},{19,3},{4,20},{20... | collective-permute-start | bytes 5308424 | tf_op jit(solution)/shard_map/ppermute | solution.py:85
  770.0 162.3 %all-to-all-start.5 = ((f32[16,24,24,96]{3,2,1,0:T(8,128)}), f32[16,24,24,96]{3,2,1,0:T(8,128)}, u32[]{:S(2)}, u32[]{:S(2)}) async-start(f32[16,24,24,96]{3,2,1,0:T(8,128)} %fusion.32), calls=%async_computation.5 | async-start | bytes 9437184 | tf_op jit(solution)/shard_map/all_to_all | solution.py:136
  815.4 40.0 %collective-permute-start.6 = (f32[24,24,768]{2,1,0:T(8,128)S(1)}, f32[24,24,768]{2,1,0:T(8,128)S(1)}, u32[]{:S(2)}, u32[]{:S(2)}) collective-permute-start(f32[24,24,768]{2,1,0:T(8,128)S(1)} %dynamic-slice_bitcast_fusion.1), channel_id=1, source_target_pairs={{0,16},{16,0},{1,17},{17,1},{2,18},{18,2},{3,19},{19,3},{4,20},{20... | collective-permute-start | bytes 5308424 | tf_op jit(solution)/shard_map/ppermute | solution.py:85
  864.4 40.8 %copy-start = (f32[48,24,768]{2,1,0:T(8,128)S(1)}, f32[48,24,768]{2,1,0:T(8,128)}, u32[]{:S(2)}) copy-start(f32[48,24,768]{2,1,0:T(8,128)} %shard_map.121) | copy-start | bytes 10616836
  866.1 39.1 %collective-permute-start.7 = (f32[24,24,768]{2,1,0:T(8,128)S(1)}, f32[24,24,768]{2,1,0:T(8,128)S(1)}, u32[]{:S(2)}, u32[]{:S(2)}) collective-permute-start(f32[24,24,768]{2,1,0:T(8,128)S(1)} %dynamic-slice_bitcast_fusion), channel_id=1, source_target_pairs={{0,16},{16,0},{1,17},{17,1},{2,18},{18,2},{3,19},{19,3},{4,20},{20... | collective-permute-start | bytes 5308424 | tf_op jit(solution)/shard_map/ppermute | solution.py:85
  932.2 8.1 copy-start.7
  932.2 111.8 %all-to-all-start.7 = ((f32[16,24,24,96]{3,2,1,0:T(8,128)}), f32[16,24,24,96]{3,2,1,0:T(8,128)}, u32[]{:S(2)}, u32[]{:S(2)}) async-start(f32[16,24,24,96]{3,2,1,0:T(8,128)} %fusion.35), calls=%async_computation.7 | async-start | bytes 9437184 | tf_op jit(solution)/shard_map/all_to_all | solution.py:136
  940.3 26.8 %copy-start.6 = (f32[16,24,1536,1]{2,1,3,0:T(8,128)S(1)}, f32[16,24,1536,1]{2,1,3,0:T(8,128)}, u32[]{:S(2)}) copy-start(f32[16,24,1536,1]{2,1,3,0:T(8,128)} %constant.176) | copy-start | bytes 7077892
  967.1 27.3 %copy-start.5 = (f32[16,24,1536,1]{2,1,3,0:T(8,128)S(1)}, f32[16,24,1536,1]{2,1,3,0:T(8,128)}, u32[]{:S(2)}) copy-start(f32[16,24,1536,1]{2,1,3,0:T(8,128)} %constant.180) | copy-start | bytes 7077892
  994.4 49.6 %copy-start.4 = (f32[16,24,1536,1]{2,1,3,0:T(8,128)S(1)}, f32[16,24,1536,1]{2,1,3,0:T(8,128)}, u32[]{:S(2)}) copy-start(f32[16,24,1536,1]{2,1,3,0:T(8,128)} %constant.181) | copy-start | bytes 7077892

commit v8 on v7

--- a/solution.py
+++ b/solution.py
@@ -129,12 +129,12 @@
         solved = vertical_solve(columns, lower_coef, upper_coef, eigen_sum, pinned)
         solved = solved.reshape(row_count, slab_levels, chunk_x, part_y)
         returned = exchange(solved, "row")
-        return jnp.einsum("hzij,hjsy->sziy", returned, inverse_y, precision=highest)
+        return jnp.einsum("hzij,hjsy->sziy", returned, inverse_y, precision=lax.Precision.HIGH)
 
     def back_x(chunk, back_y):
         table_back = cas_constant(chunk_waves(chunk), index_x, full_x).reshape(col_count, chunk_x, full_x)
         scattered = lax.all_to_all(back_y, "col", 0, 0, tiled=True)
-        return jnp.einsum("dziy,din->zyn", scattered, table_back, precision=highest)
+        return jnp.einsum("dziy,din->zyn", scattered, table_back, precision=lax.Precision.HIGH)
 
     lead = min(2, chunks)
     gathered = [lax.all_to_all(spread_x(chunk), "col", 0, 0, tiled=True) for chunk in range(lead)]

time: 1100 us -> 1030 us (0.936)
  matrix products: 500 us -> 396 us
  waiting for transfers between devices: 489 us -> 522 us
    dot_general x8, matrix products: 241 us -> 137 us  [the longest x4 75.7 us: back_x(): jnp.einsum('dziy,din->zyn', scattered, table_back, precision=lax.Precisio...]
    all_to_all x4, waiting for transfers between devices: 22.7 us -> 55.7 us  [back_x(): scattered = lax.all_to_all(back_y, 'col', 0, 0, tiled=True)]
  transfers between devices with their start and end apart: 16 -> 16, of which waited for: 12 -> 12; matrix products, arithmetic and copies ran while one was open for 40% -> 35% of each run, Pallas kernels for 2% -> 3%
where the time goes in v8:
time: 1030 us
  waiting for transfers between devices  522 us (51%)
  matrix products  396 us (38%)
  starting transfers between devices  58.3 us (6%)
  Pallas kernels  26.1 us (3%)
  other arithmetic  14.2 us (1%)
    ppermute x8, waiting for transfers between devices, exchange(): arrived.append(lax.ppermute(outgoing, axis_name, perm))  312 us
    dot_general x4, matrix products, spectra_y(): return jnp.einsum('sziy,syhj->hzij', gathered, forward_y, precision=highest)  149 us
    all_to_all x2, waiting for transfers between devices, body(): lax.all_to_all(spread_x(chunk), 'col', 0, 0, tiled=True)  115 us
    dot_general x4, matrix products, spread_x(): return jnp.einsum('zyx,xdi->dziy', source, table_chunk, precision=highest)  109 us
    dot_general x4, matrix products, back_x(): jnp.einsum('dziy,din->zyn', scattered, table_back, precision=lax.Precisio...  75.7 us
    dot_general x4, matrix products, middle(): jnp.einsum('hzij,hjsy->sziy', returned, inverse_y, precision=lax.Precisio...  61.1 us
    all_to_all x4, waiting for transfers between devices, back_x(): scattered = lax.all_to_all(back_y, 'col', 0, 0, tiled=True)  55.7 us
    all_to_all x2, waiting for transfers between devices, body(): gathered.append(lax.all_to_all(spread, 'col', 0, 0, tiled=True))  39.8 us
  transfers between devices with their start and end apart: 16, of which 12 were waited for; matrix products, arithmetic and copies ran while one was open for 35% of the time, Pallas kernels for 3%

profile of v8, /device:TPU:15, one launch (start us, length us, event | category | flops | bytes accessed | tf_op | source)
XLA Modules:
  0.0 1027.7 jit_solution(14010835629058824147)
XLA Ops:
  0.0 27.8 %fusion.42 = f32[16,24,24,96]{3,2,1,0:T(8,128)} fusion(f32[1536,16,24,1]{0,2,3,1:T(8,128)} %constant.173, f32[24,96,1536]{2,1,0:T(8,128)} %param.12), kind=kOutput, calls=%fused_computation.45 | convolution fusion | flops 16307453952 | bytes 20054016 | tf_op jit(solution)/shard_map/zyx,xdi->dziy/dot_general | solution.py:118
  34.9 27.2 %fusion.48 = f32[16,24,24,96]{3,2,1,0:T(8,128)} fusion(f32[1536,16,24,1]{0,2,3,1:T(8,128)S(1)} %copy-done.10, f32[24,96,1536]{2,1,0:T(8,128)} %param.12), kind=kOutput, calls=%fused_computation.47 | convolution fusion | flops 16307453952 | bytes 20054016 | tf_op jit(solution)/shard_map/zyx,xdi->dziy/dot_general | solution.py:118
  62.0 76.4 %all-to-all-done = f32[16,24,24,96]{3,2,1,0:T(8,128)} async-done(((f32[16,24,24,96]{3,2,1,0:T(8,128)}), f32[16,24,24,96]{3,2,1,0:T(8,128)}, u32[]{:S(2)}, u32[]{:S(2)}) %all-to-all-start) | async-done | bytes 3538976 | tf_op jit(solution)/shard_map/all_to_all | solution.py:140
  143.9 27.2 %fusion.39 = f32[16,24,24,96]{3,2,1,0:T(8,128)} fusion(f32[1536,16,24,1]{0,2,3,1:T(8,128)S(1)} %copy-done.9, f32[24,96,1536]{2,1,0:T(8,128)} %param.12), kind=kOutput, calls=%fused_computation.44 | convolution fusion | flops 16307453952 | bytes 20054016 | tf_op jit(solution)/shard_map/zyx,xdi->dziy/dot_general | solution.py:118
  171.2 37.9 %fusion.51 = f32[2,24,24,768]{3,2,0,1:T(8,128)} fusion(f32[16,96,2,768,1]{3,1,0,2,4:T(8,128)S(1)} %bitcast.286, f32[16,24,24,96]{3,2,1,0:T(8,128)} %all-to-all-done), kind=kOutput, calls=%fused_computation.48 | convolution fusion | flops 16307453952 | bytes 16515072 | tf_op jit(solution)/shard_map/sziy,syhj->hzij/dot_general | solution.py:121
  209.0 38.4 %all-to-all-done.2 = f32[16,24,24,96]{3,2,1,0:T(8,128)} async-done(((f32[16,24,24,96]{3,2,1,0:T(8,128)}), f32[16,24,24,96]{3,2,1,0:T(8,128)}, u32[]{:S(2)}, u32[]{:S(2)}) %all-to-all-start.2) | async-done | bytes 3538976 | tf_op jit(solution)/shard_map/all_to_all | solution.py:140
  252.6 27.2 %fusion.45 = f32[16,24,24,96]{3,2,1,0:T(8,128)} fusion(f32[1536,16,24,1]{0,2,3,1:T(8,128)S(1)} %copy-done.8, f32[24,96,1536]{2,1,0:T(8,128)} %param.12), kind=kOutput, calls=%fused_computation.46 | convolution fusion | flops 16307453952 | bytes 20054016 | tf_op jit(solution)/shard_map/zyx,xdi->dziy/dot_general | solution.py:118
  279.8 36.6 %fusion.54 = f32[2,24,24,768]{3,2,0,1:T(8,128)S(1)} fusion(f32[16,96,2,768,1]{3,1,0,2,4:T(8,128)} %constant.174, f32[16,24,24,96]{3,2,1,0:T(8,128)} %all-to-all-done.2), kind=kOutput, calls=%fused_computation.49 | convolution fusion | flops 16307453952 | bytes 16515072 | tf_op jit(solution)/shard_map/sziy,syhj->hzij/dot_general | solution.py:121
  316.4 39.8 %all-to-all-done.4 = f32[16,24,24,96]{3,2,1,0:T(8,128)} async-done(((f32[16,24,24,96]{3,2,1,0:T(8,128)}), f32[16,24,24,96]{3,2,1,0:T(8,128)}, u32[]{:S(2)}, u32[]{:S(2)}) %all-to-all-start.4) | async-done | bytes 3538976 | tf_op jit(solution)/shard_map/all_to_all | solution.py:146
  366.3 38.1 %collective-permute-done = f32[24,24,768]{2,1,0:T(8,128)} collective-permute-done((f32[24,24,768]{2,1,0:T(8,128)}, f32[24,24,768]{2,1,0:T(8,128)}, u32[]{:S(2)}, u32[]{:S(2)}) %collective-permute-start) | collective-permute-done | bytes 1769504 | tf_op jit(solution)/shard_map/ppermute | solution.py:85
  417.3 38.7 %collective-permute-done.1 = f32[24,24,768]{2,1,0:T(8,128)S(1)} collective-permute-done((f32[24,24,768]{2,1,0:T(8,128)S(1)}, f32[24,24,768]{2,1,0:T(8,128)S(1)}, u32[]{:S(2)}, u32[]{:S(2)}) %collective-permute-start.1) | collective-permute-done | bytes 1769504 | tf_op jit(solution)/shard_map/ppermute | solution.py:85
  456.2 15.2 %fusion.38 = f32[16,24,24,96]{3,2,1,0:T(8,128)} fusion(f32[2,768,16,96,1]{1,3,0,4,2:T(8,128)} %constant.175, f32[1,24,24,768]{3,2,0,1:T(8,128)S(1)} %get-tuple-element.18, f32[1,24,24,768]{3,2,0,1:T(8,128)S(1)} %get-tuple-element.17), kind=kOutput, calls=%fused_computation.43 | convolution fusion | flops 8154611712 | bytes 16515072 | tf_op jit(solution)/shard_map/hzij,hjsy->sziy/dot_general | solution.py:132
  471.4 8.2 all-to-all-start.1
  480.0 39.6 %collective-permute-done.2 = f32[24,24,768]{2,1,0:T(8,128)S(1)} collective-permute-done((f32[24,24,768]{2,1,0:T(8,128)S(1)}, f32[24,24,768]{2,1,0:T(8,128)S(1)}, u32[]{:S(2)}, u32[]{:S(2)}) %collective-permute-start.2) | collective-permute-done | bytes 1769504 | tf_op jit(solution)/shard_map/ppermute | solution.py:85
  530.6 38.6 %collective-permute-done.3 = f32[24,24,768]{2,1,0:T(8,128)S(1)} collective-permute-done((f32[24,24,768]{2,1,0:T(8,128)S(1)}, f32[24,24,768]{2,1,0:T(8,128)S(1)}, u32[]{:S(2)}, u32[]{:S(2)}) %collective-permute-start.3) | collective-permute-done | bytes 1769504 | tf_op jit(solution)/shard_map/ppermute | solution.py:85
  569.5 15.2 %fusion.29 = f32[16,24,24,96]{3,2,1,0:T(8,128)} fusion(f32[2,768,16,96,1]{1,3,0,4,2:T(8,128)} %constant.175, f32[1,24,24,768]{3,2,1,0:T(8,128)S(1)} %get-tuple-element.22, f32[1,24,24,768]{3,2,1,0:T(8,128)S(1)} %get-tuple-element.21), kind=kOutput, calls=%fused_computation.40 | convolution fusion | flops 8154611712 | bytes 16515072 | tf_op jit(solution)/shard_map/hzij,hjsy->sziy/dot_general | solution.py:132
  584.7 8.5 all-to-all-start.3
  593.3 37.5 %fusion.57 = f32[24,24,2,768]{3,1,2,0:T(8,128)S(1)} fusion(f32[16,96,2,768,1]{3,1,0,2,4:T(8,128)} %constant.174, f32[16,24,24,96]{3,2,1,0:T(8,128)} %all-to-all-done.4), kind=kOutput, calls=%fused_computation.50 | convolution fusion | flops 16307453952 | bytes 16515072 | tf_op jit(solution)/shard_map/sziy,syhj->hzij/dot_general | solution.py:121
  631.3 39.7 %collective-permute-done.4 = f32[24,24,768]{2,1,0:T(8,128)S(1)} collective-permute-done((f32[24,24,768]{2,1,0:T(8,128)S(1)}, f32[24,24,768]{2,1,0:T(8,128)S(1)}, u32[]{:S(2)}, u32[]{:S(2)}) %collective-permute-start.4) | collective-permute-done | bytes 1769504 | tf_op jit(solution)/shard_map/ppermute | solution.py:85
  681.9 38.8 %collective-permute-done.5 = f32[24,24,768]{2,1,0:T(8,128)S(1)} collective-permute-done((f32[24,24,768]{2,1,0:T(8,128)S(1)}, f32[24,24,768]{2,1,0:T(8,128)S(1)}, u32[]{:S(2)}, u32[]{:S(2)}) %collective-permute-start.5) | collective-permute-done | bytes 1769504 | tf_op jit(solution)/shard_map/ppermute | solution.py:85
  720.9 15.3 %fusion.32 = f32[16,24,24,96]{3,2,1,0:T(8,128)} fusion(f32[2,768,16,96,1]{1,3,0,4,2:T(8,128)} %constant.175, f32[1,24,24,768]{3,2,1,0:T(8,128)S(1)} %get-tuple-element.26, f32[1,24,24,768]{3,2,1,0:T(8,128)S(1)} %get-tuple-element.25), kind=kOutput, calls=%fused_computation.41 | convolution fusion | flops 8154611712 | bytes 16515072 | tf_op jit(solution)/shard_map/hzij,hjsy->sziy/dot_general | solution.py:132
  736.3 8.0 all-to-all-start.5
  744.3 37.5 %fusion.60 = f32[24,24,2,768]{3,1,2,0:T(8,128)S(1)} fusion(f32[16,96,2,768,1]{3,1,0,2,4:T(8,128)} %constant.174, f32[16,24,24,96]{3,2,1,0:T(8,128)} %all-to-all-done.6), kind=kOutput, calls=%fused_computation.51 | convolution fusion | flops 16307453952 | bytes 16515072 | tf_op jit(solution)/shard_map/sziy,syhj->hzij/dot_general | solution.py:121
  782.2 39.7 %collective-permute-done.6 = f32[24,24,768]{2,1,0:T(8,128)S(1)} collective-permute-done((f32[24,24,768]{2,1,0:T(8,128)S(1)}, f32[24,24,768]{2,1,0:T(8,128)S(1)}, u32[]{:S(2)}, u32[]{:S(2)}) %collective-permute-start.6) | collective-permute-done | bytes 1769504 | tf_op jit(solution)/shard_map/ppermute | solution.py:85
  832.9 38.8 %collective-permute-done.7 = f32[24,24,768]{2,1,0:T(8,128)S(1)} collective-permute-done((f32[24,24,768]{2,1,0:T(8,128)S(1)}, f32[24,24,768]{2,1,0:T(8,128)S(1)}, u32[]{:S(2)}, u32[]{:S(2)}) %collective-permute-start.7) | collective-permute-done | bytes 1769504 | tf_op jit(solution)/shard_map/ppermute | solution.py:85
  872.0 15.5 %fusion.35 = f32[16,24,24,96]{3,2,1,0:T(8,128)} fusion(f32[2,768,16,96,1]{1,3,0,4,2:T(8,128)} %constant.175, f32[1,24,24,768]{3,2,1,0:T(8,128)S(1)} %get-tuple-element.14, f32[1,24,24,768]{3,2,1,0:T(8,128)S(1)} %get-tuple-element.13), kind=kOutput, calls=%fused_computation.42 | convolution fusion | flops 8154611712 | bytes 16515072 | tf_op jit(solution)/shard_map/hzij,hjsy->sziy/dot_general | solution.py:132
  887.4 8.2 all-to-all-start.7
  895.7 15.9 %fusion.86 = f32[24,96,1536,1]{2,1,0,3:T(8,128)} fusion(f32[16,24,24,96]{3,2,1,0:T(8,128)} %all-to-all-done.3, f32[16,24,1536,1]{2,1,3,0:T(8,128)S(1)} %copy-done.7), kind=kOutput, calls=%fused_computation.117 | convolution fusion | flops 8153726976 | bytes 20054016 | tf_op jit(solution)/shard_map/dziy,din->zyn/dot_general | solution.py:137
  911.6 15.8 %fusion.85 = f32[24,96,1536,1]{2,1,0,3:T(8,128)} fusion(f32[16,24,24,96]{3,2,1,0:T(8,128)} %all-to-all-done.1, f32[16,24,1536,1]{2,1,3,0:T(8,128)S(1)} %copy-done.6), kind=kOutput, calls=%fused_computation.116 | convolution fusion | flops 8153726976 | bytes 20054016 | tf_op jit(solution)/shard_map/dziy,din->zyn/dot_general | solution.py:137
  927.3 16.2 %fusion.87 = f32[24,96,1536,1]{2,1,0,3:T(8,128)} fusion(f32[16,24,24,96]{3,2,1,0:T(8,128)} %all-to-all-done.5, f32[16,24,1536,1]{2,1,3,0:T(8,128)S(1)} %copy-done.5), kind=kOutput, calls=%fused_computation.118 | convolution fusion | flops 8153726976 | bytes 20054016 | tf_op jit(solution)/shard_map/dziy,din->zyn/dot_general | solution.py:137
  943.5 55.7 %all-to-all-done.7 = f32[16,24,24,96]{3,2,1,0:T(8,128)} async-done(((f32[16,24,24,96]{3,2,1,0:T(8,128)}), f32[16,24,24,96]{3,2,1,0:T(8,128)}, u32[]{:S(2)}, u32[]{:S(2)}) %all-to-all-start.7) | async-done | bytes 3538976 | tf_op jit(solution)/shard_map/all_to_all | solution.py:136
  999.2 27.9 %fusion = f32[24,96,1536]{2,1,0:T(8,128)} fusion(f32[24,96,1536,1]{2,1,0,3:T(8,128)} %fusion.87, f32[24,96,1536,1]{2,1,0,3:T(8,128)} %fusion.86, f32[24,96,1536,1]{2,1,0,3:T(8,128)} %fusion.85, f32[16,24,24,96]{3,2,1,0:T(8,128)} %all-to-all-done.7, f32[16,24,1536,1]{2,1,3,0:T(8,128)S(1)} %copy-done.4), kind=kOutput, calls=%fused_computation.1 | convolution fusion | flops 8167882752 | bytes 62521344 | tf_op jit(solution)/shard_map/dziy,din->zyn/dot_general | solution.py:137
  (77 shorter events, 75.9 us)
Async XLA Ops:
  27.8 7.1 copy-start.10
  27.8 110.6 %all-to-all-start = ((f32[16,24,24,96]{3,2,1,0:T(8,128)}), f32[16,24,24,96]{3,2,1,0:T(8,128)}, u32[]{:S(2)}, u32[]{:S(2)}) async-start(f32[16,24,24,96]{3,2,1,0:T(8,128)} %fusion.42), calls=%async_computation | async-start | bytes 9437184 | tf_op jit(solution)/shard_map/all_to_all | solution.py:140
  62.0 81.8 %copy-start.9 = (f32[1536,16,24,1]{0,2,3,1:T(8,128)S(1)}, f32[1536,16,24,1]{0,2,3,1:T(8,128)}, u32[]{:S(2)}) copy-start(f32[1536,16,24,1]{0,2,3,1:T(8,128)} %constant.172) | copy-start | bytes 7077892
  138.4 32.7 %slice-start = ((s8[9437184]{0:T(1024)(128)(4,1)}), s8[1048576]{0:T(1024)(128)(4,1)S(1)}, s32[]{:S(2)}) async-start(s8[9437184]{0:T(1024)(128)(4,1)} %bitcast.285), calls=%async_computation.8 | async-start | bytes 2097152
  138.4 109.0 %all-to-all-start.2 = ((f32[16,24,24,96]{3,2,1,0:T(8,128)}), f32[16,24,24,96]{3,2,1,0:T(8,128)}, u32[]{:S(2)}, u32[]{:S(2)}) async-start(f32[16,24,24,96]{3,2,1,0:T(8,128)} %fusion.48), calls=%async_computation.2 | async-start | bytes 9437184 | tf_op jit(solution)/shard_map/all_to_all | solution.py:140
  143.9 27.3 %slice-start.1 = ((s8[9437184]{0:T(1024)(128)(4,1)}), s8[4194304]{0:T(1024)(128)(4,1)S(1)}, s32[]{:S(2)}) async-start(s8[9437184]{0:T(1024)(128)(4,1)} %bitcast.285), calls=%async_computation.9 | async-start | bytes 8388608
  143.9 27.3 %slice-start.2 = ((s8[9437184]{0:T(1024)(128)(4,1)}), s8[4194304]{0:T(1024)(128)(4,1)S(1)}, s32[]{:S(2)}) async-start(s8[9437184]{0:T(1024)(128)(4,1)} %bitcast.285), calls=%async_computation.10 | async-start | bytes 8388608
  209.0 43.6 %copy-start.8 = (f32[1536,16,24,1]{0,2,3,1:T(8,128)S(1)}, f32[1536,16,24,1]{0,2,3,1:T(8,128)}, u32[]{:S(2)}) copy-start(f32[1536,16,24,1]{0,2,3,1:T(8,128)} %constant.177) | copy-start | bytes 7077892
  247.4 108.8 %all-to-all-start.4 = ((f32[16,24,24,96]{3,2,1,0:T(8,128)}), f32[16,24,24,96]{3,2,1,0:T(8,128)}, u32[]{:S(2)}, u32[]{:S(2)}) async-start(f32[16,24,24,96]{3,2,1,0:T(8,128)} %fusion.39), calls=%async_computation.4 | async-start | bytes 9437184 | tf_op jit(solution)/shard_map/all_to_all | solution.py:146
  356.2 115.2 %all-to-all-start.6 = ((f32[16,24,24,96]{3,2,1,0:T(8,128)}), f32[16,24,24,96]{3,2,1,0:T(8,128)}, u32[]{:S(2)}, u32[]{:S(2)}) async-start(f32[16,24,24,96]{3,2,1,0:T(8,128)} %fusion.45), calls=%async_computation.6 | async-start | bytes 9437184 | tf_op jit(solution)/shard_map/all_to_all | solution.py:146
  364.3 40.1 %collective-permute-start = (f32[24,24,768]{2,1,0:T(8,128)}, f32[24,24,768]{2,1,0:T(8,128)}, u32[]{:S(2)}, u32[]{:S(2)}) collective-permute-start(f32[24,24,768]{2,1,0:T(8,128)} %dynamic-slice_bitcast_fusion.7), channel_id=1, source_target_pairs={{0,16},{16,0},{1,17},{17,1},{2,18},{18,2},{3,19},{19,3},{4,20},{20... | collective-permute-start | bytes 5308424 | tf_op jit(solution)/shard_map/ppermute | solution.py:85
  415.2 40.7 %copy-start.1 = (f32[48,24,768]{2,1,0:T(8,128)S(1)}, f32[48,24,768]{2,1,0:T(8,128)}, u32[]{:S(2)}) copy-start(f32[48,24,768]{2,1,0:T(8,128)} %shard_map.118) | copy-start | bytes 10616836
  417.0 39.0 %collective-permute-start.1 = (f32[24,24,768]{2,1,0:T(8,128)S(1)}, f32[24,24,768]{2,1,0:T(8,128)S(1)}, u32[]{:S(2)}, u32[]{:S(2)}) collective-permute-start(f32[24,24,768]{2,1,0:T(8,128)S(1)} %dynamic-slice_bitcast_fusion.6), channel_id=1, source_target_pairs={{0,16},{16,0},{1,17},{17,1},{2,18},{18,2},{3,19},{19,3},{4,20},{20... | collective-permute-start | bytes 5308424 | tf_op jit(solution)/shard_map/ppermute | solution.py:85
  471.4 113.4 %all-to-all-start.1 = ((f32[16,24,24,96]{3,2,1,0:T(8,128)}), f32[16,24,24,96]{3,2,1,0:T(8,128)}, u32[]{:S(2)}, u32[]{:S(2)}) async-start(f32[16,24,24,96]{3,2,1,0:T(8,128)} %fusion.38), calls=%async_computation.1 | async-start | bytes 9437184 | tf_op jit(solution)/shard_map/all_to_all | solution.py:136
  479.7 39.9 %collective-permute-start.2 = (f32[24,24,768]{2,1,0:T(8,128)S(1)}, f32[24,24,768]{2,1,0:T(8,128)S(1)}, u32[]{:S(2)}, u32[]{:S(2)}) collective-permute-start(f32[24,24,768]{2,1,0:T(8,128)S(1)} %dynamic-slice_bitcast_fusion.5), channel_id=1, source_target_pairs={{0,16},{16,0},{1,17},{17,1},{2,18},{18,2},{3,19},{19,3},{4,20},{20... | collective-permute-start | bytes 5308424 | tf_op jit(solution)/shard_map/ppermute | solution.py:85
  528.6 40.7 %copy-start.2 = (f32[48,24,768]{2,1,0:T(8,128)S(1)}, f32[48,24,768]{2,1,0:T(8,128)}, u32[]{:S(2)}) copy-start(f32[48,24,768]{2,1,0:T(8,128)} %shard_map.119) | copy-start | bytes 10616836
  530.3 39.0 %collective-permute-start.3 = (f32[24,24,768]{2,1,0:T(8,128)S(1)}, f32[24,24,768]{2,1,0:T(8,128)S(1)}, u32[]{:S(2)}, u32[]{:S(2)}) collective-permute-start(f32[24,24,768]{2,1,0:T(8,128)S(1)} %dynamic-slice_bitcast_fusion.4), channel_id=1, source_target_pairs={{0,16},{16,0},{1,17},{17,1},{2,18},{18,2},{3,19},{19,3},{4,20},{20... | collective-permute-start | bytes 5308424 | tf_op jit(solution)/shard_map/ppermute | solution.py:85
  584.7 151.5 %all-to-all-start.3 = ((f32[16,24,24,96]{3,2,1,0:T(8,128)}), f32[16,24,24,96]{3,2,1,0:T(8,128)}, u32[]{:S(2)}, u32[]{:S(2)}) async-start(f32[16,24,24,96]{3,2,1,0:T(8,128)} %fusion.29), calls=%async_computation.3 | async-start | bytes 9437184 | tf_op jit(solution)/shard_map/all_to_all | solution.py:136
  630.9 40.0 %collective-permute-start.4 = (f32[24,24,768]{2,1,0:T(8,128)S(1)}, f32[24,24,768]{2,1,0:T(8,128)S(1)}, u32[]{:S(2)}, u32[]{:S(2)}) collective-permute-start(f32[24,24,768]{2,1,0:T(8,128)S(1)} %dynamic-slice_bitcast_fusion.3), channel_id=1, source_target_pairs={{0,16},{16,0},{1,17},{17,1},{2,18},{18,2},{3,19},{19,3},{4,20},{20... | collective-permute-start | bytes 5308424 | tf_op jit(solution)/shard_map/ppermute | solution.py:85
  679.8 40.8 %copy-start.3 = (f32[48,24,768]{2,1,0:T(8,128)S(1)}, f32[48,24,768]{2,1,0:T(8,128)}, u32[]{:S(2)}) copy-start(f32[48,24,768]{2,1,0:T(8,128)} %shard_map.120) | copy-start | bytes 10616836
  681.6 39.1 %collective-permute-start.5 = (f32[24,24,768]{2,1,0:T(8,128)S(1)}, f32[24,24,768]{2,1,0:T(8,128)S(1)}, u32[]{:S(2)}, u32[]{:S(2)}) collective-permute-start(f32[24,24,768]{2,1,0:T(8,128)S(1)} %dynamic-slice_bitcast_fusion.2), channel_id=1, source_target_pairs={{0,16},{16,0},{1,17},{17,1},{2,18},{18,2},{3,19},{19,3},{4,20},{20... | collective-permute-start | bytes 5308424 | tf_op jit(solution)/shard_map/ppermute | solution.py:85
  736.3 151.2 %all-to-all-start.5 = ((f32[16,24,24,96]{3,2,1,0:T(8,128)}), f32[16,24,24,96]{3,2,1,0:T(8,128)}, u32[]{:S(2)}, u32[]{:S(2)}) async-start(f32[16,24,24,96]{3,2,1,0:T(8,128)} %fusion.32), calls=%async_computation.5 | async-start | bytes 9437184 | tf_op jit(solution)/shard_map/all_to_all | solution.py:136
  781.9 40.0 %collective-permute-start.6 = (f32[24,24,768]{2,1,0:T(8,128)S(1)}, f32[24,24,768]{2,1,0:T(8,128)S(1)}, u32[]{:S(2)}, u32[]{:S(2)}) collective-permute-start(f32[24,24,768]{2,1,0:T(8,128)S(1)} %dynamic-slice_bitcast_fusion.1), channel_id=1, source_target_pairs={{0,16},{16,0},{1,17},{17,1},{2,18},{18,2},{3,19},{19,3},{4,20},{20... | collective-permute-start | bytes 5308424 | tf_op jit(solution)/shard_map/ppermute | solution.py:85
  830.9 40.8 %copy-start = (f32[48,24,768]{2,1,0:T(8,128)S(1)}, f32[48,24,768]{2,1,0:T(8,128)}, u32[]{:S(2)}) copy-start(f32[48,24,768]{2,1,0:T(8,128)} %shard_map.121) | copy-start | bytes 10616836
  832.6 39.1 %collective-permute-start.7 = (f32[24,24,768]{2,1,0:T(8,128)S(1)}, f32[24,24,768]{2,1,0:T(8,128)S(1)}, u32[]{:S(2)}, u32[]{:S(2)}) collective-permute-start(f32[24,24,768]{2,1,0:T(8,128)S(1)} %dynamic-slice_bitcast_fusion), channel_id=1, source_target_pairs={{0,16},{16,0},{1,17},{17,1},{2,18},{18,2},{3,19},{19,3},{4,20},{20... | collective-permute-start | bytes 5308424 | tf_op jit(solution)/shard_map/ppermute | solution.py:85
  887.4 8.2 copy-start.7
  887.4 111.8 %all-to-all-start.7 = ((f32[16,24,24,96]{3,2,1,0:T(8,128)}), f32[16,24,24,96]{3,2,1,0:T(8,128)}, u32[]{:S(2)}, u32[]{:S(2)}) async-start(f32[16,24,24,96]{3,2,1,0:T(8,128)} %fusion.35), calls=%async_computation.7 | async-start | bytes 9437184 | tf_op jit(solution)/shard_map/all_to_all | solution.py:136
  895.7 15.9 %copy-start.6 = (f32[16,24,1536,1]{2,1,3,0:T(8,128)S(1)}, f32[16,24,1536,1]{2,1,3,0:T(8,128)}, u32[]{:S(2)}) copy-start(f32[16,24,1536,1]{2,1,3,0:T(8,128)} %constant.176) | copy-start | bytes 7077892
  911.6 15.8 %copy-start.5 = (f32[16,24,1536,1]{2,1,3,0:T(8,128)S(1)}, f32[16,24,1536,1]{2,1,3,0:T(8,128)}, u32[]{:S(2)}) copy-start(f32[16,24,1536,1]{2,1,3,0:T(8,128)} %constant.180) | copy-start | bytes 7077892
  927.3 71.9 %copy-start.4 = (f32[16,24,1536,1]{2,1,3,0:T(8,128)S(1)}, f32[16,24,1536,1]{2,1,3,0:T(8,128)}, u32[]{:S(2)}) copy-start(f32[16,24,1536,1]{2,1,3,0:T(8,128)} %constant.181) | copy-start | bytes 7077892

commit v9 on v8

--- a/solution.py
+++ b/solution.py
@@ -93,7 +93,7 @@
     return jnp.stack(placed)
 
 
-def body(source, lower_coef, upper_coef, chunks=4):
+def body(source, lower_coef, upper_coef, chunks=6):
     highest = lax.Precision.HIGHEST
     slab_levels, slab_rows, full_x = source.shape
     col_count = lax.axis_size("col")

time: 1030 us -> 1060 us (1.029)
  waiting for transfers between devices: 522 us -> 479 us
  starting transfers between devices: 58.3 us -> 84.1 us
  matrix products: 396 us -> 414 us
  local copies, waits for them, and re-layouts: 10.2 us -> 25.3 us
    all_to_all x2, waiting for transfers between devices: 115 us -> 72.5 us  [body(): lax.all_to_all(spread_x(chunk), 'col', 0, 0, tiled=True)]
    all_to_all x4 -> x6, waiting for transfers between devices: 55.7 us -> 38.2 us  [back_x(): scattered = lax.all_to_all(back_y, 'col', 0, 0, tiled=True)]
    all_to_all x4 -> x6, starting transfers between devices: 33 us -> 47.8 us  [back_x(): scattered = lax.all_to_all(back_y, 'col', 0, 0, tiled=True)]
    dot_general x4 -> x6, matrix products: 149 us -> 136 us  [spectra_y(): return jnp.einsum('sziy,syhj->hzij', gathered, forward_y, precision=highest)]
    dot_general x4 -> x6, matrix products: 109 us -> 122 us  [spread_x(): return jnp.einsum('zyx,xdi->dziy', source, table_chunk, precision=highest)]
    all_to_all x2 -> x4, waiting for transfers between devices: 39.8 us -> 52.3 us  [body(): gathered.append(lax.all_to_all(spread, 'col', 0, 0, tiled=True))]
    dot_general x4 -> x6, matrix products: 75.7 us -> 87.5 us  [back_x(): jnp.einsum('dziy,din->zyn', scattered, table_back, precision=lax.Precisio...]
    dot_general x4 -> x6, matrix products: 61.1 us -> 67.8 us  [middle(): jnp.einsum('hzij,hjsy->sziy', returned, inverse_y, precision=lax.Precisio...]
  transfers between devices with their start and end apart: 16 -> 24, of which waited for: 12 -> 18; matrix products, arithmetic and copies ran while one was open for 35% -> 37% of each run, Pallas kernels for 3% -> 3%
where the time goes in v9:
time: 1060 us; the launch traced here: 1050 us
  waiting for transfers between devices  479 us (45%)
  matrix products  414 us (39%)
  starting transfers between devices  84.1 us (8%)
  Pallas kernels  28.8 us (3%)
  local copies, waits for them, and re-layouts  25.3 us (2%)
  other arithmetic  15.8 us (1%)
    ppermute x12, waiting for transfers between devices, exchange(): arrived.append(lax.ppermute(outgoing, axis_name, perm))  316 us
    dot_general x6, matrix products, spectra_y(): return jnp.einsum('sziy,syhj->hzij', gathered, forward_y, precision=highest)  136 us
    dot_general x6, matrix products, spread_x(): return jnp.einsum('zyx,xdi->dziy', source, table_chunk, precision=highest)  122 us
    dot_general x6, matrix products, back_x(): jnp.einsum('dziy,din->zyn', scattered, table_back, precision=lax.Precisio...  87.5 us
    all_to_all x2, waiting for transfers between devices, body(): lax.all_to_all(spread_x(chunk), 'col', 0, 0, tiled=True)  72.5 us
    dot_general x6, matrix products, middle(): jnp.einsum('hzij,hjsy->sziy', returned, inverse_y, precision=lax.Precisio...  67.8 us
    all_to_all x4, waiting for transfers between devices, body(): gathered.append(lax.all_to_all(spread, 'col', 0, 0, tiled=True))  52.3 us
    all_to_all x6, starting transfers between devices, back_x(): scattered = lax.all_to_all(back_y, 'col', 0, 0, tiled=True)  47.8 us
  transfers between devices with their start and end apart: 24, of which 18 were waited for; matrix products, arithmetic and copies ran while one was open for 37% of the time, Pallas kernels for 3%

profile of v9, /device:TPU:15, one launch (start us, length us, event | category | flops | bytes accessed | tf_op | source)
XLA Modules:
  0.0 1047.9 jit_solution(703667001740218008)
XLA Ops:
  0.0 20.2 %fusion.62 = f32[16,24,16,96]{3,2,1,0:T(8,128)} fusion(f32[1536,16,16,1]{0,2,3,1:T(8,128)} %constant.235, f32[24,96,1536]{2,1,0:T(8,128)} %param.16), kind=kOutput, calls=%fused_computation.67 | convolution fusion | flops 10871635968 | bytes 18087936 | tf_op jit(solution)/shard_map/zyx,xdi->dziy/dot_general | solution.py:118
  26.8 20.2 %fusion.68 = f32[16,24,16,96]{3,2,1,0:T(8,128)} fusion(f32[1536,16,16,1]{0,2,3,1:T(8,128)} %constant.240, f32[24,96,1536]{2,1,0:T(8,128)} %param.16), kind=kOutput, calls=%fused_computation.69 | convolution fusion | flops 10871635968 | bytes 18087936 | tf_op jit(solution)/shard_map/zyx,xdi->dziy/dot_general | solution.py:118
  47.0 49.6 %all-to-all-done = f32[16,24,16,96]{3,2,1,0:T(8,128)S(1)} async-done(((f32[16,24,16,96]{3,2,1,0:T(8,128)}), f32[16,24,16,96]{3,2,1,0:T(8,128)S(1)}, u32[]{:S(2)}, u32[]{:S(2)}) %all-to-all-start) | async-done | bytes 2359328 | tf_op jit(solution)/shard_map/all_to_all | solution.py:140
  103.9 20.4 %fusion.59 = f32[16,24,16,96]{3,2,1,0:T(8,128)} fusion(f32[1536,16,16,1]{0,2,3,1:T(8,128)} %constant.234, f32[24,96,1536]{2,1,0:T(8,128)} %param.16), kind=kOutput, calls=%fused_computation.66 | convolution fusion | flops 10871635968 | bytes 18087936 | tf_op jit(solution)/shard_map/zyx,xdi->dziy/dot_general | solution.py:118
  124.3 26.5 %fusion.77 = f32[2,24,16,768]{3,2,0,1:T(8,128)} fusion(f32[16,96,2,768,1]{3,1,0,2,4:T(8,128)} %constant.236, f32[16,24,16,96]{3,2,1,0:T(8,128)S(1)} %copy-done.15), kind=kOutput, calls=%fused_computation.72 | convolution fusion | flops 10871635968 | bytes 14155776 | tf_op jit(solution)/shard_map/sziy,syhj->hzij/dot_general | solution.py:121
  150.7 22.9 %all-to-all-done.2 = f32[16,24,16,96]{3,2,1,0:T(8,128)S(1)} async-done(((f32[16,24,16,96]{3,2,1,0:T(8,128)}), f32[16,24,16,96]{3,2,1,0:T(8,128)S(1)}, u32[]{:S(2)}, u32[]{:S(2)}) %all-to-all-start.2) | async-done | bytes 2359328 | tf_op jit(solution)/shard_map/all_to_all | solution.py:140
  180.5 20.4 %fusion.65 = f32[16,24,16,96]{3,2,1,0:T(8,128)} fusion(f32[1536,16,16,1]{0,2,3,1:T(8,128)} %constant.239, f32[24,96,1536]{2,1,0:T(8,128)} %param.16), kind=kOutput, calls=%fused_computation.68 | convolution fusion | flops 10871635968 | bytes 18087936 | tf_op jit(solution)/shard_map/zyx,xdi->dziy/dot_general | solution.py:118
  200.9 26.5 %fusion.80 = f32[2,24,16,768]{3,2,0,1:T(8,128)} fusion(f32[16,96,2,768,1]{3,1,0,2,4:T(8,128)} %constant.236, f32[16,24,16,96]{3,2,1,0:T(8,128)S(1)} %copy-done.13), kind=kOutput, calls=%fused_computation.73 | convolution fusion | flops 10871635968 | bytes 14155776 | tf_op jit(solution)/shard_map/sziy,syhj->hzij/dot_general | solution.py:121
  227.3 22.9 %all-to-all-done.4 = f32[16,24,16,96]{3,2,1,0:T(8,128)S(1)} async-done(((f32[16,24,16,96]{3,2,1,0:T(8,128)}), f32[16,24,16,96]{3,2,1,0:T(8,128)S(1)}, u32[]{:S(2)}, u32[]{:S(2)}) %all-to-all-start.4) | async-done | bytes 2359328 | tf_op jit(solution)/shard_map/all_to_all | solution.py:146
  261.0 25.1 %collective-permute-done = f32[24,16,768]{2,1,0:T(8,128)} collective-permute-done((f32[24,16,768]{2,1,0:T(8,128)S(1)}, f32[24,16,768]{2,1,0:T(8,128)}, u32[]{:S(2)}, u32[]{:S(2)}) %collective-permute-start) | collective-permute-done | bytes 1179680 | tf_op jit(solution)/shard_map/ppermute | solution.py:85
  295.8 26.0 %collective-permute-done.1 = f32[24,16,768]{2,1,0:T(8,128)S(1)} collective-permute-done((f32[24,16,768]{2,1,0:T(8,128)S(1)}, f32[24,16,768]{2,1,0:T(8,128)S(1)}, u32[]{:S(2)}, u32[]{:S(2)}) %collective-permute-start.1) | collective-permute-done | bytes 1179680 | tf_op jit(solution)/shard_map/ppermute | solution.py:85
  343.0 26.9 %collective-permute-done.2 = f32[24,16,768]{2,1,0:T(8,128)S(1)} collective-permute-done((f32[24,16,768]{2,1,0:T(8,128)S(1)}, f32[24,16,768]{2,1,0:T(8,128)S(1)}, u32[]{:S(2)}, u32[]{:S(2)}) %collective-permute-start.2) | collective-permute-done | bytes 1179680 | tf_op jit(solution)/shard_map/ppermute | solution.py:85
  378.4 26.0 %collective-permute-done.3 = f32[24,16,768]{2,1,0:T(8,128)S(1)} collective-permute-done((f32[24,16,768]{2,1,0:T(8,128)S(1)}, f32[24,16,768]{2,1,0:T(8,128)S(1)}, u32[]{:S(2)}, u32[]{:S(2)}) %collective-permute-start.3) | collective-permute-done | bytes 1179680 | tf_op jit(solution)/shard_map/ppermute | solution.py:85
  426.1 20.4 %fusion.71 = f32[16,24,16,96]{3,2,1,0:T(8,128)} fusion(f32[1536,16,16,1]{0,2,3,1:T(8,128)} %constant.242, f32[24,96,1536]{2,1,0:T(8,128)} %param.16), kind=kOutput, calls=%fused_computation.70 | convolution fusion | flops 10871635968 | bytes 18087936 | tf_op jit(solution)/shard_map/zyx,xdi->dziy/dot_general | solution.py:118
  446.5 26.5 %fusion.83 = f32[2,24,16,768]{3,2,0,1:T(8,128)} fusion(f32[16,96,2,768,1]{3,1,0,2,4:T(8,128)} %constant.236, f32[16,24,16,96]{3,2,1,0:T(8,128)S(1)} %copy-done.9), kind=kOutput, calls=%fused_computation.74 | convolution fusion | flops 10871635968 | bytes 14155776 | tf_op jit(solution)/shard_map/sziy,syhj->hzij/dot_general | solution.py:121
  472.9 23.0 %all-to-all-done.3 = f32[16,24,16,96]{3,2,1,0:T(8,128)} async-done(((f32[16,24,16,96]{3,2,1,0:T(8,128)}), f32[16,24,16,96]{3,2,1,0:T(8,128)}, u32[]{:S(2)}, u32[]{:S(2)}) %all-to-all-start.3) | async-done | bytes 2359328 | tf_op jit(solution)/shard_map/all_to_all | solution.py:136
  500.8 20.3 %fusion.74 = f32[16,24,16,96]{3,2,1,0:T(8,128)} fusion(f32[1536,16,16,1]{0,2,3,1:T(8,128)} %constant.244, f32[24,96,1536]{2,1,0:T(8,128)} %param.16), kind=kOutput, calls=%fused_computation.71 | convolution fusion | flops 10871635968 | bytes 18087936 | tf_op jit(solution)/shard_map/zyx,xdi->dziy/dot_general | solution.py:118
  521.1 20.3 %fusion.86 = f32[2,24,16,768]{3,2,0,1:T(8,128)} fusion(f32[16,96,2,768,1]{3,1,0,2,4:T(8,128)} %constant.236, f32[16,24,16,96]{3,2,1,0:T(8,128)} %all-to-all-done.6), kind=kOutput, calls=%fused_computation.75 | convolution fusion | flops 10871635968 | bytes 14155776 | tf_op jit(solution)/shard_map/sziy,syhj->hzij/dot_general | solution.py:121
  541.3 29.3 %all-to-all-done.8 = f32[16,24,16,96]{3,2,1,0:T(8,128)S(1)} async-done(((f32[16,24,16,96]{3,2,1,0:T(8,128)}), f32[16,24,16,96]{3,2,1,0:T(8,128)S(1)}, u32[]{:S(2)}, u32[]{:S(2)}) %all-to-all-start.8) | async-done | bytes 2359328 | tf_op jit(solution)/shard_map/all_to_all | solution.py:146
  579.4 26.9 %collective-permute-done.4 = f32[24,16,768]{2,1,0:T(8,128)S(1)} collective-permute-done((f32[24,16,768]{2,1,0:T(8,128)S(1)}, f32[24,16,768]{2,1,0:T(8,128)S(1)}, u32[]{:S(2)}, u32[]{:S(2)}) %collective-permute-start.4) | collective-permute-done | bytes 1179680 | tf_op jit(solution)/shard_map/ppermute | solution.py:85
  614.8 26.0 %collective-permute-done.5 = f32[24,16,768]{2,1,0:T(8,128)S(1)} collective-permute-done((f32[24,16,768]{2,1,0:T(8,128)S(1)}, f32[24,16,768]{2,1,0:T(8,128)S(1)}, u32[]{:S(2)}, u32[]{:S(2)}) %collective-permute-start.5) | collective-permute-done | bytes 1179680 | tf_op jit(solution)/shard_map/ppermute | solution.py:85
  663.6 26.9 %collective-permute-done.6 = f32[24,16,768]{2,1,0:T(8,128)S(1)} collective-permute-done((f32[24,16,768]{2,1,0:T(8,128)S(1)}, f32[24,16,768]{2,1,0:T(8,128)S(1)}, u32[]{:S(2)}, u32[]{:S(2)}) %collective-permute-start.6) | collective-permute-done | bytes 1179680 | tf_op jit(solution)/shard_map/ppermute | solution.py:85
  699.2 26.0 %collective-permute-done.7 = f32[24,16,768]{2,1,0:T(8,128)S(1)} collective-permute-done((f32[24,16,768]{2,1,0:T(8,128)S(1)}, f32[24,16,768]{2,1,0:T(8,128)S(1)}, u32[]{:S(2)}, u32[]{:S(2)}) %collective-permute-start.7) | collective-permute-done | bytes 1179680 | tf_op jit(solution)/shard_map/ppermute | solution.py:85
  745.1 18.4 %fusion.89 = f32[24,16,2,768]{3,1,2,0:T(8,128)S(1)} fusion(f32[16,96,2,768,1]{3,1,0,2,4:T(8,128)} %constant.236, f32[16,24,16,96]{3,2,1,0:T(8,128)} %copy-done.11), kind=kOutput, calls=%fused_computation.76 | convolution fusion | flops 10871635968 | bytes 14155776 | tf_op jit(solution)/shard_map/sziy,syhj->hzij/dot_general | solution.py:121
  763.9 27.1 %collective-permute-done.8 = f32[24,16,768]{2,1,0:T(8,128)S(1)} collective-permute-done((f32[24,16,768]{2,1,0:T(8,128)S(1)}, f32[24,16,768]{2,1,0:T(8,128)S(1)}, u32[]{:S(2)}, u32[]{:S(2)}) %collective-permute-start.8) | collective-permute-done | bytes 1179680 | tf_op jit(solution)/shard_map/ppermute | solution.py:85
  799.4 26.1 %collective-permute-done.9 = f32[24,16,768]{2,1,0:T(8,128)S(1)} collective-permute-done((f32[24,16,768]{2,1,0:T(8,128)S(1)}, f32[24,16,768]{2,1,0:T(8,128)S(1)}, u32[]{:S(2)}, u32[]{:S(2)}) %collective-permute-start.9) | collective-permute-done | bytes 1179680 | tf_op jit(solution)/shard_map/ppermute | solution.py:85
  845.1 18.4 %fusion.92 = f32[24,16,2,768]{3,1,2,0:T(8,128)S(1)} fusion(f32[16,96,2,768,1]{3,1,0,2,4:T(8,128)} %constant.236, f32[16,24,16,96]{3,2,1,0:T(8,128)} %copy-done.10), kind=kOutput, calls=%fused_computation.77 | convolution fusion | flops 10871635968 | bytes 14155776 | tf_op jit(solution)/shard_map/sziy,syhj->hzij/dot_general | solution.py:121
  863.9 27.1 %collective-permute-done.10 = f32[24,16,768]{2,1,0:T(8,128)S(1)} collective-permute-done((f32[24,16,768]{2,1,0:T(8,128)S(1)}, f32[24,16,768]{2,1,0:T(8,128)S(1)}, u32[]{:S(2)}, u32[]{:S(2)}) %collective-permute-start.10) | collective-permute-done | bytes 1179680 | tf_op jit(solution)/shard_map/ppermute | solution.py:85
  899.4 26.1 %collective-permute-done.11 = f32[24,16,768]{2,1,0:T(8,128)S(1)} collective-permute-done((f32[24,16,768]{2,1,0:T(8,128)S(1)}, f32[24,16,768]{2,1,0:T(8,128)S(1)}, u32[]{:S(2)}, u32[]{:S(2)}) %collective-permute-start.11) | collective-permute-done | bytes 1179680 | tf_op jit(solution)/shard_map/ppermute | solution.py:85
  965.5 12.4 %fusion.130 = f32[24,96,1536,1]{2,1,0,3:T(8,128)} fusion(f32[16,24,16,96]{3,2,1,0:T(8,128)} %all-to-all-done.7, f32[16,16,1536,1]{2,1,3,0:T(8,128)S(1)} %copy-done.22), kind=kOutput, calls=%fused_computation.175 | convolution fusion | flops 5435817984 | bytes 18087936 | tf_op jit(solution)/shard_map/dziy,din->zyn/dot_general | solution.py:137
  999.6 15.2 %all-to-all-done.11 = f32[16,24,16,96]{3,2,1,0:T(8,128)} async-done(((f32[16,24,16,96]{3,2,1,0:T(8,128)}), f32[16,24,16,96]{3,2,1,0:T(8,128)}, u32[]{:S(2)}, u32[]{:S(2)}) %all-to-all-start.11) | async-done | bytes 2359328 | tf_op jit(solution)/shard_map/all_to_all | solution.py:136
  1014.8 32.7 %fusion = f32[24,96,1536]{2,1,0:T(8,128)} fusion(f32[24,96,1536,1]{2,1,0,3:T(8,128)} %fusion.131, f32[24,96,1536,1]{2,1,0,3:T(8,128)} %fusion.130, f32[24,96,1536,1]{2,1,0,3:T(8,128)} %fusion.129, f32[24,96,1536,1]{2,1,0,3:T(8,128)} %fusion.128, f32[24,96,1536,1]{2,1,0,3:T(8,128)} %fusion.127, f32[16,24,16,96]{3,2,1,0:T(8,128)} %all-to-all-done.11, ...), kind=kOutput, calls=%fused_computation.1 | convolution fusion | flops 5457051648 | bytes 88866816 | tf_op jit(solution)/shard_map/dziy,din->zyn/dot_general | solution.py:137
  (136 shorter events, 264.3 us)
Async XLA Ops:
  20.2 76.4 %all-to-all-start = ((f32[16,24,16,96]{3,2,1,0:T(8,128)}), f32[16,24,16,96]{3,2,1,0:T(8,128)S(1)}, u32[]{:S(2)}, u32[]{:S(2)}) async-start(f32[16,24,16,96]{3,2,1,0:T(8,128)} %fusion.62), calls=%async_computation | async-start | bytes 6291456 | tf_op jit(solution)/shard_map/all_to_all | solution.py:140
  98.4 75.3 %all-to-all-start.2 = ((f32[16,24,16,96]{3,2,1,0:T(8,128)}), f32[16,24,16,96]{3,2,1,0:T(8,128)S(1)}, u32[]{:S(2)}, u32[]{:S(2)}) async-start(f32[16,24,16,96]{3,2,1,0:T(8,128)} %fusion.68), calls=%async_computation.2 | async-start | bytes 6291456 | tf_op jit(solution)/shard_map/all_to_all | solution.py:140
  175.3 75.0 %all-to-all-start.4 = ((f32[16,24,16,96]{3,2,1,0:T(8,128)}), f32[16,24,16,96]{3,2,1,0:T(8,128)S(1)}, u32[]{:S(2)}, u32[]{:S(2)}) async-start(f32[16,24,16,96]{3,2,1,0:T(8,128)} %fusion.59), calls=%async_computation.4 | async-start | bytes 6291456 | tf_op jit(solution)/shard_map/all_to_all | solution.py:146
  252.0 81.4 %all-to-all-start.6 = ((f32[16,24,16,96]{3,2,1,0:T(8,128)}), f32[16,24,16,96]{3,2,1,0:T(8,128)}, u32[]{:S(2)}, u32[]{:S(2)}) async-start(f32[16,24,16,96]{3,2,1,0:T(8,128)} %fusion.65), calls=%async_computation.6 | async-start | bytes 6291456 | tf_op jit(solution)/shard_map/all_to_all | solution.py:146
  257.2 28.9 %copy-start.17 = (f32[2,24,16,768]{3,2,0,1:T(8,128)S(1)}, f32[2,24,16,768]{3,2,0,1:T(8,128)}, u32[]{:S(2)}) copy-start(f32[2,24,16,768]{3,2,0,1:T(8,128)} %fusion.77) | copy-start | bytes 7077892
  258.8 27.4 %collective-permute-start = (f32[24,16,768]{2,1,0:T(8,128)S(1)}, f32[24,16,768]{2,1,0:T(8,128)}, u32[]{:S(2)}, u32[]{:S(2)}) collective-permute-start(f32[24,16,768]{2,1,0:T(8,128)S(1)} %dynamic-slice_bitcast_fusion.11), channel_id=1, source_target_pairs={{0,16},{16,0},{1,17},{17,1},{2,18},{18,2},{3,19},{19,3},{4,20},{20... | collective-permute-start | bytes 3538952 | tf_op jit(solution)/shard_map/ppermute | solution.py:85
  294.0 27.8 %copy-start.3 = (f32[48,16,768]{2,1,0:T(8,128)S(1)}, f32[48,16,768]{2,1,0:T(8,128)}, u32[]{:S(2)}) copy-start(f32[48,16,768]{2,1,0:T(8,128)} %shard_map.154) | copy-start | bytes 7077892
  295.5 26.3 %collective-permute-start.1 = (f32[24,16,768]{2,1,0:T(8,128)S(1)}, f32[24,16,768]{2,1,0:T(8,128)S(1)}, u32[]{:S(2)}, u32[]{:S(2)}) collective-permute-start(f32[24,16,768]{2,1,0:T(8,128)S(1)} %dynamic-slice_bitcast_fusion.10), channel_id=1, source_target_pairs={{0,16},{16,0},{1,17},{17,1},{2,18},{18,2},{3,19},{19,3},{4,20},{20... | collective-permute-start | bytes 3538952 | tf_op jit(solution)/shard_map/ppermute | solution.py:85
  333.4 82.7 %all-to-all-start.1 = ((f32[16,24,16,96]{3,2,1,0:T(8,128)}), f32[16,24,16,96]{3,2,1,0:T(8,128)S(1)}, u32[]{:S(2)}, u32[]{:S(2)}) async-start(f32[16,24,16,96]{3,2,1,0:T(8,128)} %fusion.58), calls=%async_computation.1 | async-start | bytes 6291456 | tf_op jit(solution)/shard_map/all_to_all | solution.py:136
  341.2 28.8 %copy-start.16 = (f32[2,24,16,768]{3,2,0,1:T(8,128)S(1)}, f32[2,24,16,768]{3,2,0,1:T(8,128)}, u32[]{:S(2)}) copy-start(f32[2,24,16,768]{3,2,0,1:T(8,128)} %fusion.80) | copy-start | bytes 7077892
  342.7 27.3 %collective-permute-start.2 = (f32[24,16,768]{2,1,0:T(8,128)S(1)}, f32[24,16,768]{2,1,0:T(8,128)S(1)}, u32[]{:S(2)}, u32[]{:S(2)}) collective-permute-start(f32[24,16,768]{2,1,0:T(8,128)S(1)} %dynamic-slice_bitcast_fusion.9), channel_id=1, source_target_pairs={{0,16},{16,0},{1,17},{17,1},{2,18},{18,2},{3,19},{19,3},{4,20},{20... | collective-permute-start | bytes 3538952 | tf_op jit(solution)/shard_map/ppermute | solution.py:85
  378.1 26.3 %collective-permute-start.3 = (f32[24,16,768]{2,1,0:T(8,128)S(1)}, f32[24,16,768]{2,1,0:T(8,128)S(1)}, u32[]{:S(2)}, u32[]{:S(2)}) collective-permute-start(f32[24,16,768]{2,1,0:T(8,128)S(1)} %dynamic-slice_bitcast_fusion.8), channel_id=1, source_target_pairs={{0,16},{16,0},{1,17},{17,1},{2,18},{18,2},{3,19},{19,3},{4,20},{20... | collective-permute-start | bytes 3538952 | tf_op jit(solution)/shard_map/ppermute | solution.py:85
  417.7 78.2 %all-to-all-start.3 = ((f32[16,24,16,96]{3,2,1,0:T(8,128)}), f32[16,24,16,96]{3,2,1,0:T(8,128)}, u32[]{:S(2)}, u32[]{:S(2)}) async-start(f32[16,24,16,96]{3,2,1,0:T(8,128)} %fusion.43), calls=%async_computation.3 | async-start | bytes 6291456 | tf_op jit(solution)/shard_map/all_to_all | solution.py:136
  495.9 74.8 %all-to-all-start.8 = ((f32[16,24,16,96]{3,2,1,0:T(8,128)}), f32[16,24,16,96]{3,2,1,0:T(8,128)S(1)}, u32[]{:S(2)}, u32[]{:S(2)}) async-start(f32[16,24,16,96]{3,2,1,0:T(8,128)} %fusion.71), calls=%async_computation.8 | async-start | bytes 6291456 | tf_op jit(solution)/shard_map/all_to_all | solution.py:146
  572.4 80.0 %all-to-all-start.10 = ((f32[16,24,16,96]{3,2,1,0:T(8,128)}), f32[16,24,16,96]{3,2,1,0:T(8,128)S(1)}, u32[]{:S(2)}, u32[]{:S(2)}) async-start(f32[16,24,16,96]{3,2,1,0:T(8,128)} %fusion.74), calls=%async_computation.10 | async-start | bytes 6291456 | tf_op jit(solution)/shard_map/all_to_all | solution.py:146
  577.6 28.8 %copy-start.19 = (f32[2,24,16,768]{3,2,0,1:T(8,128)S(1)}, f32[2,24,16,768]{3,2,0,1:T(8,128)}, u32[]{:S(2)}) copy-start(f32[2,24,16,768]{3,2,0,1:T(8,128)} %fusion.83) | copy-start | bytes 7077892
  579.1 27.3 %collective-permute-start.4 = (f32[24,16,768]{2,1,0:T(8,128)S(1)}, f32[24,16,768]{2,1,0:T(8,128)S(1)}, u32[]{:S(2)}, u32[]{:S(2)}) collective-permute-start(f32[24,16,768]{2,1,0:T(8,128)S(1)} %dynamic-slice_bitcast_fusion.7), channel_id=1, source_target_pairs={{0,16},{16,0},{1,17},{17,1},{2,18},{18,2},{3,19},{19,3},{4,20},{20... | collective-permute-start | bytes 3538952 | tf_op jit(solution)/shard_map/ppermute | solution.py:85
  613.0 27.8 %copy-start.5 = (f32[48,16,768]{2,1,0:T(8,128)S(1)}, f32[48,16,768]{2,1,0:T(8,128)}, u32[]{:S(2)}) copy-start(f32[48,16,768]{2,1,0:T(8,128)} %shard_map.156) | copy-start | bytes 7077892
  614.5 26.3 %collective-permute-start.5 = (f32[24,16,768]{2,1,0:T(8,128)S(1)}, f32[24,16,768]{2,1,0:T(8,128)S(1)}, u32[]{:S(2)}, u32[]{:S(2)}) collective-permute-start(f32[24,16,768]{2,1,0:T(8,128)S(1)} %dynamic-slice_bitcast_fusion.6), channel_id=1, source_target_pairs={{0,16},{16,0},{1,17},{17,1},{2,18},{18,2},{3,19},{19,3},{4,20},{20... | collective-permute-start | bytes 3538952 | tf_op jit(solution)/shard_map/ppermute | solution.py:85
  654.0 82.7 %all-to-all-start.5 = ((f32[16,24,16,96]{3,2,1,0:T(8,128)}), f32[16,24,16,96]{3,2,1,0:T(8,128)S(1)}, u32[]{:S(2)}, u32[]{:S(2)}) async-start(f32[16,24,16,96]{3,2,1,0:T(8,128)} %fusion.46), calls=%async_computation.5 | async-start | bytes 6291456 | tf_op jit(solution)/shard_map/all_to_all | solution.py:136
  661.8 28.8 %copy-start.18 = (f32[2,24,16,768]{3,2,0,1:T(8,128)S(1)}, f32[2,24,16,768]{3,2,0,1:T(8,128)}, u32[]{:S(2)}) copy-start(f32[2,24,16,768]{3,2,0,1:T(8,128)} %fusion.86) | copy-start | bytes 7077892
  663.3 27.3 %collective-permute-start.6 = (f32[24,16,768]{2,1,0:T(8,128)S(1)}, f32[24,16,768]{2,1,0:T(8,128)S(1)}, u32[]{:S(2)}, u32[]{:S(2)}) collective-permute-start(f32[24,16,768]{2,1,0:T(8,128)S(1)} %dynamic-slice_bitcast_fusion.5), channel_id=1, source_target_pairs={{0,16},{16,0},{1,17},{17,1},{2,18},{18,2},{3,19},{19,3},{4,20},{20... | collective-permute-start | bytes 3538952 | tf_op jit(solution)/shard_map/ppermute | solution.py:85
  698.8 26.3 %collective-permute-start.7 = (f32[24,16,768]{2,1,0:T(8,128)S(1)}, f32[24,16,768]{2,1,0:T(8,128)S(1)}, u32[]{:S(2)}, u32[]{:S(2)}) collective-permute-start(f32[24,16,768]{2,1,0:T(8,128)S(1)} %dynamic-slice_bitcast_fusion.4), channel_id=1, source_target_pairs={{0,16},{16,0},{1,17},{17,1},{2,18},{18,2},{3,19},{19,3},{4,20},{20... | collective-permute-start | bytes 3538952 | tf_op jit(solution)/shard_map/ppermute | solution.py:85
  736.8 100.4 %all-to-all-start.7 = ((f32[16,24,16,96]{3,2,1,0:T(8,128)}), f32[16,24,16,96]{3,2,1,0:T(8,128)}, u32[]{:S(2)}, u32[]{:S(2)}) async-start(f32[16,24,16,96]{3,2,1,0:T(8,128)} %fusion.49), calls=%async_computation.7 | async-start | bytes 6291456 | tf_op jit(solution)/shard_map/all_to_all | solution.py:136
  763.6 27.4 %collective-permute-start.8 = (f32[24,16,768]{2,1,0:T(8,128)S(1)}, f32[24,16,768]{2,1,0:T(8,128)S(1)}, u32[]{:S(2)}, u32[]{:S(2)}) collective-permute-start(f32[24,16,768]{2,1,0:T(8,128)S(1)} %dynamic-slice_bitcast_fusion.3), channel_id=1, source_target_pairs={{0,16},{16,0},{1,17},{17,1},{2,18},{18,2},{3,19},{19,3},{4,20},{20... | collective-permute-start | bytes 3538952 | tf_op jit(solution)/shard_map/ppermute | solution.py:85
  797.6 27.9 %copy-start.7 = (f32[48,16,768]{2,1,0:T(8,128)S(1)}, f32[48,16,768]{2,1,0:T(8,128)}, u32[]{:S(2)}) copy-start(f32[48,16,768]{2,1,0:T(8,128)} %shard_map.158) | copy-start | bytes 7077892
  799.1 26.4 %collective-permute-start.9 = (f32[24,16,768]{2,1,0:T(8,128)S(1)}, f32[24,16,768]{2,1,0:T(8,128)S(1)}, u32[]{:S(2)}, u32[]{:S(2)}) collective-permute-start(f32[24,16,768]{2,1,0:T(8,128)S(1)} %dynamic-slice_bitcast_fusion.2), channel_id=1, source_target_pairs={{0,16},{16,0},{1,17},{17,1},{2,18},{18,2},{3,19},{19,3},{4,20},{20... | collective-permute-start | bytes 3538952 | tf_op jit(solution)/shard_map/ppermute | solution.py:85
  837.1 100.0 %all-to-all-start.9 = ((f32[16,24,16,96]{3,2,1,0:T(8,128)}), f32[16,24,16,96]{3,2,1,0:T(8,128)}, u32[]{:S(2)}, u32[]{:S(2)}) async-start(f32[16,24,16,96]{3,2,1,0:T(8,128)} %fusion.52), calls=%async_computation.9 | async-start | bytes 6291456 | tf_op jit(solution)/shard_map/all_to_all | solution.py:136
  863.6 27.4 %collective-permute-start.10 = (f32[24,16,768]{2,1,0:T(8,128)S(1)}, f32[24,16,768]{2,1,0:T(8,128)S(1)}, u32[]{:S(2)}, u32[]{:S(2)}) collective-permute-start(f32[24,16,768]{2,1,0:T(8,128)S(1)} %dynamic-slice_bitcast_fusion.1), channel_id=1, source_target_pairs={{0,16},{16,0},{1,17},{17,1},{2,18},{18,2},{3,19},{19,3},{4,20},{20... | collective-permute-start | bytes 3538952 | tf_op jit(solution)/shard_map/ppermute | solution.py:85
  897.6 27.9 %copy-start.2 = (f32[48,16,768]{2,1,0:T(8,128)S(1)}, f32[48,16,768]{2,1,0:T(8,128)}, u32[]{:S(2)}) copy-start(f32[48,16,768]{2,1,0:T(8,128)} %shard_map.159) | copy-start | bytes 7077892
  899.1 26.4 %collective-permute-start.11 = (f32[24,16,768]{2,1,0:T(8,128)S(1)}, f32[24,16,768]{2,1,0:T(8,128)S(1)}, u32[]{:S(2)}, u32[]{:S(2)}) collective-permute-start(f32[24,16,768]{2,1,0:T(8,128)S(1)} %dynamic-slice_bitcast_fusion), channel_id=1, source_target_pairs={{0,16},{16,0},{1,17},{17,1},{2,18},{18,2},{3,19},{19,3},{4,20},{20... | collective-permute-start | bytes 3538952 | tf_op jit(solution)/shard_map/ppermute | solution.py:85
  937.1 77.7 %all-to-all-start.11 = ((f32[16,24,16,96]{3,2,1,0:T(8,128)}), f32[16,24,16,96]{3,2,1,0:T(8,128)}, u32[]{:S(2)}, u32[]{:S(2)}) async-start(f32[16,24,16,96]{3,2,1,0:T(8,128)} %fusion.55), calls=%async_computation.11 | async-start | bytes 6291456 | tf_op jit(solution)/shard_map/all_to_all | solution.py:136
  (17 other events, 208.2 us)

commit v10 on v8

--- a/solution.py
+++ b/solution.py
@@ -146,6 +146,8 @@
             gathered.append(lax.all_to_all(spread, "col", 0, 0, tiled=True))
         part = back_x(chunk, middle(chunk, spectra))
         pressure = part if pressure is None else pressure + part
+        if chunk + 1 < chunks:
+            pressure = lax.optimization_barrier(pressure)
     return pressure * scale
 
 

time: 1030 us -> 1030 us (level)
  transfers between devices with their start and end apart: 16 -> 16, of which waited for: 12 -> 12; matrix products, arithmetic and copies ran while one was open for 35% -> 36% of each run, Pallas kernels for 3% -> 3%
where the time goes in v10:
time: 1030 us; the launch traced here: 1020 us
  waiting for transfers between devices  521 us (51%)
  matrix products  388 us (38%)
  starting transfers between devices  58.9 us (6%)
  Pallas kernels  25.9 us (3%)
  other arithmetic  14 us (1%)
    ppermute x8, waiting for transfers between devices, exchange(): arrived.append(lax.ppermute(outgoing, axis_name, perm))  312 us
    dot_general x4, matrix products, spectra_y(): return jnp.einsum('sziy,syhj->hzij', gathered, forward_y, precision=highest)  149 us
    all_to_all x2, waiting for transfers between devices, body(): lax.all_to_all(spread_x(chunk), 'col', 0, 0, tiled=True)  115 us
    dot_general x4, matrix products, spread_x(): return jnp.einsum('zyx,xdi->dziy', source, table_chunk, precision=highest)  109 us
    dot_general x4, matrix products, back_x(): jnp.einsum('dziy,din->zyn', scattered, table_back, precision=lax.Precisio...  68.5 us
    dot_general x4, matrix products, middle(): jnp.einsum('hzij,hjsy->sziy', returned, inverse_y, precision=lax.Precisio...  61.2 us
    all_to_all x4, waiting for transfers between devices, back_x(): scattered = lax.all_to_all(back_y, 'col', 0, 0, tiled=True)  54.3 us
    all_to_all x2, waiting for transfers between devices, body(): gathered.append(lax.all_to_all(spread, 'col', 0, 0, tiled=True))  39.8 us
  transfers between devices with their start and end apart: 16, of which 12 were waited for; matrix products, arithmetic and copies ran while one was open for 36% of the time, Pallas kernels for 3%

profile of v10, /device:TPU:15, one launch (start us, length us, event | category | flops | bytes accessed | tf_op | source)
XLA Modules:
  0.0 1018.9 jit_solution(1017331797426608736)
XLA Ops:
  0.0 27.8 %fusion.42 = f32[16,24,24,96]{3,2,1,0:T(8,128)} fusion(f32[1536,16,24,1]{0,2,3,1:T(8,128)} %constant.173, f32[24,96,1536]{2,1,0:T(8,128)} %param.12), kind=kOutput, calls=%fused_computation.46 | convolution fusion | flops 16307453952 | bytes 20054016 | tf_op jit(solution)/shard_map/zyx,xdi->dziy/dot_general | solution.py:118
  35.0 27.1 %fusion.48 = f32[16,24,24,96]{3,2,1,0:T(8,128)} fusion(f32[1536,16,24,1]{0,2,3,1:T(8,128)S(1)} %copy-done.7, f32[24,96,1536]{2,1,0:T(8,128)} %param.12), kind=kOutput, calls=%fused_computation.48 | convolution fusion | flops 16307453952 | bytes 20054016 | tf_op jit(solution)/shard_map/zyx,xdi->dziy/dot_general | solution.py:118
  62.1 76.4 %all-to-all-done = f32[16,24,24,96]{3,2,1,0:T(8,128)} async-done(((f32[16,24,24,96]{3,2,1,0:T(8,128)}), f32[16,24,24,96]{3,2,1,0:T(8,128)}, u32[]{:S(2)}, u32[]{:S(2)}) %all-to-all-start) | async-done | bytes 3538976 | tf_op jit(solution)/shard_map/all_to_all | solution.py:140
  144.2 27.2 %fusion.39 = f32[16,24,24,96]{3,2,1,0:T(8,128)} fusion(f32[1536,16,24,1]{0,2,3,1:T(8,128)S(1)} %copy-done.6, f32[24,96,1536]{2,1,0:T(8,128)} %param.12), kind=kOutput, calls=%fused_computation.45 | convolution fusion | flops 16307453952 | bytes 20054016 | tf_op jit(solution)/shard_map/zyx,xdi->dziy/dot_general | solution.py:118
  171.5 37.6 %fusion.51 = f32[2,24,24,768]{3,2,0,1:T(8,128)} fusion(f32[16,96,2,768,1]{3,1,0,2,4:T(8,128)S(1)} %bitcast.282, f32[16,24,24,96]{3,2,1,0:T(8,128)} %all-to-all-done), kind=kOutput, calls=%fused_computation.49 | convolution fusion | flops 16307453952 | bytes 16515072 | tf_op jit(solution)/shard_map/sziy,syhj->hzij/dot_general | solution.py:121
  209.1 38.7 %all-to-all-done.2 = f32[16,24,24,96]{3,2,1,0:T(8,128)} async-done(((f32[16,24,24,96]{3,2,1,0:T(8,128)}), f32[16,24,24,96]{3,2,1,0:T(8,128)}, u32[]{:S(2)}, u32[]{:S(2)}) %all-to-all-start.2) | async-done | bytes 3538976 | tf_op jit(solution)/shard_map/all_to_all | solution.py:140
  253.0 27.1 %fusion.45 = f32[16,24,24,96]{3,2,1,0:T(8,128)} fusion(f32[1536,16,24,1]{0,2,3,1:T(8,128)S(1)} %copy-done.5, f32[24,96,1536]{2,1,0:T(8,128)} %param.12), kind=kOutput, calls=%fused_computation.47 | convolution fusion | flops 16307453952 | bytes 20054016 | tf_op jit(solution)/shard_map/zyx,xdi->dziy/dot_general | solution.py:118
  280.2 36.6 %fusion.54 = f32[2,24,24,768]{3,2,0,1:T(8,128)S(1)} fusion(f32[16,96,2,768,1]{3,1,0,2,4:T(8,128)} %constant.174, f32[16,24,24,96]{3,2,1,0:T(8,128)} %all-to-all-done.2), kind=kOutput, calls=%fused_computation.50 | convolution fusion | flops 16307453952 | bytes 16515072 | tf_op jit(solution)/shard_map/sziy,syhj->hzij/dot_general | solution.py:121
  316.8 39.8 %all-to-all-done.4 = f32[16,24,24,96]{3,2,1,0:T(8,128)} async-done(((f32[16,24,24,96]{3,2,1,0:T(8,128)}), f32[16,24,24,96]{3,2,1,0:T(8,128)}, u32[]{:S(2)}, u32[]{:S(2)}) %all-to-all-start.4) | async-done | bytes 3538976 | tf_op jit(solution)/shard_map/all_to_all | solution.py:146
  366.8 38.1 %collective-permute-done = f32[24,24,768]{2,1,0:T(8,128)} collective-permute-done((f32[24,24,768]{2,1,0:T(8,128)}, f32[24,24,768]{2,1,0:T(8,128)}, u32[]{:S(2)}, u32[]{:S(2)}) %collective-permute-start) | collective-permute-done | bytes 1769504 | tf_op jit(solution)/shard_map/ppermute | solution.py:85
  417.7 38.7 %collective-permute-done.1 = f32[24,24,768]{2,1,0:T(8,128)S(1)} collective-permute-done((f32[24,24,768]{2,1,0:T(8,128)S(1)}, f32[24,24,768]{2,1,0:T(8,128)S(1)}, u32[]{:S(2)}, u32[]{:S(2)}) %collective-permute-start.1) | collective-permute-done | bytes 1769504 | tf_op jit(solution)/shard_map/ppermute | solution.py:85
  456.6 15.2 %fusion.38 = f32[16,24,24,96]{3,2,1,0:T(8,128)} fusion(f32[2,768,16,96,1]{1,3,0,4,2:T(8,128)} %constant.175, f32[1,24,24,768]{3,2,0,1:T(8,128)S(1)} %get-tuple-element.26, f32[1,24,24,768]{3,2,0,1:T(8,128)S(1)} %get-tuple-element.25), kind=kOutput, calls=%fused_computation.44 | convolution fusion | flops 8154611712 | bytes 16515072 | tf_op jit(solution)/shard_map/hzij,hjsy->sziy/dot_general | solution.py:132
  471.8 8.4 all-to-all-start.1
  480.7 39.6 %collective-permute-done.2 = f32[24,24,768]{2,1,0:T(8,128)S(1)} collective-permute-done((f32[24,24,768]{2,1,0:T(8,128)S(1)}, f32[24,24,768]{2,1,0:T(8,128)S(1)}, u32[]{:S(2)}, u32[]{:S(2)}) %collective-permute-start.2) | collective-permute-done | bytes 1769504 | tf_op jit(solution)/shard_map/ppermute | solution.py:85
  531.1 38.6 %collective-permute-done.3 = f32[24,24,768]{2,1,0:T(8,128)S(1)} collective-permute-done((f32[24,24,768]{2,1,0:T(8,128)S(1)}, f32[24,24,768]{2,1,0:T(8,128)S(1)}, u32[]{:S(2)}, u32[]{:S(2)}) %collective-permute-start.3) | collective-permute-done | bytes 1769504 | tf_op jit(solution)/shard_map/ppermute | solution.py:85
  570.0 15.2 %fusion.29 = f32[16,24,24,96]{3,2,1,0:T(8,128)} fusion(f32[2,768,16,96,1]{1,3,0,4,2:T(8,128)} %constant.175, f32[1,24,24,768]{3,2,1,0:T(8,128)S(1)} %get-tuple-element.22, f32[1,24,24,768]{3,2,1,0:T(8,128)S(1)} %get-tuple-element.21), kind=kOutput, calls=%fused_computation.41 | convolution fusion | flops 8154611712 | bytes 16515072 | tf_op jit(solution)/shard_map/hzij,hjsy->sziy/dot_general | solution.py:132
  585.2 8.2 all-to-all-start.3
  593.4 37.5 %fusion.57 = f32[24,24,2,768]{3,1,2,0:T(8,128)S(1)} fusion(f32[16,96,2,768,1]{3,1,0,2,4:T(8,128)} %constant.174, f32[16,24,24,96]{3,2,1,0:T(8,128)} %all-to-all-done.4), kind=kOutput, calls=%fused_computation.51 | convolution fusion | flops 16307453952 | bytes 16515072 | tf_op jit(solution)/shard_map/sziy,syhj->hzij/dot_general | solution.py:121
  631.4 39.7 %collective-permute-done.4 = f32[24,24,768]{2,1,0:T(8,128)S(1)} collective-permute-done((f32[24,24,768]{2,1,0:T(8,128)S(1)}, f32[24,24,768]{2,1,0:T(8,128)S(1)}, u32[]{:S(2)}, u32[]{:S(2)}) %collective-permute-start.4) | collective-permute-done | bytes 1769504 | tf_op jit(solution)/shard_map/ppermute | solution.py:85
  681.9 38.8 %collective-permute-done.5 = f32[24,24,768]{2,1,0:T(8,128)S(1)} collective-permute-done((f32[24,24,768]{2,1,0:T(8,128)S(1)}, f32[24,24,768]{2,1,0:T(8,128)S(1)}, u32[]{:S(2)}, u32[]{:S(2)}) %collective-permute-start.5) | collective-permute-done | bytes 1769504 | tf_op jit(solution)/shard_map/ppermute | solution.py:85
  721.0 15.4 %fusion.32 = f32[16,24,24,96]{3,2,1,0:T(8,128)} fusion(f32[2,768,16,96,1]{1,3,0,4,2:T(8,128)} %constant.175, f32[1,24,24,768]{3,2,1,0:T(8,128)S(1)} %get-tuple-element.18, f32[1,24,24,768]{3,2,1,0:T(8,128)S(1)} %get-tuple-element.17), kind=kOutput, calls=%fused_computation.42 | convolution fusion | flops 8154611712 | bytes 16515072 | tf_op jit(solution)/shard_map/hzij,hjsy->sziy/dot_general | solution.py:132
  736.3 8.1 all-to-all-start.5
  744.4 37.5 %fusion.60 = f32[24,24,2,768]{3,1,2,0:T(8,128)S(1)} fusion(f32[16,96,2,768,1]{3,1,0,2,4:T(8,128)} %constant.174, f32[16,24,24,96]{3,2,1,0:T(8,128)} %all-to-all-done.6), kind=kOutput, calls=%fused_computation.52 | convolution fusion | flops 16307453952 | bytes 16515072 | tf_op jit(solution)/shard_map/sziy,syhj->hzij/dot_general | solution.py:121
  782.4 39.7 %collective-permute-done.6 = f32[24,24,768]{2,1,0:T(8,128)S(1)} collective-permute-done((f32[24,24,768]{2,1,0:T(8,128)S(1)}, f32[24,24,768]{2,1,0:T(8,128)S(1)}, u32[]{:S(2)}, u32[]{:S(2)}) %collective-permute-start.6) | collective-permute-done | bytes 1769504 | tf_op jit(solution)/shard_map/ppermute | solution.py:85
  832.8 38.8 %collective-permute-done.7 = f32[24,24,768]{2,1,0:T(8,128)S(1)} collective-permute-done((f32[24,24,768]{2,1,0:T(8,128)S(1)}, f32[24,24,768]{2,1,0:T(8,128)S(1)}, u32[]{:S(2)}, u32[]{:S(2)}) %collective-permute-start.7) | collective-permute-done | bytes 1769504 | tf_op jit(solution)/shard_map/ppermute | solution.py:85
  871.9 15.5 %fusion.35 = f32[16,24,24,96]{3,2,1,0:T(8,128)} fusion(f32[2,768,16,96,1]{1,3,0,4,2:T(8,128)} %constant.175, f32[1,24,24,768]{3,2,1,0:T(8,128)S(1)} %get-tuple-element.14, f32[1,24,24,768]{3,2,1,0:T(8,128)S(1)} %get-tuple-element.13), kind=kOutput, calls=%fused_computation.43 | convolution fusion | flops 8154611712 | bytes 16515072 | tf_op jit(solution)/shard_map/hzij,hjsy->sziy/dot_general | solution.py:132
  887.4 8.5 all-to-all-start.7
  895.9 15.7 %convolution_bitcast_fusion = f32[24,96,1536]{2,1,0:T(8,128)} fusion(f32[16,24,24,96]{3,2,1,0:T(8,128)} %all-to-all-done.1, f32[16,24,1536,1]{2,1,3,0:T(8,128)S(1)} %copy-done.4), kind=kOutput, calls=%fused_computation.12 | convolution fusion | flops 8153726976 | bytes 20054016 | tf_op jit(solution)/shard_map/dziy,din->zyn/dot_general | solution.py:137
  911.6 16.6 %bitcast_add_fusion.2 = f32[24,96,1536]{2,1,0:T(8,128)S(1)} fusion(f32[24,96,1536]{2,1,0:T(8,128)} %convolution_bitcast_fusion, f32[16,24,24,96]{3,2,1,0:T(8,128)} %all-to-all-done.3, f32[16,24,1536,1]{2,1,3,0:T(8,128)} %constant.179), kind=kOutput, calls=%fused_computation.3 | convolution fusion | flops 8157265920 | bytes 34209792 | tf_op jit(solution)/shard_map/dziy,din->zyn/dot_general | solution.py:137
  928.2 17.0 %bitcast_add_fusion.1 = f32[24,96,1536]{2,1,0:T(8,128)} fusion(f32[24,96,1536]{2,1,0:T(8,128)S(1)} %bitcast_add_fusion.2, f32[16,24,24,96]{3,2,1,0:T(8,128)} %all-to-all-done.5, f32[16,24,1536,1]{2,1,3,0:T(8,128)} %constant.180), kind=kOutput, calls=%fused_computation.2 | convolution fusion | flops 8157265920 | bytes 34209792 | tf_op jit(solution)/shard_map/dziy,din->zyn/dot_general | solution.py:137
  945.2 54.3 %all-to-all-done.7 = f32[16,24,24,96]{3,2,1,0:T(8,128)} async-done(((f32[16,24,24,96]{3,2,1,0:T(8,128)}), f32[16,24,24,96]{3,2,1,0:T(8,128)}, u32[]{:S(2)}, u32[]{:S(2)}) %all-to-all-start.7) | async-done | bytes 3538976 | tf_op jit(solution)/shard_map/all_to_all | solution.py:136
  999.5 19.3 %fusion = f32[24,96,1536]{2,1,0:T(8,128)} fusion(f32[24,96,1536]{2,1,0:T(8,128)} %bitcast_add_fusion.1, f32[16,24,24,96]{3,2,1,0:T(8,128)} %all-to-all-done.7, f32[16,24,1536,1]{2,1,3,0:T(8,128)} %constant.181), kind=kOutput, calls=%fused_computation.1 | convolution fusion | flops 8160804864 | bytes 34209792 | tf_op jit(solution)/shard_map/dziy,din->zyn/dot_general | solution.py:137
  (71 shorter events, 75.8 us)
Async XLA Ops:
  27.8 7.1 copy-start.7
  27.8 110.7 %all-to-all-start = ((f32[16,24,24,96]{3,2,1,0:T(8,128)}), f32[16,24,24,96]{3,2,1,0:T(8,128)}, u32[]{:S(2)}, u32[]{:S(2)}) async-start(f32[16,24,24,96]{3,2,1,0:T(8,128)} %fusion.42), calls=%async_computation | async-start | bytes 9437184 | tf_op jit(solution)/shard_map/all_to_all | solution.py:140
  62.1 82.1 %copy-start.6 = (f32[1536,16,24,1]{0,2,3,1:T(8,128)S(1)}, f32[1536,16,24,1]{0,2,3,1:T(8,128)}, u32[]{:S(2)}) copy-start(f32[1536,16,24,1]{0,2,3,1:T(8,128)} %constant.172) | copy-start | bytes 7077892
  138.5 33.0 %slice-start = ((s8[9437184]{0:T(1024)(128)(4,1)}), s8[1048576]{0:T(1024)(128)(4,1)S(1)}, s32[]{:S(2)}) async-start(s8[9437184]{0:T(1024)(128)(4,1)} %bitcast.281), calls=%async_computation.8 | async-start | bytes 2097152
  138.5 109.3 %all-to-all-start.2 = ((f32[16,24,24,96]{3,2,1,0:T(8,128)}), f32[16,24,24,96]{3,2,1,0:T(8,128)}, u32[]{:S(2)}, u32[]{:S(2)}) async-start(f32[16,24,24,96]{3,2,1,0:T(8,128)} %fusion.48), calls=%async_computation.2 | async-start | bytes 9437184 | tf_op jit(solution)/shard_map/all_to_all | solution.py:140
  144.2 27.3 %slice-start.1 = ((s8[9437184]{0:T(1024)(128)(4,1)}), s8[4194304]{0:T(1024)(128)(4,1)S(1)}, s32[]{:S(2)}) async-start(s8[9437184]{0:T(1024)(128)(4,1)} %bitcast.281), calls=%async_computation.9 | async-start | bytes 8388608
  144.2 27.3 %slice-start.2 = ((s8[9437184]{0:T(1024)(128)(4,1)}), s8[4194304]{0:T(1024)(128)(4,1)S(1)}, s32[]{:S(2)}) async-start(s8[9437184]{0:T(1024)(128)(4,1)} %bitcast.281), calls=%async_computation.10 | async-start | bytes 8388608
  209.1 43.9 %copy-start.5 = (f32[1536,16,24,1]{0,2,3,1:T(8,128)S(1)}, f32[1536,16,24,1]{0,2,3,1:T(8,128)}, u32[]{:S(2)}) copy-start(f32[1536,16,24,1]{0,2,3,1:T(8,128)} %constant.177) | copy-start | bytes 7077892
  247.8 108.8 %all-to-all-start.4 = ((f32[16,24,24,96]{3,2,1,0:T(8,128)}), f32[16,24,24,96]{3,2,1,0:T(8,128)}, u32[]{:S(2)}, u32[]{:S(2)}) async-start(f32[16,24,24,96]{3,2,1,0:T(8,128)} %fusion.39), calls=%async_computation.4 | async-start | bytes 9437184 | tf_op jit(solution)/shard_map/all_to_all | solution.py:146
  356.6 115.2 %all-to-all-start.6 = ((f32[16,24,24,96]{3,2,1,0:T(8,128)}), f32[16,24,24,96]{3,2,1,0:T(8,128)}, u32[]{:S(2)}, u32[]{:S(2)}) async-start(f32[16,24,24,96]{3,2,1,0:T(8,128)} %fusion.45), calls=%async_computation.6 | async-start | bytes 9437184 | tf_op jit(solution)/shard_map/all_to_all | solution.py:146
  364.7 40.1 %collective-permute-start = (f32[24,24,768]{2,1,0:T(8,128)}, f32[24,24,768]{2,1,0:T(8,128)}, u32[]{:S(2)}, u32[]{:S(2)}) collective-permute-start(f32[24,24,768]{2,1,0:T(8,128)} %dynamic-slice_bitcast_fusion.7), channel_id=1, source_target_pairs={{0,16},{16,0},{1,17},{17,1},{2,18},{18,2},{3,19},{19,3},{4,20},{20... | collective-permute-start | bytes 5308424 | tf_op jit(solution)/shard_map/ppermute | solution.py:85
  415.6 40.7 %copy-start.1 = (f32[48,24,768]{2,1,0:T(8,128)S(1)}, f32[48,24,768]{2,1,0:T(8,128)}, u32[]{:S(2)}) copy-start(f32[48,24,768]{2,1,0:T(8,128)} %shard_map.118) | copy-start | bytes 10616836
  417.4 39.0 %collective-permute-start.1 = (f32[24,24,768]{2,1,0:T(8,128)S(1)}, f32[24,24,768]{2,1,0:T(8,128)S(1)}, u32[]{:S(2)}, u32[]{:S(2)}) collective-permute-start(f32[24,24,768]{2,1,0:T(8,128)S(1)} %dynamic-slice_bitcast_fusion.6), channel_id=1, source_target_pairs={{0,16},{16,0},{1,17},{17,1},{2,18},{18,2},{3,19},{19,3},{4,20},{20... | collective-permute-start | bytes 5308424 | tf_op jit(solution)/shard_map/ppermute | solution.py:85
  471.8 113.4 %all-to-all-start.1 = ((f32[16,24,24,96]{3,2,1,0:T(8,128)}), f32[16,24,24,96]{3,2,1,0:T(8,128)}, u32[]{:S(2)}, u32[]{:S(2)}) async-start(f32[16,24,24,96]{3,2,1,0:T(8,128)} %fusion.38), calls=%async_computation.1 | async-start | bytes 9437184 | tf_op jit(solution)/shard_map/all_to_all | solution.py:136
  480.4 39.9 %collective-permute-start.2 = (f32[24,24,768]{2,1,0:T(8,128)S(1)}, f32[24,24,768]{2,1,0:T(8,128)S(1)}, u32[]{:S(2)}, u32[]{:S(2)}) collective-permute-start(f32[24,24,768]{2,1,0:T(8,128)S(1)} %dynamic-slice_bitcast_fusion.5), channel_id=1, source_target_pairs={{0,16},{16,0},{1,17},{17,1},{2,18},{18,2},{3,19},{19,3},{4,20},{20... | collective-permute-start | bytes 5308424 | tf_op jit(solution)/shard_map/ppermute | solution.py:85
  529.0 40.7 %copy-start.2 = (f32[48,24,768]{2,1,0:T(8,128)S(1)}, f32[48,24,768]{2,1,0:T(8,128)}, u32[]{:S(2)}) copy-start(f32[48,24,768]{2,1,0:T(8,128)} %shard_map.119) | copy-start | bytes 10616836
  530.7 39.0 %collective-permute-start.3 = (f32[24,24,768]{2,1,0:T(8,128)S(1)}, f32[24,24,768]{2,1,0:T(8,128)S(1)}, u32[]{:S(2)}, u32[]{:S(2)}) collective-permute-start(f32[24,24,768]{2,1,0:T(8,128)S(1)} %dynamic-slice_bitcast_fusion.4), channel_id=1, source_target_pairs={{0,16},{16,0},{1,17},{17,1},{2,18},{18,2},{3,19},{19,3},{4,20},{20... | collective-permute-start | bytes 5308424 | tf_op jit(solution)/shard_map/ppermute | solution.py:85
  585.2 151.2 %all-to-all-start.3 = ((f32[16,24,24,96]{3,2,1,0:T(8,128)}), f32[16,24,24,96]{3,2,1,0:T(8,128)}, u32[]{:S(2)}, u32[]{:S(2)}) async-start(f32[16,24,24,96]{3,2,1,0:T(8,128)} %fusion.29), calls=%async_computation.3 | async-start | bytes 9437184 | tf_op jit(solution)/shard_map/all_to_all | solution.py:136
  631.0 40.0 %collective-permute-start.4 = (f32[24,24,768]{2,1,0:T(8,128)S(1)}, f32[24,24,768]{2,1,0:T(8,128)S(1)}, u32[]{:S(2)}, u32[]{:S(2)}) collective-permute-start(f32[24,24,768]{2,1,0:T(8,128)S(1)} %dynamic-slice_bitcast_fusion.3), channel_id=1, source_target_pairs={{0,16},{16,0},{1,17},{17,1},{2,18},{18,2},{3,19},{19,3},{4,20},{20... | collective-permute-start | bytes 5308424 | tf_op jit(solution)/shard_map/ppermute | solution.py:85
  679.9 40.8 %copy-start.3 = (f32[48,24,768]{2,1,0:T(8,128)S(1)}, f32[48,24,768]{2,1,0:T(8,128)}, u32[]{:S(2)}) copy-start(f32[48,24,768]{2,1,0:T(8,128)} %shard_map.120) | copy-start | bytes 10616836
  681.6 39.1 %collective-permute-start.5 = (f32[24,24,768]{2,1,0:T(8,128)S(1)}, f32[24,24,768]{2,1,0:T(8,128)S(1)}, u32[]{:S(2)}, u32[]{:S(2)}) collective-permute-start(f32[24,24,768]{2,1,0:T(8,128)S(1)} %dynamic-slice_bitcast_fusion.2), channel_id=1, source_target_pairs={{0,16},{16,0},{1,17},{17,1},{2,18},{18,2},{3,19},{19,3},{4,20},{20... | collective-permute-start | bytes 5308424 | tf_op jit(solution)/shard_map/ppermute | solution.py:85
  736.3 151.1 %all-to-all-start.5 = ((f32[16,24,24,96]{3,2,1,0:T(8,128)}), f32[16,24,24,96]{3,2,1,0:T(8,128)}, u32[]{:S(2)}, u32[]{:S(2)}) async-start(f32[16,24,24,96]{3,2,1,0:T(8,128)} %fusion.32), calls=%async_computation.5 | async-start | bytes 9437184 | tf_op jit(solution)/shard_map/all_to_all | solution.py:136
  782.1 40.0 %collective-permute-start.6 = (f32[24,24,768]{2,1,0:T(8,128)S(1)}, f32[24,24,768]{2,1,0:T(8,128)S(1)}, u32[]{:S(2)}, u32[]{:S(2)}) collective-permute-start(f32[24,24,768]{2,1,0:T(8,128)S(1)} %dynamic-slice_bitcast_fusion.1), channel_id=1, source_target_pairs={{0,16},{16,0},{1,17},{17,1},{2,18},{18,2},{3,19},{19,3},{4,20},{20... | collective-permute-start | bytes 5308424 | tf_op jit(solution)/shard_map/ppermute | solution.py:85
  830.8 40.8 %copy-start = (f32[48,24,768]{2,1,0:T(8,128)S(1)}, f32[48,24,768]{2,1,0:T(8,128)}, u32[]{:S(2)}) copy-start(f32[48,24,768]{2,1,0:T(8,128)} %shard_map.121) | copy-start | bytes 10616836
  832.6 39.1 %collective-permute-start.7 = (f32[24,24,768]{2,1,0:T(8,128)S(1)}, f32[24,24,768]{2,1,0:T(8,128)S(1)}, u32[]{:S(2)}, u32[]{:S(2)}) collective-permute-start(f32[24,24,768]{2,1,0:T(8,128)S(1)} %dynamic-slice_bitcast_fusion), channel_id=1, source_target_pairs={{0,16},{16,0},{1,17},{17,1},{2,18},{18,2},{3,19},{19,3},{4,20},{20... | collective-permute-start | bytes 5308424 | tf_op jit(solution)/shard_map/ppermute | solution.py:85
  887.4 8.5 copy-start.4
  887.4 112.0 %all-to-all-start.7 = ((f32[16,24,24,96]{3,2,1,0:T(8,128)}), f32[16,24,24,96]{3,2,1,0:T(8,128)}, u32[]{:S(2)}, u32[]{:S(2)}) async-start(f32[16,24,24,96]{3,2,1,0:T(8,128)} %fusion.35), calls=%async_computation.7 | async-start | bytes 9437184 | tf_op jit(solution)/shard_map/all_to_all | solution.py:136

commit v11 on v10

--- a/solution.py
+++ b/solution.py
@@ -16,10 +16,10 @@
     return jnp.cos(angles) + jnp.sin(angles)
 
 
-def cas_constant(row_index, col_index, length):
+def cas_constant(row_index, col_index, length, factor=1.0):
     product = np.outer(row_index, col_index) % length
     angles = product.astype(np.float64) * (2.0 * math.pi / length)
-    return jnp.asarray((np.cos(angles) + np.sin(angles)).astype(np.float32))
+    return jnp.asarray(((np.cos(angles) + np.sin(angles)) * factor).astype(np.float32))
 
 
 def eigen_values(wave_index, length):
@@ -132,7 +132,7 @@
         return jnp.einsum("hzij,hjsy->sziy", returned, inverse_y, precision=lax.Precision.HIGH)
 
     def back_x(chunk, back_y):
-        table_back = cas_constant(chunk_waves(chunk), index_x, full_x).reshape(col_count, chunk_x, full_x)
+        table_back = cas_constant(chunk_waves(chunk), index_x, full_x, scale).reshape(col_count, chunk_x, full_x)
         scattered = lax.all_to_all(back_y, "col", 0, 0, tiled=True)
         return jnp.einsum("dziy,din->zyn", scattered, table_back, precision=lax.Precision.HIGH)
 
@@ -148,7 +148,7 @@
         pressure = part if pressure is None else pressure + part
         if chunk + 1 < chunks:
             pressure = lax.optimization_barrier(pressure)
-    return pressure * scale
+    return pressure
 
 
 def solution(mesh):

time: 1030 us -> 1030 us (level)
  no operation moved by 1% of the time
where the time goes in v11:
time: 1030 us; the launch traced here: 1020 us
  waiting for transfers between devices  521 us (51%)
  matrix products  388 us (38%)
  starting transfers between devices  58.9 us (6%)
  Pallas kernels  25.9 us (3%)
  other arithmetic  14 us (1%)
    ppermute x8, waiting for transfers between devices, exchange(): arrived.append(lax.ppermute(outgoing, axis_name, perm))  312 us
    dot_general x4, matrix products, spectra_y(): return jnp.einsum('sziy,syhj->hzij', gathered, forward_y, precision=highest)  149 us
    all_to_all x2, waiting for transfers between devices, body(): lax.all_to_all(spread_x(chunk), 'col', 0, 0, tiled=True)  115 us
    dot_general x4, matrix products, spread_x(): return jnp.einsum('zyx,xdi->dziy', source, table_chunk, precision=highest)  109 us
    dot_general x4, matrix products, back_x(): jnp.einsum('dziy,din->zyn', scattered, table_back, precision=lax.Precisio...  68.4 us
    dot_general x4, matrix products, middle(): jnp.einsum('hzij,hjsy->sziy', returned, inverse_y, precision=lax.Precisio...  61.2 us
    all_to_all x4, waiting for transfers between devices, back_x(): scattered = lax.all_to_all(back_y, 'col', 0, 0, tiled=True)  54.3 us
    all_to_all x2, waiting for transfers between devices, body(): gathered.append(lax.all_to_all(spread, 'col', 0, 0, tiled=True))  39.8 us
  transfers between devices with their start and end apart: 16, of which 12 were waited for; matrix products, arithmetic and copies ran while one was open for 36% of the time, Pallas kernels for 3%

profile of v11, /device:TPU:15, one launch (start us, length us, event | category | flops | bytes accessed | tf_op | source)
XLA Modules:
  0.0 1018.8 jit_solution(15197253689228605040)
XLA Ops:
  0.0 27.8 %fusion.41 = f32[16,24,24,96]{3,2,1,0:T(8,128)} fusion(f32[1536,16,24,1]{0,2,3,1:T(8,128)} %constant.171, f32[24,96,1536]{2,1,0:T(8,128)} %param.12), kind=kOutput, calls=%fused_computation.45 | convolution fusion | flops 16307453952 | bytes 20054016 | tf_op jit(solution)/shard_map/zyx,xdi->dziy/dot_general | solution.py:118
  35.0 27.1 %fusion.47 = f32[16,24,24,96]{3,2,1,0:T(8,128)} fusion(f32[1536,16,24,1]{0,2,3,1:T(8,128)S(1)} %copy-done.7, f32[24,96,1536]{2,1,0:T(8,128)} %param.12), kind=kOutput, calls=%fused_computation.47 | convolution fusion | flops 16307453952 | bytes 20054016 | tf_op jit(solution)/shard_map/zyx,xdi->dziy/dot_general | solution.py:118
  62.1 76.4 %all-to-all-done = f32[16,24,24,96]{3,2,1,0:T(8,128)} async-done(((f32[16,24,24,96]{3,2,1,0:T(8,128)}), f32[16,24,24,96]{3,2,1,0:T(8,128)}, u32[]{:S(2)}, u32[]{:S(2)}) %all-to-all-start) | async-done | bytes 3538976 | tf_op jit(solution)/shard_map/all_to_all | solution.py:140
  144.2 27.2 %fusion.38 = f32[16,24,24,96]{3,2,1,0:T(8,128)} fusion(f32[1536,16,24,1]{0,2,3,1:T(8,128)S(1)} %copy-done.6, f32[24,96,1536]{2,1,0:T(8,128)} %param.12), kind=kOutput, calls=%fused_computation.44 | convolution fusion | flops 16307453952 | bytes 20054016 | tf_op jit(solution)/shard_map/zyx,xdi->dziy/dot_general | solution.py:118
  171.5 37.6 %fusion.50 = f32[2,24,24,768]{3,2,0,1:T(8,128)} fusion(f32[16,96,2,768,1]{3,1,0,2,4:T(8,128)S(1)} %bitcast.280, f32[16,24,24,96]{3,2,1,0:T(8,128)} %all-to-all-done), kind=kOutput, calls=%fused_computation.48 | convolution fusion | flops 16307453952 | bytes 16515072 | tf_op jit(solution)/shard_map/sziy,syhj->hzij/dot_general | solution.py:121
  209.1 38.7 %all-to-all-done.2 = f32[16,24,24,96]{3,2,1,0:T(8,128)} async-done(((f32[16,24,24,96]{3,2,1,0:T(8,128)}), f32[16,24,24,96]{3,2,1,0:T(8,128)}, u32[]{:S(2)}, u32[]{:S(2)}) %all-to-all-start.2) | async-done | bytes 3538976 | tf_op jit(solution)/shard_map/all_to_all | solution.py:140
  253.0 27.1 %fusion.44 = f32[16,24,24,96]{3,2,1,0:T(8,128)} fusion(f32[1536,16,24,1]{0,2,3,1:T(8,128)S(1)} %copy-done.5, f32[24,96,1536]{2,1,0:T(8,128)} %param.12), kind=kOutput, calls=%fused_computation.46 | convolution fusion | flops 16307453952 | bytes 20054016 | tf_op jit(solution)/shard_map/zyx,xdi->dziy/dot_general | solution.py:118
  280.2 36.6 %fusion.53 = f32[2,24,24,768]{3,2,0,1:T(8,128)S(1)} fusion(f32[16,96,2,768,1]{3,1,0,2,4:T(8,128)} %constant.172, f32[16,24,24,96]{3,2,1,0:T(8,128)} %all-to-all-done.2), kind=kOutput, calls=%fused_computation.49 | convolution fusion | flops 16307453952 | bytes 16515072 | tf_op jit(solution)/shard_map/sziy,syhj->hzij/dot_general | solution.py:121
  316.8 39.8 %all-to-all-done.4 = f32[16,24,24,96]{3,2,1,0:T(8,128)} async-done(((f32[16,24,24,96]{3,2,1,0:T(8,128)}), f32[16,24,24,96]{3,2,1,0:T(8,128)}, u32[]{:S(2)}, u32[]{:S(2)}) %all-to-all-start.4) | async-done | bytes 3538976 | tf_op jit(solution)/shard_map/all_to_all | solution.py:146
  366.8 38.1 %collective-permute-done = f32[24,24,768]{2,1,0:T(8,128)} collective-permute-done((f32[24,24,768]{2,1,0:T(8,128)}, f32[24,24,768]{2,1,0:T(8,128)}, u32[]{:S(2)}, u32[]{:S(2)}) %collective-permute-start) | collective-permute-done | bytes 1769504 | tf_op jit(solution)/shard_map/ppermute | solution.py:85
  417.7 38.7 %collective-permute-done.1 = f32[24,24,768]{2,1,0:T(8,128)S(1)} collective-permute-done((f32[24,24,768]{2,1,0:T(8,128)S(1)}, f32[24,24,768]{2,1,0:T(8,128)S(1)}, u32[]{:S(2)}, u32[]{:S(2)}) %collective-permute-start.1) | collective-permute-done | bytes 1769504 | tf_op jit(solution)/shard_map/ppermute | solution.py:85
  456.6 15.2 %fusion.37 = f32[16,24,24,96]{3,2,1,0:T(8,128)} fusion(f32[2,768,16,96,1]{1,3,0,4,2:T(8,128)} %constant.173, f32[1,24,24,768]{3,2,0,1:T(8,128)S(1)} %get-tuple-element.26, f32[1,24,24,768]{3,2,0,1:T(8,128)S(1)} %get-tuple-element.25), kind=kOutput, calls=%fused_computation.43 | convolution fusion | flops 8154611712 | bytes 16515072 | tf_op jit(solution)/shard_map/hzij,hjsy->sziy/dot_general | solution.py:132
  471.8 8.4 all-to-all-start.1
  480.7 39.6 %collective-permute-done.2 = f32[24,24,768]{2,1,0:T(8,128)S(1)} collective-permute-done((f32[24,24,768]{2,1,0:T(8,128)S(1)}, f32[24,24,768]{2,1,0:T(8,128)S(1)}, u32[]{:S(2)}, u32[]{:S(2)}) %collective-permute-start.2) | collective-permute-done | bytes 1769504 | tf_op jit(solution)/shard_map/ppermute | solution.py:85
  531.1 38.6 %collective-permute-done.3 = f32[24,24,768]{2,1,0:T(8,128)S(1)} collective-permute-done((f32[24,24,768]{2,1,0:T(8,128)S(1)}, f32[24,24,768]{2,1,0:T(8,128)S(1)}, u32[]{:S(2)}, u32[]{:S(2)}) %collective-permute-start.3) | collective-permute-done | bytes 1769504 | tf_op jit(solution)/shard_map/ppermute | solution.py:85
  570.0 15.2 %fusion.28 = f32[16,24,24,96]{3,2,1,0:T(8,128)} fusion(f32[2,768,16,96,1]{1,3,0,4,2:T(8,128)} %constant.173, f32[1,24,24,768]{3,2,1,0:T(8,128)S(1)} %get-tuple-element.22, f32[1,24,24,768]{3,2,1,0:T(8,128)S(1)} %get-tuple-element.21), kind=kOutput, calls=%fused_computation.40 | convolution fusion | flops 8154611712 | bytes 16515072 | tf_op jit(solution)/shard_map/hzij,hjsy->sziy/dot_general | solution.py:132
  585.2 8.2 all-to-all-start.3
  593.4 37.5 %fusion.56 = f32[24,24,2,768]{3,1,2,0:T(8,128)S(1)} fusion(f32[16,96,2,768,1]{3,1,0,2,4:T(8,128)} %constant.172, f32[16,24,24,96]{3,2,1,0:T(8,128)} %all-to-all-done.4), kind=kOutput, calls=%fused_computation.50 | convolution fusion | flops 16307453952 | bytes 16515072 | tf_op jit(solution)/shard_map/sziy,syhj->hzij/dot_general | solution.py:121
  631.4 39.7 %collective-permute-done.4 = f32[24,24,768]{2,1,0:T(8,128)S(1)} collective-permute-done((f32[24,24,768]{2,1,0:T(8,128)S(1)}, f32[24,24,768]{2,1,0:T(8,128)S(1)}, u32[]{:S(2)}, u32[]{:S(2)}) %collective-permute-start.4) | collective-permute-done | bytes 1769504 | tf_op jit(solution)/shard_map/ppermute | solution.py:85
  681.9 38.8 %collective-permute-done.5 = f32[24,24,768]{2,1,0:T(8,128)S(1)} collective-permute-done((f32[24,24,768]{2,1,0:T(8,128)S(1)}, f32[24,24,768]{2,1,0:T(8,128)S(1)}, u32[]{:S(2)}, u32[]{:S(2)}) %collective-permute-start.5) | collective-permute-done | bytes 1769504 | tf_op jit(solution)/shard_map/ppermute | solution.py:85
  721.0 15.4 %fusion.31 = f32[16,24,24,96]{3,2,1,0:T(8,128)} fusion(f32[2,768,16,96,1]{1,3,0,4,2:T(8,128)} %constant.173, f32[1,24,24,768]{3,2,1,0:T(8,128)S(1)} %get-tuple-element.18, f32[1,24,24,768]{3,2,1,0:T(8,128)S(1)} %get-tuple-element.17), kind=kOutput, calls=%fused_computation.41 | convolution fusion | flops 8154611712 | bytes 16515072 | tf_op jit(solution)/shard_map/hzij,hjsy->sziy/dot_general | solution.py:132
  736.3 8.1 all-to-all-start.5
  744.4 37.5 %fusion.59 = f32[24,24,2,768]{3,1,2,0:T(8,128)S(1)} fusion(f32[16,96,2,768,1]{3,1,0,2,4:T(8,128)} %constant.172, f32[16,24,24,96]{3,2,1,0:T(8,128)} %all-to-all-done.6), kind=kOutput, calls=%fused_computation.51 | convolution fusion | flops 16307453952 | bytes 16515072 | tf_op jit(solution)/shard_map/sziy,syhj->hzij/dot_general | solution.py:121
  782.4 39.7 %collective-permute-done.6 = f32[24,24,768]{2,1,0:T(8,128)S(1)} collective-permute-done((f32[24,24,768]{2,1,0:T(8,128)S(1)}, f32[24,24,768]{2,1,0:T(8,128)S(1)}, u32[]{:S(2)}, u32[]{:S(2)}) %collective-permute-start.6) | collective-permute-done | bytes 1769504 | tf_op jit(solution)/shard_map/ppermute | solution.py:85
  832.8 38.8 %collective-permute-done.7 = f32[24,24,768]{2,1,0:T(8,128)S(1)} collective-permute-done((f32[24,24,768]{2,1,0:T(8,128)S(1)}, f32[24,24,768]{2,1,0:T(8,128)S(1)}, u32[]{:S(2)}, u32[]{:S(2)}) %collective-permute-start.7) | collective-permute-done | bytes 1769504 | tf_op jit(solution)/shard_map/ppermute | solution.py:85
  871.9 15.5 %fusion.34 = f32[16,24,24,96]{3,2,1,0:T(8,128)} fusion(f32[2,768,16,96,1]{1,3,0,4,2:T(8,128)} %constant.173, f32[1,24,24,768]{3,2,1,0:T(8,128)S(1)} %get-tuple-element.14, f32[1,24,24,768]{3,2,1,0:T(8,128)S(1)} %get-tuple-element.13), kind=kOutput, calls=%fused_computation.42 | convolution fusion | flops 8154611712 | bytes 16515072 | tf_op jit(solution)/shard_map/hzij,hjsy->sziy/dot_general | solution.py:132
  887.4 8.5 all-to-all-start.7
  895.9 15.7 %convolution_bitcast_fusion = f32[24,96,1536]{2,1,0:T(8,128)} fusion(f32[16,24,24,96]{3,2,1,0:T(8,128)} %all-to-all-done.1, f32[16,24,1536,1]{2,1,3,0:T(8,128)S(1)} %copy-done.4), kind=kOutput, calls=%fused_computation.11 | convolution fusion | flops 8153726976 | bytes 20054016 | tf_op jit(solution)/shard_map/dziy,din->zyn/dot_general | solution.py:137
  911.6 16.6 %bitcast_add_fusion.2 = f32[24,96,1536]{2,1,0:T(8,128)S(1)} fusion(f32[24,96,1536]{2,1,0:T(8,128)} %convolution_bitcast_fusion, f32[16,24,24,96]{3,2,1,0:T(8,128)} %all-to-all-done.3, f32[16,24,1536,1]{2,1,3,0:T(8,128)} %constant.177), kind=kOutput, calls=%fused_computation.2 | convolution fusion | flops 8157265920 | bytes 34209792 | tf_op jit(solution)/shard_map/dziy,din->zyn/dot_general | solution.py:137
  928.2 17.0 %bitcast_add_fusion.1 = f32[24,96,1536]{2,1,0:T(8,128)} fusion(f32[24,96,1536]{2,1,0:T(8,128)S(1)} %bitcast_add_fusion.2, f32[16,24,24,96]{3,2,1,0:T(8,128)} %all-to-all-done.5, f32[16,24,1536,1]{2,1,3,0:T(8,128)} %constant.178), kind=kOutput, calls=%fused_computation.1 | convolution fusion | flops 8157265920 | bytes 34209792 | tf_op jit(solution)/shard_map/dziy,din->zyn/dot_general | solution.py:137
  945.2 54.3 %all-to-all-done.7 = f32[16,24,24,96]{3,2,1,0:T(8,128)} async-done(((f32[16,24,24,96]{3,2,1,0:T(8,128)}), f32[16,24,24,96]{3,2,1,0:T(8,128)}, u32[]{:S(2)}, u32[]{:S(2)}) %all-to-all-start.7) | async-done | bytes 3538976 | tf_op jit(solution)/shard_map/all_to_all | solution.py:136
  999.5 19.2 %bitcast_add_fusion = f32[24,96,1536]{2,1,0:T(8,128)} fusion(f32[24,96,1536]{2,1,0:T(8,128)} %bitcast_add_fusion.1, f32[16,24,24,96]{3,2,1,0:T(8,128)} %all-to-all-done.7, f32[16,24,1536,1]{2,1,3,0:T(8,128)} %constant.179), kind=kOutput, calls=%fused_computation | convolution fusion | flops 8157265920 | bytes 34209792 | tf_op jit(solution)/shard_map/dziy,din->zyn/dot_general | solution.py:137
  (71 shorter events, 75.8 us)
Async XLA Ops:
  27.8 7.1 copy-start.7
  27.8 110.7 %all-to-all-start = ((f32[16,24,24,96]{3,2,1,0:T(8,128)}), f32[16,24,24,96]{3,2,1,0:T(8,128)}, u32[]{:S(2)}, u32[]{:S(2)}) async-start(f32[16,24,24,96]{3,2,1,0:T(8,128)} %fusion.41), calls=%async_computation | async-start | bytes 9437184 | tf_op jit(solution)/shard_map/all_to_all | solution.py:140
  62.1 82.1 %copy-start.6 = (f32[1536,16,24,1]{0,2,3,1:T(8,128)S(1)}, f32[1536,16,24,1]{0,2,3,1:T(8,128)}, u32[]{:S(2)}) copy-start(f32[1536,16,24,1]{0,2,3,1:T(8,128)} %constant.170) | copy-start | bytes 7077892
  138.5 33.0 %slice-start = ((s8[9437184]{0:T(1024)(128)(4,1)}), s8[1048576]{0:T(1024)(128)(4,1)S(1)}, s32[]{:S(2)}) async-start(s8[9437184]{0:T(1024)(128)(4,1)} %bitcast.279), calls=%async_computation.8 | async-start | bytes 2097152
  138.5 109.3 %all-to-all-start.2 = ((f32[16,24,24,96]{3,2,1,0:T(8,128)}), f32[16,24,24,96]{3,2,1,0:T(8,128)}, u32[]{:S(2)}, u32[]{:S(2)}) async-start(f32[16,24,24,96]{3,2,1,0:T(8,128)} %fusion.47), calls=%async_computation.2 | async-start | bytes 9437184 | tf_op jit(solution)/shard_map/all_to_all | solution.py:140
  144.2 27.3 %slice-start.1 = ((s8[9437184]{0:T(1024)(128)(4,1)}), s8[4194304]{0:T(1024)(128)(4,1)S(1)}, s32[]{:S(2)}) async-start(s8[9437184]{0:T(1024)(128)(4,1)} %bitcast.279), calls=%async_computation.9 | async-start | bytes 8388608
  144.2 27.3 %slice-start.2 = ((s8[9437184]{0:T(1024)(128)(4,1)}), s8[4194304]{0:T(1024)(128)(4,1)S(1)}, s32[]{:S(2)}) async-start(s8[9437184]{0:T(1024)(128)(4,1)} %bitcast.279), calls=%async_computation.10 | async-start | bytes 8388608
  209.1 43.9 %copy-start.5 = (f32[1536,16,24,1]{0,2,3,1:T(8,128)S(1)}, f32[1536,16,24,1]{0,2,3,1:T(8,128)}, u32[]{:S(2)}) copy-start(f32[1536,16,24,1]{0,2,3,1:T(8,128)} %constant.175) | copy-start | bytes 7077892
  247.8 108.8 %all-to-all-start.4 = ((f32[16,24,24,96]{3,2,1,0:T(8,128)}), f32[16,24,24,96]{3,2,1,0:T(8,128)}, u32[]{:S(2)}, u32[]{:S(2)}) async-start(f32[16,24,24,96]{3,2,1,0:T(8,128)} %fusion.38), calls=%async_computation.4 | async-start | bytes 9437184 | tf_op jit(solution)/shard_map/all_to_all | solution.py:146
  356.6 115.2 %all-to-all-start.6 = ((f32[16,24,24,96]{3,2,1,0:T(8,128)}), f32[16,24,24,96]{3,2,1,0:T(8,128)}, u32[]{:S(2)}, u32[]{:S(2)}) async-start(f32[16,24,24,96]{3,2,1,0:T(8,128)} %fusion.44), calls=%async_computation.6 | async-start | bytes 9437184 | tf_op jit(solution)/shard_map/all_to_all | solution.py:146
  364.7 40.1 %collective-permute-start = (f32[24,24,768]{2,1,0:T(8,128)}, f32[24,24,768]{2,1,0:T(8,128)}, u32[]{:S(2)}, u32[]{:S(2)}) collective-permute-start(f32[24,24,768]{2,1,0:T(8,128)} %dynamic-slice_bitcast_fusion.7), channel_id=1, source_target_pairs={{0,16},{16,0},{1,17},{17,1},{2,18},{18,2},{3,19},{19,3},{4,20},{20... | collective-permute-start | bytes 5308424 | tf_op jit(solution)/shard_map/ppermute | solution.py:85
  415.6 40.7 %copy-start.1 = (f32[48,24,768]{2,1,0:T(8,128)S(1)}, f32[48,24,768]{2,1,0:T(8,128)}, u32[]{:S(2)}) copy-start(f32[48,24,768]{2,1,0:T(8,128)} %shard_map.118) | copy-start | bytes 10616836
  417.4 39.0 %collective-permute-start.1 = (f32[24,24,768]{2,1,0:T(8,128)S(1)}, f32[24,24,768]{2,1,0:T(8,128)S(1)}, u32[]{:S(2)}, u32[]{:S(2)}) collective-permute-start(f32[24,24,768]{2,1,0:T(8,128)S(1)} %dynamic-slice_bitcast_fusion.6), channel_id=1, source_target_pairs={{0,16},{16,0},{1,17},{17,1},{2,18},{18,2},{3,19},{19,3},{4,20},{20... | collective-permute-start | bytes 5308424 | tf_op jit(solution)/shard_map/ppermute | solution.py:85
  471.8 113.4 %all-to-all-start.1 = ((f32[16,24,24,96]{3,2,1,0:T(8,128)}), f32[16,24,24,96]{3,2,1,0:T(8,128)}, u32[]{:S(2)}, u32[]{:S(2)}) async-start(f32[16,24,24,96]{3,2,1,0:T(8,128)} %fusion.37), calls=%async_computation.1 | async-start | bytes 9437184 | tf_op jit(solution)/shard_map/all_to_all | solution.py:136
  480.4 39.9 %collective-permute-start.2 = (f32[24,24,768]{2,1,0:T(8,128)S(1)}, f32[24,24,768]{2,1,0:T(8,128)S(1)}, u32[]{:S(2)}, u32[]{:S(2)}) collective-permute-start(f32[24,24,768]{2,1,0:T(8,128)S(1)} %dynamic-slice_bitcast_fusion.5), channel_id=1, source_target_pairs={{0,16},{16,0},{1,17},{17,1},{2,18},{18,2},{3,19},{19,3},{4,20},{20... | collective-permute-start | bytes 5308424 | tf_op jit(solution)/shard_map/ppermute | solution.py:85
  529.0 40.7 %copy-start.2 = (f32[48,24,768]{2,1,0:T(8,128)S(1)}, f32[48,24,768]{2,1,0:T(8,128)}, u32[]{:S(2)}) copy-start(f32[48,24,768]{2,1,0:T(8,128)} %shard_map.119) | copy-start | bytes 10616836
  530.7 39.0 %collective-permute-start.3 = (f32[24,24,768]{2,1,0:T(8,128)S(1)}, f32[24,24,768]{2,1,0:T(8,128)S(1)}, u32[]{:S(2)}, u32[]{:S(2)}) collective-permute-start(f32[24,24,768]{2,1,0:T(8,128)S(1)} %dynamic-slice_bitcast_fusion.4), channel_id=1, source_target_pairs={{0,16},{16,0},{1,17},{17,1},{2,18},{18,2},{3,19},{19,3},{4,20},{20... | collective-permute-start | bytes 5308424 | tf_op jit(solution)/shard_map/ppermute | solution.py:85
  585.2 151.2 %all-to-all-start.3 = ((f32[16,24,24,96]{3,2,1,0:T(8,128)}), f32[16,24,24,96]{3,2,1,0:T(8,128)}, u32[]{:S(2)}, u32[]{:S(2)}) async-start(f32[16,24,24,96]{3,2,1,0:T(8,128)} %fusion.28), calls=%async_computation.3 | async-start | bytes 9437184 | tf_op jit(solution)/shard_map/all_to_all | solution.py:136
  631.0 40.0 %collective-permute-start.4 = (f32[24,24,768]{2,1,0:T(8,128)S(1)}, f32[24,24,768]{2,1,0:T(8,128)S(1)}, u32[]{:S(2)}, u32[]{:S(2)}) collective-permute-start(f32[24,24,768]{2,1,0:T(8,128)S(1)} %dynamic-slice_bitcast_fusion.3), channel_id=1, source_target_pairs={{0,16},{16,0},{1,17},{17,1},{2,18},{18,2},{3,19},{19,3},{4,20},{20... | collective-permute-start | bytes 5308424 | tf_op jit(solution)/shard_map/ppermute | solution.py:85
  679.9 40.8 %copy-start.3 = (f32[48,24,768]{2,1,0:T(8,128)S(1)}, f32[48,24,768]{2,1,0:T(8,128)}, u32[]{:S(2)}) copy-start(f32[48,24,768]{2,1,0:T(8,128)} %shard_map.120) | copy-start | bytes 10616836
  681.6 39.1 %collective-permute-start.5 = (f32[24,24,768]{2,1,0:T(8,128)S(1)}, f32[24,24,768]{2,1,0:T(8,128)S(1)}, u32[]{:S(2)}, u32[]{:S(2)}) collective-permute-start(f32[24,24,768]{2,1,0:T(8,128)S(1)} %dynamic-slice_bitcast_fusion.2), channel_id=1, source_target_pairs={{0,16},{16,0},{1,17},{17,1},{2,18},{18,2},{3,19},{19,3},{4,20},{20... | collective-permute-start | bytes 5308424 | tf_op jit(solution)/shard_map/ppermute | solution.py:85
  736.3 151.1 %all-to-all-start.5 = ((f32[16,24,24,96]{3,2,1,0:T(8,128)}), f32[16,24,24,96]{3,2,1,0:T(8,128)}, u32[]{:S(2)}, u32[]{:S(2)}) async-start(f32[16,24,24,96]{3,2,1,0:T(8,128)} %fusion.31), calls=%async_computation.5 | async-start | bytes 9437184 | tf_op jit(solution)/shard_map/all_to_all | solution.py:136
  782.1 40.0 %collective-permute-start.6 = (f32[24,24,768]{2,1,0:T(8,128)S(1)}, f32[24,24,768]{2,1,0:T(8,128)S(1)}, u32[]{:S(2)}, u32[]{:S(2)}) collective-permute-start(f32[24,24,768]{2,1,0:T(8,128)S(1)} %dynamic-slice_bitcast_fusion.1), channel_id=1, source_target_pairs={{0,16},{16,0},{1,17},{17,1},{2,18},{18,2},{3,19},{19,3},{4,20},{20... | collective-permute-start | bytes 5308424 | tf_op jit(solution)/shard_map/ppermute | solution.py:85
  830.8 40.8 %copy-start = (f32[48,24,768]{2,1,0:T(8,128)S(1)}, f32[48,24,768]{2,1,0:T(8,128)}, u32[]{:S(2)}) copy-start(f32[48,24,768]{2,1,0:T(8,128)} %shard_map.121) | copy-start | bytes 10616836
  832.6 39.1 %collective-permute-start.7 = (f32[24,24,768]{2,1,0:T(8,128)S(1)}, f32[24,24,768]{2,1,0:T(8,128)S(1)}, u32[]{:S(2)}, u32[]{:S(2)}) collective-permute-start(f32[24,24,768]{2,1,0:T(8,128)S(1)} %dynamic-slice_bitcast_fusion), channel_id=1, source_target_pairs={{0,16},{16,0},{1,17},{17,1},{2,18},{18,2},{3,19},{19,3},{4,20},{20... | collective-permute-start | bytes 5308424 | tf_op jit(solution)/shard_map/ppermute | solution.py:85
  887.4 8.5 copy-start.4
  887.4 112.0 %all-to-all-start.7 = ((f32[16,24,24,96]{3,2,1,0:T(8,128)}), f32[16,24,24,96]{3,2,1,0:T(8,128)}, u32[]{:S(2)}, u32[]{:S(2)}) async-start(f32[16,24,24,96]{3,2,1,0:T(8,128)} %fusion.34), calls=%async_computation.7 | async-start | bytes 9437184 | tf_op jit(solution)/shard_map/all_to_all | solution.py:136
